TPU v7x, 256 devices: a whole 4x4x8 slice. The times are simulated.
256 devices in a mesh: gx: 32 (over z, x_hi, core), gy: 8 (over x_lo, y).
Axes of the slice: x: 4 (x_hi: 2, x_lo: 2; x = x_hi * 2 + x_lo), y: 4, z: 8, core: 2. Of those that a mesh axis runs over, the one named last changes fastest.
Arguments:
- magnet: float32 [3, 256, 128, 128], P(None, 'gx', 'gy'), may hold values from -5 to 5
- grain_ids: int32 [256, 128, 128], P('gx', 'gy'), may hold values from 0 to 3
- exch_table: float32 [4], replicated, may hold values from 0.05 to 0.4
- sat_table: float32 [4], replicated, may hold values from 0.5 to 4
- surface_map: int32 [64, 8, 128], P('gx', 'gy'), may hold values from 0 to 127, each once within a row
- near_list: int32 [32, 16, 8], P('gx', 'gy'), may hold values from 0 to 15
- near_blocks: bfloat16 [32, 16, 8, 128, 128], P('gx', 'gy'), may hold values from -0.1875 to 0.1875
Outputs:
- field: float32 [3, 256, 128, 128], P(None, 'gx', 'gy')
- potential: float32 [256, 128, 128], P('gx', 'gy')
All inputs are finite; a program needn't handle non-finite values.
Results may differ from a plain program's by a relative error of at most 0.0019.
Values may be sent and summed in bfloat16 or wider, within the bound.
No kernel may reach another device: no remote copies, remote signals or barrier semaphores. Data moves between devices by JAX's collectives and lax.ppermute only.
A program may use at most 64 MiB of HBM per device.

v0:
```python
import jax
import jax.numpy as jnp
from jax import lax
from jax.sharding import PartitionSpec as P

NODES = 128
SWEEPS = 8
EXT_SWEEPS = 4
NMAT = 4


SCREEN = 0.25
DIAG = 6.0 + SCREEN


def padded_2(block, sides, width):
    for axis, dim in sides:
        count = lax.axis_size(axis)
        forward = [(i, i + 1) for i in range(count - 1)]
        backward = [(target, source) for source, target in forward]
        low = lax.ppermute(
            lax.slice_in_dim(block, block.shape[dim] - width, None, axis=dim), axis, forward
        )
        high = lax.ppermute(lax.slice_in_dim(block, 0, width, axis=dim), axis, backward)
        block = jnp.concatenate([low, block, high], axis=dim)
    return block


def near_sum(widened):
    padded = jnp.pad(widened, ((0, 0), (0, 0), (0, 0), (1, 1)))
    total = widened[:, 2:, 1:-1] + widened[:, :-2, 1:-1]
    total = total + widened[:, 1:-1, 2:] + widened[:, 1:-1, :-2]
    total = total + padded[:, 1:-1, 1:-1, 2:] + padded[:, 1:-1, 1:-1, :-2]
    return total


def lookup(grain_ids, table):
    result = jnp.zeros(grain_ids.shape, jnp.float32)
    for index in range(NMAT):
        result = result + (grain_ids == index).astype(jnp.float32) * table[index]
    return result


def reset_planes(values, lower, upper, edge):
    size_x = values.shape[1]
    size_y = values.shape[2]
    values = values.at[:, edge : size_x - edge, edge : size_y - edge, 0].set(lower)
    return values.at[:, edge : size_x - edge, edge : size_y - edge, -1].set(upper)


def body(magnet, grain_ids, exch_table, sat_table, surface_map, near_list, near_blocks):
    cells_x = magnet.shape[1]
    cells_y = magnet.shape[2]
    exch_coef = lookup(grain_ids, exch_table)
    sat_coef = lookup(grain_ids, sat_table)
    widened = padded_2(magnet, (("gx", 1), ("gy", 2)), 1)
    laplace = near_sum(widened) - 6.0 * magnet
    padded = jnp.pad(widened, ((0, 0), (0, 0), (0, 0), (1, 1)))
    diverge = (
        widened[0, 2:, 1:-1]
        - widened[0, :-2, 1:-1]
        + widened[1, 1:-1, 2:]
        - widened[1, 1:-1, :-2]
        + padded[2, 1:-1, 1:-1, 2:]
        - padded[2, 1:-1, 1:-1, :-2]
    ) * 0.5
    source = (-sat_coef * diverge)[None]
    scalar = jnp.zeros(source.shape, jnp.float32)
    for sweep in range(SWEEPS):
        beside_all = padded_2(scalar, (("gx", 1), ("gy", 2)), 1)
        scalar = (near_sum(beside_all) + source) / DIAG
    face_vals = jnp.stack([scalar[0, :, :, 0], scalar[0, :, :, -1]]).reshape(2, cells_x * cells_y)
    node_map = surface_map[:, 0, :]
    panels = jnp.take_along_axis(face_vals, node_map, axis=1)
    low_panels = panels.astype(jnp.bfloat16)
    local_list = near_list[0]
    blank_pick = jnp.zeros((local_list.shape[0], local_list.shape[1], NODES), jnp.bfloat16)
    piece = lax.all_gather(low_panels, "gy", axis=0, tiled=True)
    inside = (local_list >= 0) & (local_list < piece.shape[0])
    picked = piece[jnp.clip(local_list, 0, piece.shape[0] - 1)]
    chosen = jnp.where(inside[:, :, None], picked, blank_pick)
    double = (
        jnp.einsum("tkij,tkj->ti", near_blocks[0], chosen, preferred_element_type=jnp.float32)
        - 0.5 * panels
    )
    row_index = jnp.arange(2, dtype=jnp.int32)[:, None]
    cells = jnp.zeros((2, cells_x * cells_y), jnp.float32).at[row_index, node_map].set(double)
    planes = cells.reshape(2, cells_x, cells_y)
    empty = jnp.zeros((cells_x, cells_y), jnp.float32)
    lower = jnp.stack([planes[0], empty])
    upper = jnp.stack([empty, planes[1]])
    extend = reset_planes(
        jnp.zeros((lower.shape[0],) + scalar.shape[1:], jnp.float32), lower, upper, 0
    )
    for sweep in range(EXT_SWEEPS):
        beside_all = padded_2(extend.astype(jnp.bfloat16), (("gx", 1), ("gy", 2)), 1).astype(
            extend.dtype
        )
        extend = reset_planes(near_sum(beside_all) / DIAG, lower, upper, 0)
    potential = scalar[0] + extend[0] + extend[1]
    beside_all = padded_2(potential[None].astype(jnp.bfloat16), (("gx", 1), ("gy", 2)), 1).astype(
        jnp.float32
    )
    padded = jnp.pad(beside_all, ((0, 0), (0, 0), (0, 0), (1, 1)))
    grad_x = (beside_all[0, 2:, 1:-1] - beside_all[0, :-2, 1:-1]) * 0.5
    grad_y = (beside_all[0, 1:-1, 2:] - beside_all[0, 1:-1, :-2]) * 0.5
    grad_z = (padded[0, 1:-1, 1:-1, 2:] - padded[0, 1:-1, 1:-1, :-2]) * 0.5
    field = exch_coef[None] * laplace - jnp.stack([grad_x, grad_y, grad_z])
    return (field, potential)


def solution(mesh):
    return jax.shard_map(
        body,
        mesh=mesh,
        in_specs=(
            P(None, "gx", "gy", None),
            P("gx", "gy", None),
            P(),
            P(),
            P("gx", "gy", None),
            P("gx", "gy", None),
            P("gx", "gy", None, None, None),
        ),
        out_specs=(P(None, "gx", "gy", None), P("gx", "gy", None)),
        check_vma=False,
    )
```

profile of v0, /device:TPU:125, one launch (start us, length us, event | category | flops | bytes accessed | tf_op | source)
XLA Modules:
  0.0 332.2 jit_solution(17468871267090058179)
XLA Ops:
  0.7 5.4 %collective-permute-start.5 = (f32[1,1,16,128]{3,2,1,0:T(8,128)S(1)}, f32[1,1,16,128]{3,2,1,0:T(8,128)S(1)}, u32[]{:S(2)}, u32[]{:S(2)}) collective-permute-start(f32[1,1,16,128]{3,2,1,0:T(8,128)S(1)} %broadcast.309), channel_id=1, source_target_pairs={{0,8},{8,16},{16,24},{24,32},{32,40},{40,48},{48,56},{56,64},{64,7... | collective-permute-start | bytes 24584 | tf_op jit(solution)/shard_map/ppermute | solution.py:21
  11.4 6.7 %collective-permute-start.1 = (f32[3,1,16,128]{3,2,1,0:T(8,128)S(1)}, f32[3,1,16,128]{3,2,1,0:T(8,128)S(1)}, u32[]{:S(2)}, u32[]{:S(2)}) collective-permute-start(f32[3,1,16,128]{3,2,1,0:T(8,128)S(1)} %get-tuple-element.151), channel_id=1, source_target_pairs={{0,8},{8,16},{16,24},{24,32},{32,40},{40,48},{48,56},{56,64},{64,7... | collective-permute-start | bytes 73736 | tf_op jit(solution)/shard_map/ppermute | solution.py:21
  22.1 3.4 %collective-permute-start.7 = (f32[1,10,1,128]{3,2,1,0:T(1,128)S(1)}, f32[1,10,1,128]{3,2,1,0:T(1,128)S(1)}, u32[]{:S(2)}, u32[]{:S(2)}) collective-permute-start(f32[1,10,1,128]{3,2,1,0:T(1,128)S(1)} %get-tuple-element.177), channel_id=1, source_target_pairs={{0,1},{1,2},{2,3},{3,4},{4,5},{5,6},{6,7},{8,9},{9,10},{10,11},{11... | collective-permute-start | bytes 15368 | tf_op jit(solution)/shard_map/ppermute | solution.py:21
  29.9 5.0 %collective-permute-start.3 = (f32[3,10,1,128]{3,2,1,0:T(1,128)S(1)}, f32[3,10,1,128]{3,2,1,0:T(1,128)S(1)}, u32[]{:S(2)}, u32[]{:S(2)}) collective-permute-start(f32[3,10,1,128]{3,2,1,0:T(1,128)S(1)} %get-tuple-element.144), channel_id=1, source_target_pairs={{0,1},{1,2},{2,3},{3,4},{4,5},{5,6},{6,7},{8,9},{9,10},{10,11},{11... | collective-permute-start | bytes 46088 | tf_op jit(solution)/shard_map/ppermute | solution.py:21
  38.8 4.1 %collective-permute-start.9 = (f32[1,1,16,128]{3,2,1,0:T(8,128)S(1)}, f32[1,1,16,128]{3,2,1,0:T(8,128)S(1)}, u32[]{:S(2)}, u32[]{:S(2)}) collective-permute-start(f32[1,1,16,128]{3,2,1,0:T(8,128)S(1)} %get-tuple-element.199), channel_id=1, source_target_pairs={{0,8},{8,16},{16,24},{24,32},{32,40},{40,48},{48,56},{56,64},{64,7... | collective-permute-start | bytes 24584 | tf_op jit(solution)/shard_map/ppermute | solution.py:21
  44.9 6.6 %collective-permute-done.8 = f32[1,1,16,128]{3,2,1,0:T(8,128)S(1)} collective-permute-done((f32[1,1,16,128]{3,2,1,0:T(8,128)S(1)}, f32[1,1,16,128]{3,2,1,0:T(8,128)S(1)}, u32[]{:S(2)}, u32[]{:S(2)}) %collective-permute-start.8) | collective-permute-done | bytes 8224 | tf_op jit(solution)/shard_map/ppermute | solution.py:24
  51.5 6.6 %collective-permute-start.11 = (f32[1,10,1,128]{3,2,1,0:T(1,128)S(1)}, f32[1,10,1,128]{3,2,1,0:T(1,128)S(1)}, u32[]{:S(2)}, u32[]{:S(2)}) collective-permute-start(f32[1,10,1,128]{3,2,1,0:T(1,128)S(1)} %get-tuple-element.175), channel_id=1, source_target_pairs={{0,1},{1,2},{2,3},{3,4},{4,5},{5,6},{6,7},{8,9},{9,10},{10,11},{11... | collective-permute-start | bytes 15368 | tf_op jit(solution)/shard_map/ppermute | solution.py:21
  60.1 4.5 %collective-permute-done.10 = f32[1,10,1,128]{3,2,1,0:T(1,128)S(1)} collective-permute-done((f32[1,10,1,128]{3,2,1,0:T(1,128)S(1)}, f32[1,10,1,128]{3,2,1,0:T(1,128)S(1)}, u32[]{:S(2)}, u32[]{:S(2)}) %collective-permute-start.10) | collective-permute-done | bytes 5152 | tf_op jit(solution)/shard_map/ppermute | solution.py:24
  69.6 6.6 %collective-permute-done.12 = f32[1,1,16,128]{3,2,1,0:T(8,128)S(1)} collective-permute-done((f32[1,1,16,128]{3,2,1,0:T(8,128)S(1)}, f32[1,1,16,128]{3,2,1,0:T(8,128)S(1)}, u32[]{:S(2)}, u32[]{:S(2)}) %collective-permute-start.12) | collective-permute-done | bytes 8224 | tf_op jit(solution)/shard_map/ppermute | solution.py:24
  78.3 3.3 collective-permute-start.14
  90.0 6.6 %collective-permute-done.16 = f32[1,1,16,128]{3,2,1,0:T(8,128)S(1)} collective-permute-done((f32[1,1,16,128]{3,2,1,0:T(8,128)S(1)}, f32[1,1,16,128]{3,2,1,0:T(8,128)S(1)}, u32[]{:S(2)}, u32[]{:S(2)}) %collective-permute-start.16) | collective-permute-done | bytes 8224 | tf_op jit(solution)/shard_map/ppermute | solution.py:24
  98.7 3.3 collective-permute-start.18
  110.4 6.6 %collective-permute-done.20 = f32[1,1,16,128]{3,2,1,0:T(8,128)S(1)} collective-permute-done((f32[1,1,16,128]{3,2,1,0:T(8,128)S(1)}, f32[1,1,16,128]{3,2,1,0:T(8,128)S(1)}, u32[]{:S(2)}, u32[]{:S(2)}) %collective-permute-start.20) | collective-permute-done | bytes 8224 | tf_op jit(solution)/shard_map/ppermute | solution.py:24
  119.1 3.3 collective-permute-start.22
  130.8 6.6 %collective-permute-done.24 = f32[1,1,16,128]{3,2,1,0:T(8,128)S(1)} collective-permute-done((f32[1,1,16,128]{3,2,1,0:T(8,128)S(1)}, f32[1,1,16,128]{3,2,1,0:T(8,128)S(1)}, u32[]{:S(2)}, u32[]{:S(2)}) %collective-permute-start.24) | collective-permute-done | bytes 8224 | tf_op jit(solution)/shard_map/ppermute | solution.py:24
  139.5 3.3 collective-permute-start.26
  151.2 6.6 %collective-permute-done.28 = f32[1,1,16,128]{3,2,1,0:T(8,128)S(1)} collective-permute-done((f32[1,1,16,128]{3,2,1,0:T(8,128)S(1)}, f32[1,1,16,128]{3,2,1,0:T(8,128)S(1)}, u32[]{:S(2)}, u32[]{:S(2)}) %collective-permute-start.28) | collective-permute-done | bytes 8224 | tf_op jit(solution)/shard_map/ppermute | solution.py:24
  171.7 6.6 %collective-permute-done.32 = f32[1,1,16,128]{3,2,1,0:T(8,128)S(1)} collective-permute-done((f32[1,1,16,128]{3,2,1,0:T(8,128)S(1)}, f32[1,1,16,128]{3,2,1,0:T(8,128)S(1)}, u32[]{:S(2)}, u32[]{:S(2)}) %collective-permute-start.32) | collective-permute-done | bytes 8224 | tf_op jit(solution)/shard_map/ppermute | solution.py:24
  189.8 11.4 %all-gather = bf16[8,2,128]{2,1,0:T(2,128)(2,1)S(1)} all-gather(bf16[1,2,128]{2,1,0:T(2,128)(2,1)S(1)} %get-tuple-element.139), channel_id=1, replica_groups=mesh['gx'=32,'gy'=8] {'gy'}, dimensions={0}, use_global_device_ids=true | all-gather | bytes 4608 | tf_op jit(solution)/shard_map/all_gather | solution.py:78
  202.1 11.5 %scatter_fusion = f32[2,128]{1,0:T(2,128)S(1)} fusion(f32[2,128]{1,0:T(2,128)S(1)} %broadcast_in_dim.38, s32[256]{0:T(256)S(1)} %get-tuple-element.210, f32[256]{0:T(256)S(1)} %subtract_bitcast_fusion), kind=kCustom, calls=%fused_computation.2 | custom fusion | bytes 5120 | tf_op jit(solution)/shard_map/scatter | solution.py:87
  215.3 6.5 %collective-permute-start.36 = (bf16[2,1,16,128]{3,2,1,0:T(8,128)(2,1)S(1)}, bf16[2,1,16,128]{3,2,1,0:T(8,128)(2,1)S(1)}, u32[]{:S(2)}, u32[]{:S(2)}) collective-permute-start(bf16[2,1,16,128]{3,2,1,0:T(8,128)(2,1)S(1)} %get-tuple-element.185), channel_id=1, source_target_pairs={{0,8},{8,16},{16,24},{24,32},{32,40},{40,48},{48,56},{56,64},{64,7... | collective-permute-start | bytes 24584 | tf_op jit(solution)/shard_map/ppermute | solution.py:21
  223.8 6.6 %collective-permute-done.37 = bf16[2,1,16,128]{3,2,1,0:T(8,128)(2,1)S(1)} collective-permute-done((bf16[2,1,16,128]{3,2,1,0:T(8,128)(2,1)S(1)}, bf16[2,1,16,128]{3,2,1,0:T(8,128)(2,1)S(1)}, u32[]{:S(2)}, u32[]{:S(2)}) %collective-permute-start.37) | collective-permute-done | bytes 8224 | tf_op jit(solution)/shard_map/ppermute | solution.py:24
  232.4 6.6 %collective-permute-start.38 = (bf16[2,10,1,128]{3,0,2,1:T(2,128)(2,1)S(1)}, bf16[2,10,1,128]{3,0,2,1:T(2,128)(2,1)S(1)}, u32[]{:S(2)}, u32[]{:S(2)}) collective-permute-start(bf16[2,10,1,128]{3,0,2,1:T(2,128)(2,1)S(1)} %copy.588), channel_id=1, source_target_pairs={{0,1},{1,2},{2,3},{3,4},{4,5},{5,6},{6,7},{8,9},{9,10},{10,11},{11... | collective-permute-start | bytes 15368 | tf_op jit(solution)/shard_map/ppermute | solution.py:21
  245.7 6.4 %collective-permute-done.41 = bf16[2,1,16,128]{3,2,1,0:T(8,128)(2,1)S(1)} collective-permute-done((bf16[2,1,16,128]{3,2,1,0:T(8,128)(2,1)S(1)}, bf16[2,1,16,128]{3,2,1,0:T(8,128)(2,1)S(1)}, u32[]{:S(2)}, u32[]{:S(2)}) %collective-permute-start.41) | collective-permute-done | bytes 8224 | tf_op jit(solution)/shard_map/ppermute | solution.py:24
  254.1 6.6 %collective-permute-start.42 = (bf16[2,10,1,128]{3,0,2,1:T(2,128)(2,1)S(1)}, bf16[2,10,1,128]{3,0,2,1:T(2,128)(2,1)S(1)}, u32[]{:S(2)}, u32[]{:S(2)}) collective-permute-start(bf16[2,10,1,128]{3,0,2,1:T(2,128)(2,1)S(1)} %copy.594), channel_id=1, source_target_pairs={{0,1},{1,2},{2,3},{3,4},{4,5},{5,6},{6,7},{8,9},{9,10},{10,11},{11... | collective-permute-start | bytes 15368 | tf_op jit(solution)/shard_map/ppermute | solution.py:21
  267.5 6.4 %collective-permute-done.45 = bf16[2,1,16,128]{3,2,1,0:T(8,128)(2,1)S(1)} collective-permute-done((bf16[2,1,16,128]{3,2,1,0:T(8,128)(2,1)S(1)}, bf16[2,1,16,128]{3,2,1,0:T(8,128)(2,1)S(1)}, u32[]{:S(2)}, u32[]{:S(2)}) %collective-permute-start.45) | collective-permute-done | bytes 8224 | tf_op jit(solution)/shard_map/ppermute | solution.py:24
  275.9 6.6 %collective-permute-start.46 = (bf16[2,10,1,128]{3,0,2,1:T(2,128)(2,1)S(1)}, bf16[2,10,1,128]{3,0,2,1:T(2,128)(2,1)S(1)}, u32[]{:S(2)}, u32[]{:S(2)}) collective-permute-start(bf16[2,10,1,128]{3,0,2,1:T(2,128)(2,1)S(1)} %copy.600), channel_id=1, source_target_pairs={{0,1},{1,2},{2,3},{3,4},{4,5},{5,6},{6,7},{8,9},{9,10},{10,11},{11... | collective-permute-start | bytes 15368 | tf_op jit(solution)/shard_map/ppermute | solution.py:21
  289.2 6.4 %collective-permute-done.49 = bf16[2,1,16,128]{3,2,1,0:T(8,128)(2,1)S(1)} collective-permute-done((bf16[2,1,16,128]{3,2,1,0:T(8,128)(2,1)S(1)}, bf16[2,1,16,128]{3,2,1,0:T(8,128)(2,1)S(1)}, u32[]{:S(2)}, u32[]{:S(2)}) %collective-permute-start.49) | collective-permute-done | bytes 8224 | tf_op jit(solution)/shard_map/ppermute | solution.py:24
  297.6 6.6 %collective-permute-start.50 = (bf16[2,10,1,128]{3,0,2,1:T(2,128)(2,1)S(1)}, bf16[2,10,1,128]{3,0,2,1:T(2,128)(2,1)S(1)}, u32[]{:S(2)}, u32[]{:S(2)}) collective-permute-start(bf16[2,10,1,128]{3,0,2,1:T(2,128)(2,1)S(1)} %copy.606), channel_id=1, source_target_pairs={{0,1},{1,2},{2,3},{3,4},{4,5},{5,6},{6,7},{8,9},{9,10},{10,11},{11... | collective-permute-start | bytes 15368 | tf_op jit(solution)/shard_map/ppermute | solution.py:21
  311.6 6.4 %collective-permute-done.53 = bf16[1,1,16,128]{3,2,1,0:T(8,128)(2,1)S(1)} collective-permute-done((bf16[1,1,16,128]{3,2,1,0:T(8,128)(2,1)S(1)}, bf16[1,1,16,128]{3,2,1,0:T(8,128)(2,1)S(1)}, u32[]{:S(2)}, u32[]{:S(2)}) %collective-permute-start.53) | collective-permute-done | bytes 4128 | tf_op jit(solution)/shard_map/ppermute | solution.py:24
  318.0 6.6 %collective-permute-start.54 = (bf16[1,10,1,128]{3,2,1,0:T(2,128)(2,1)S(1)}, bf16[1,10,1,128]{3,2,1,0:T(2,128)(2,1)S(1)}, u32[]{:S(2)}, u32[]{:S(2)}) collective-permute-start(bf16[1,10,1,128]{3,2,1,0:T(2,128)(2,1)S(1)} %get-tuple-element.201), channel_id=1, source_target_pairs={{0,1},{1,2},{2,3},{3,4},{4,5},{5,6},{6,7},{8,9},{9,10},{10,11},{11... | collective-permute-start | bytes 7688 | tf_op jit(solution)/shard_map/ppermute | solution.py:21
  326.6 4.5 %collective-permute-done.55 = bf16[1,10,1,128]{3,2,1,0:T(2,128)(2,1)S(1)} collective-permute-done((bf16[1,10,1,128]{3,2,1,0:T(2,128)(2,1)S(1)}, bf16[1,10,1,128]{3,2,1,0:T(2,128)(2,1)S(1)}, u32[]{:S(2)}, u32[]{:S(2)}) %collective-permute-start.55) | collective-permute-done | bytes 2592 | tf_op jit(solution)/shard_map/ppermute | solution.py:24
  (209 shorter events, 135.5 us)
Async XLA Ops:
  0.7 21.4 %collective-permute-start.5 = (f32[1,1,16,128]{3,2,1,0:T(8,128)S(1)}, f32[1,1,16,128]{3,2,1,0:T(8,128)S(1)}, u32[]{:S(2)}, u32[]{:S(2)}) collective-permute-start(f32[1,1,16,128]{3,2,1,0:T(8,128)S(1)} %broadcast.309), channel_id=1, source_target_pairs={{0,8},{8,16},{16,24},{24,32},{32,40},{40,48},{48,56},{56,64},{64,7... | collective-permute-start | bytes 24584 | tf_op jit(solution)/shard_map/ppermute | solution.py:21
  6.1 16.0 %collective-permute-start.4 = (f32[1,1,16,128]{3,2,1,0:T(8,128)S(1)}, f32[1,1,16,128]{3,2,1,0:T(8,128)S(1)}, u32[]{:S(2)}, u32[]{:S(2)}) collective-permute-start(f32[1,1,16,128]{3,2,1,0:T(8,128)S(1)} %broadcast.309), channel_id=1, source_target_pairs={{8,0},{16,8},{24,16},{32,24},{40,32},{48,40},{56,48},{64,56},{72,6... | collective-permute-start | bytes 24584 | tf_op jit(solution)/shard_map/ppermute | solution.py:24
  8.8 18.7 %collective-permute-start = (f32[3,1,16,128]{3,2,1,0:T(8,128)S(1)}, f32[3,1,16,128]{3,2,1,0:T(8,128)S(1)}, u32[]{:S(2)}, u32[]{:S(2)}) collective-permute-start(f32[3,1,16,128]{3,2,1,0:T(8,128)S(1)} %get-tuple-element.150), channel_id=1, source_target_pairs={{8,0},{16,8},{24,16},{32,24},{40,32},{48,40},{56,48},{64,56},{72,6... | collective-permute-start | bytes 73736 | tf_op jit(solution)/shard_map/ppermute | solution.py:24
  11.4 16.0 %collective-permute-start.1 = (f32[3,1,16,128]{3,2,1,0:T(8,128)S(1)}, f32[3,1,16,128]{3,2,1,0:T(8,128)S(1)}, u32[]{:S(2)}, u32[]{:S(2)}) collective-permute-start(f32[3,1,16,128]{3,2,1,0:T(8,128)S(1)} %get-tuple-element.151), channel_id=1, source_target_pairs={{0,8},{8,16},{16,24},{24,32},{32,40},{40,48},{48,56},{56,64},{64,7... | collective-permute-start | bytes 73736 | tf_op jit(solution)/shard_map/ppermute | solution.py:21
  22.1 12.9 %collective-permute-start.7 = (f32[1,10,1,128]{3,2,1,0:T(1,128)S(1)}, f32[1,10,1,128]{3,2,1,0:T(1,128)S(1)}, u32[]{:S(2)}, u32[]{:S(2)}) collective-permute-start(f32[1,10,1,128]{3,2,1,0:T(1,128)S(1)} %get-tuple-element.177), channel_id=1, source_target_pairs={{0,1},{1,2},{2,3},{3,4},{4,5},{5,6},{6,7},{8,9},{9,10},{10,11},{11... | collective-permute-start | bytes 15368 | tf_op jit(solution)/shard_map/ppermute | solution.py:21
  25.5 9.5 %collective-permute-start.6 = (f32[1,10,1,128]{3,2,1,0:T(1,128)S(1)}, f32[1,10,1,128]{3,2,1,0:T(1,128)S(1)}, u32[]{:S(2)}, u32[]{:S(2)}) collective-permute-start(f32[1,10,1,128]{3,2,1,0:T(1,128)S(1)} %get-tuple-element.178), channel_id=1, source_target_pairs={{1,0},{2,1},{3,2},{4,3},{5,4},{6,5},{7,6},{9,8},{10,9},{11,10},{12... | collective-permute-start | bytes 15368 | tf_op jit(solution)/shard_map/ppermute | solution.py:24
  27.5 7.6 %collective-permute-start.2 = (f32[3,10,1,128]{3,2,1,0:T(1,128)S(1)}, f32[3,10,1,128]{3,2,1,0:T(1,128)S(1)}, u32[]{:S(2)}, u32[]{:S(2)}) collective-permute-start(f32[3,10,1,128]{3,2,1,0:T(1,128)S(1)} %get-tuple-element.143), channel_id=1, source_target_pairs={{1,0},{2,1},{3,2},{4,3},{5,4},{6,5},{7,6},{9,8},{10,9},{11,10},{12... | collective-permute-start | bytes 46088 | tf_op jit(solution)/shard_map/ppermute | solution.py:24
  42.9 8.6 %collective-permute-start.8 = (f32[1,1,16,128]{3,2,1,0:T(8,128)S(1)}, f32[1,1,16,128]{3,2,1,0:T(8,128)S(1)}, u32[]{:S(2)}, u32[]{:S(2)}) collective-permute-start(f32[1,1,16,128]{3,2,1,0:T(8,128)S(1)} %get-tuple-element.200), channel_id=1, source_target_pairs={{8,0},{16,8},{24,16},{32,24},{40,32},{48,40},{56,48},{64,56},{72,6... | collective-permute-start | bytes 24584 | tf_op jit(solution)/shard_map/ppermute | solution.py:24
  51.5 8.6 %collective-permute-start.11 = (f32[1,10,1,128]{3,2,1,0:T(1,128)S(1)}, f32[1,10,1,128]{3,2,1,0:T(1,128)S(1)}, u32[]{:S(2)}, u32[]{:S(2)}) collective-permute-start(f32[1,10,1,128]{3,2,1,0:T(1,128)S(1)} %get-tuple-element.175), channel_id=1, source_target_pairs={{0,1},{1,2},{2,3},{3,4},{4,5},{5,6},{6,7},{8,9},{9,10},{10,11},{11... | collective-permute-start | bytes 15368 | tf_op jit(solution)/shard_map/ppermute | solution.py:21
  58.2 6.5 %collective-permute-start.10 = (f32[1,10,1,128]{3,2,1,0:T(1,128)S(1)}, f32[1,10,1,128]{3,2,1,0:T(1,128)S(1)}, u32[]{:S(2)}, u32[]{:S(2)}) collective-permute-start(f32[1,10,1,128]{3,2,1,0:T(1,128)S(1)} %get-tuple-element.176), channel_id=1, source_target_pairs={{1,0},{2,1},{3,2},{4,3},{5,4},{6,5},{7,6},{9,8},{10,9},{11,10},{12... | collective-permute-start | bytes 15368 | tf_op jit(solution)/shard_map/ppermute | solution.py:24
  67.7 8.6 %collective-permute-start.12 = (f32[1,1,16,128]{3,2,1,0:T(8,128)S(1)}, f32[1,1,16,128]{3,2,1,0:T(8,128)S(1)}, u32[]{:S(2)}, u32[]{:S(2)}) collective-permute-start(f32[1,1,16,128]{3,2,1,0:T(8,128)S(1)} %get-tuple-element.198), channel_id=1, source_target_pairs={{8,0},{16,8},{24,16},{32,24},{40,32},{48,40},{56,48},{64,56},{72,6... | collective-permute-start | bytes 24584 | tf_op jit(solution)/shard_map/ppermute | solution.py:24
  88.1 8.6 %collective-permute-start.16 = (f32[1,1,16,128]{3,2,1,0:T(8,128)S(1)}, f32[1,1,16,128]{3,2,1,0:T(8,128)S(1)}, u32[]{:S(2)}, u32[]{:S(2)}) collective-permute-start(f32[1,1,16,128]{3,2,1,0:T(8,128)S(1)} %get-tuple-element.196), channel_id=1, source_target_pairs={{8,0},{16,8},{24,16},{32,24},{40,32},{48,40},{56,48},{64,56},{72,6... | collective-permute-start | bytes 24584 | tf_op jit(solution)/shard_map/ppermute | solution.py:24
  108.5 8.6 %collective-permute-start.20 = (f32[1,1,16,128]{3,2,1,0:T(8,128)S(1)}, f32[1,1,16,128]{3,2,1,0:T(8,128)S(1)}, u32[]{:S(2)}, u32[]{:S(2)}) collective-permute-start(f32[1,1,16,128]{3,2,1,0:T(8,128)S(1)} %get-tuple-element.194), channel_id=1, source_target_pairs={{8,0},{16,8},{24,16},{32,24},{40,32},{48,40},{56,48},{64,56},{72,6... | collective-permute-start | bytes 24584 | tf_op jit(solution)/shard_map/ppermute | solution.py:24
  119.1 6.5 %collective-permute-start.22 = (f32[1,10,1,128]{3,2,1,0:T(1,128)S(1)}, f32[1,10,1,128]{3,2,1,0:T(1,128)S(1)}, u32[]{:S(2)}, u32[]{:S(2)}) collective-permute-start(f32[1,10,1,128]{3,2,1,0:T(1,128)S(1)} %get-tuple-element.170), channel_id=1, source_target_pairs={{1,0},{2,1},{3,2},{4,3},{5,4},{6,5},{7,6},{9,8},{10,9},{11,10},{12... | collective-permute-start | bytes 15368 | tf_op jit(solution)/shard_map/ppermute | solution.py:24
  128.9 8.6 %collective-permute-start.24 = (f32[1,1,16,128]{3,2,1,0:T(8,128)S(1)}, f32[1,1,16,128]{3,2,1,0:T(8,128)S(1)}, u32[]{:S(2)}, u32[]{:S(2)}) collective-permute-start(f32[1,1,16,128]{3,2,1,0:T(8,128)S(1)} %get-tuple-element.192), channel_id=1, source_target_pairs={{8,0},{16,8},{24,16},{32,24},{40,32},{48,40},{56,48},{64,56},{72,6... | collective-permute-start | bytes 24584 | tf_op jit(solution)/shard_map/ppermute | solution.py:24
  149.3 8.6 %collective-permute-start.28 = (f32[1,1,16,128]{3,2,1,0:T(8,128)S(1)}, f32[1,1,16,128]{3,2,1,0:T(8,128)S(1)}, u32[]{:S(2)}, u32[]{:S(2)}) collective-permute-start(f32[1,1,16,128]{3,2,1,0:T(8,128)S(1)} %get-tuple-element.190), channel_id=1, source_target_pairs={{8,0},{16,8},{24,16},{32,24},{40,32},{48,40},{56,48},{64,56},{72,6... | collective-permute-start | bytes 24584 | tf_op jit(solution)/shard_map/ppermute | solution.py:24
  169.7 8.6 %collective-permute-start.32 = (f32[1,1,16,128]{3,2,1,0:T(8,128)S(1)}, f32[1,1,16,128]{3,2,1,0:T(8,128)S(1)}, u32[]{:S(2)}, u32[]{:S(2)}) collective-permute-start(f32[1,1,16,128]{3,2,1,0:T(8,128)S(1)} %get-tuple-element.188), channel_id=1, source_target_pairs={{8,0},{16,8},{24,16},{32,24},{40,32},{48,40},{56,48},{64,56},{72,6... | collective-permute-start | bytes 24584 | tf_op jit(solution)/shard_map/ppermute | solution.py:24
  215.3 8.4 %collective-permute-start.36 = (bf16[2,1,16,128]{3,2,1,0:T(8,128)(2,1)S(1)}, bf16[2,1,16,128]{3,2,1,0:T(8,128)(2,1)S(1)}, u32[]{:S(2)}, u32[]{:S(2)}) collective-permute-start(bf16[2,1,16,128]{3,2,1,0:T(8,128)(2,1)S(1)} %get-tuple-element.185), channel_id=1, source_target_pairs={{0,8},{8,16},{16,24},{24,32},{32,40},{40,48},{48,56},{56,64},{64,7... | collective-permute-start | bytes 24584 | tf_op jit(solution)/shard_map/ppermute | solution.py:21
  221.8 8.6 %collective-permute-start.37 = (bf16[2,1,16,128]{3,2,1,0:T(8,128)(2,1)S(1)}, bf16[2,1,16,128]{3,2,1,0:T(8,128)(2,1)S(1)}, u32[]{:S(2)}, u32[]{:S(2)}) collective-permute-start(bf16[2,1,16,128]{3,2,1,0:T(8,128)(2,1)S(1)} %get-tuple-element.186), channel_id=1, source_target_pairs={{8,0},{16,8},{24,16},{32,24},{40,32},{48,40},{56,48},{64,56},{72,6... | collective-permute-start | bytes 24584 | tf_op jit(solution)/shard_map/ppermute | solution.py:24
  230.5 8.6 %collective-permute-start.39 = (bf16[2,10,1,128]{3,0,2,1:T(2,128)(2,1)S(1)}, bf16[2,10,1,128]{3,0,2,1:T(2,128)(2,1)S(1)}, u32[]{:S(2)}, u32[]{:S(2)}) collective-permute-start(bf16[2,10,1,128]{3,0,2,1:T(2,128)(2,1)S(1)} %copy.589), channel_id=1, source_target_pairs={{1,0},{2,1},{3,2},{4,3},{5,4},{6,5},{7,6},{9,8},{10,9},{11,10},{12... | collective-permute-start | bytes 15368 | tf_op jit(solution)/shard_map/ppermute | solution.py:24
  232.4 7.4 %collective-permute-start.38 = (bf16[2,10,1,128]{3,0,2,1:T(2,128)(2,1)S(1)}, bf16[2,10,1,128]{3,0,2,1:T(2,128)(2,1)S(1)}, u32[]{:S(2)}, u32[]{:S(2)}) collective-permute-start(bf16[2,10,1,128]{3,0,2,1:T(2,128)(2,1)S(1)} %copy.588), channel_id=1, source_target_pairs={{0,1},{1,2},{2,3},{3,4},{4,5},{5,6},{6,7},{8,9},{9,10},{10,11},{11... | collective-permute-start | bytes 15368 | tf_op jit(solution)/shard_map/ppermute | solution.py:21
  243.6 8.6 %collective-permute-start.41 = (bf16[2,1,16,128]{3,2,1,0:T(8,128)(2,1)S(1)}, bf16[2,1,16,128]{3,2,1,0:T(8,128)(2,1)S(1)}, u32[]{:S(2)}, u32[]{:S(2)}) collective-permute-start(bf16[2,1,16,128]{3,2,1,0:T(8,128)(2,1)S(1)} %get-tuple-element.184), channel_id=1, source_target_pairs={{8,0},{16,8},{24,16},{32,24},{40,32},{48,40},{56,48},{64,56},{72,6... | collective-permute-start | bytes 24584 | tf_op jit(solution)/shard_map/ppermute | solution.py:24
  252.2 8.6 %collective-permute-start.43 = (bf16[2,10,1,128]{3,0,2,1:T(2,128)(2,1)S(1)}, bf16[2,10,1,128]{3,0,2,1:T(2,128)(2,1)S(1)}, u32[]{:S(2)}, u32[]{:S(2)}) collective-permute-start(bf16[2,10,1,128]{3,0,2,1:T(2,128)(2,1)S(1)} %copy.595), channel_id=1, source_target_pairs={{1,0},{2,1},{3,2},{4,3},{5,4},{6,5},{7,6},{9,8},{10,9},{11,10},{12... | collective-permute-start | bytes 15368 | tf_op jit(solution)/shard_map/ppermute | solution.py:24
  254.1 7.4 %collective-permute-start.42 = (bf16[2,10,1,128]{3,0,2,1:T(2,128)(2,1)S(1)}, bf16[2,10,1,128]{3,0,2,1:T(2,128)(2,1)S(1)}, u32[]{:S(2)}, u32[]{:S(2)}) collective-permute-start(bf16[2,10,1,128]{3,0,2,1:T(2,128)(2,1)S(1)} %copy.594), channel_id=1, source_target_pairs={{0,1},{1,2},{2,3},{3,4},{4,5},{5,6},{6,7},{8,9},{9,10},{10,11},{11... | collective-permute-start | bytes 15368 | tf_op jit(solution)/shard_map/ppermute | solution.py:21
  265.3 8.6 %collective-permute-start.45 = (bf16[2,1,16,128]{3,2,1,0:T(8,128)(2,1)S(1)}, bf16[2,1,16,128]{3,2,1,0:T(8,128)(2,1)S(1)}, u32[]{:S(2)}, u32[]{:S(2)}) collective-permute-start(bf16[2,1,16,128]{3,2,1,0:T(8,128)(2,1)S(1)} %get-tuple-element.182), channel_id=1, source_target_pairs={{8,0},{16,8},{24,16},{32,24},{40,32},{48,40},{56,48},{64,56},{72,6... | collective-permute-start | bytes 24584 | tf_op jit(solution)/shard_map/ppermute | solution.py:24
  273.9 8.6 %collective-permute-start.47 = (bf16[2,10,1,128]{3,0,2,1:T(2,128)(2,1)S(1)}, bf16[2,10,1,128]{3,0,2,1:T(2,128)(2,1)S(1)}, u32[]{:S(2)}, u32[]{:S(2)}) collective-permute-start(bf16[2,10,1,128]{3,0,2,1:T(2,128)(2,1)S(1)} %copy.601), channel_id=1, source_target_pairs={{1,0},{2,1},{3,2},{4,3},{5,4},{6,5},{7,6},{9,8},{10,9},{11,10},{12... | collective-permute-start | bytes 15368 | tf_op jit(solution)/shard_map/ppermute | solution.py:24
  275.9 7.4 %collective-permute-start.46 = (bf16[2,10,1,128]{3,0,2,1:T(2,128)(2,1)S(1)}, bf16[2,10,1,128]{3,0,2,1:T(2,128)(2,1)S(1)}, u32[]{:S(2)}, u32[]{:S(2)}) collective-permute-start(bf16[2,10,1,128]{3,0,2,1:T(2,128)(2,1)S(1)} %copy.600), channel_id=1, source_target_pairs={{0,1},{1,2},{2,3},{3,4},{4,5},{5,6},{6,7},{8,9},{9,10},{10,11},{11... | collective-permute-start | bytes 15368 | tf_op jit(solution)/shard_map/ppermute | solution.py:21
  287.1 8.6 %collective-permute-start.49 = (bf16[2,1,16,128]{3,2,1,0:T(8,128)(2,1)S(1)}, bf16[2,1,16,128]{3,2,1,0:T(8,128)(2,1)S(1)}, u32[]{:S(2)}, u32[]{:S(2)}) collective-permute-start(bf16[2,1,16,128]{3,2,1,0:T(8,128)(2,1)S(1)} %get-tuple-element.180), channel_id=1, source_target_pairs={{8,0},{16,8},{24,16},{32,24},{40,32},{48,40},{56,48},{64,56},{72,6... | collective-permute-start | bytes 24584 | tf_op jit(solution)/shard_map/ppermute | solution.py:24
  295.7 8.6 %collective-permute-start.51 = (bf16[2,10,1,128]{3,0,2,1:T(2,128)(2,1)S(1)}, bf16[2,10,1,128]{3,0,2,1:T(2,128)(2,1)S(1)}, u32[]{:S(2)}, u32[]{:S(2)}) collective-permute-start(bf16[2,10,1,128]{3,0,2,1:T(2,128)(2,1)S(1)} %copy.607), channel_id=1, source_target_pairs={{1,0},{2,1},{3,2},{4,3},{5,4},{6,5},{7,6},{9,8},{10,9},{11,10},{12... | collective-permute-start | bytes 15368 | tf_op jit(solution)/shard_map/ppermute | solution.py:24
  297.6 7.4 %collective-permute-start.50 = (bf16[2,10,1,128]{3,0,2,1:T(2,128)(2,1)S(1)}, bf16[2,10,1,128]{3,0,2,1:T(2,128)(2,1)S(1)}, u32[]{:S(2)}, u32[]{:S(2)}) collective-permute-start(bf16[2,10,1,128]{3,0,2,1:T(2,128)(2,1)S(1)} %copy.606), channel_id=1, source_target_pairs={{0,1},{1,2},{2,3},{3,4},{4,5},{5,6},{6,7},{8,9},{9,10},{10,11},{11... | collective-permute-start | bytes 15368 | tf_op jit(solution)/shard_map/ppermute | solution.py:21
  309.5 8.5 %collective-permute-start.53 = (bf16[1,1,16,128]{3,2,1,0:T(8,128)(2,1)S(1)}, bf16[1,1,16,128]{3,2,1,0:T(8,128)(2,1)S(1)}, u32[]{:S(2)}, u32[]{:S(2)}) collective-permute-start(bf16[1,1,16,128]{3,2,1,0:T(8,128)(2,1)S(1)} %get-tuple-element.204), channel_id=1, source_target_pairs={{8,0},{16,8},{24,16},{32,24},{40,32},{48,40},{56,48},{64,56},{72,6... | collective-permute-start | bytes 12296 | tf_op jit(solution)/shard_map/ppermute | solution.py:24
  318.0 8.6 %collective-permute-start.54 = (bf16[1,10,1,128]{3,2,1,0:T(2,128)(2,1)S(1)}, bf16[1,10,1,128]{3,2,1,0:T(2,128)(2,1)S(1)}, u32[]{:S(2)}, u32[]{:S(2)}) collective-permute-start(bf16[1,10,1,128]{3,2,1,0:T(2,128)(2,1)S(1)} %get-tuple-element.201), channel_id=1, source_target_pairs={{0,1},{1,2},{2,3},{3,4},{4,5},{5,6},{6,7},{8,9},{9,10},{10,11},{11... | collective-permute-start | bytes 7688 | tf_op jit(solution)/shard_map/ppermute | solution.py:21
  (31 other events, 376.8 us)
where the time goes:
time: 334 us; the launch traced here: 332 us
  starting transfers between devices  173 us (52%)
  waiting for transfers between devices  110 us (33%)
  local copies, waits for them, and re-layouts  24.5 us (7%)
  blocking collectives  11.4 us (3%)
  other arithmetic  10.4 us (3%)
    ppermute x28, starting transfers between devices, padded_2(): lax.ppermute(lax.slice_in_dim(block, block.shape[dim] - width, None, axis...  109 us
    ppermute x28, waiting for transfers between devices, padded_2(): lax.ppermute(lax.slice_in_dim(block, 0, width, axis=dim), axis, backward)  107 us
    ppermute x28, starting transfers between devices, padded_2(): lax.ppermute(lax.slice_in_dim(block, 0, width, axis=dim), axis, backward)  64 us
    scatter x1, local copies, waits for them, and re-layouts, body(): jnp.zeros((2, cells_x * cells_y), jnp.float32).at[row_index, node_map]  11.5 us
    all_gather x1, blocking collectives, body(): piece = lax.all_gather(low_panels, 'gy', axis=0, tiled=True)  11.4 us
  transfers between devices with their start and end apart: 56, of which 25 were waited for; matrix products, arithmetic and copies ran while one was open for 2% of the time, Pallas kernels for 0%

commit v1 on v0

v1 whole, which is shorter than its diff:
```python
import jax
import jax.numpy as jnp
from jax import lax
from jax.sharding import PartitionSpec as P

NODES = 128
SWEEPS = 8
EXT_SWEEPS = 4
NMAT = 4


SCREEN = 0.25
DIAG = 6.0 + SCREEN


def _pairs(count, step):
    return [(i, i + step) for i in range(count) if 0 <= i + step < count]


def _pack(arrays):
    return jnp.concatenate([a.reshape(-1) for a in arrays])


def _unpack(flat, like):
    out = []
    start = 0
    for a in like:
        out.append(flat[start : start + a.size].reshape(a.shape))
        start += a.size
    return out


def swap(axis, to_next, to_prev):
    count = lax.axis_size(axis)
    if len(to_next) == 1:
        from_prev = [lax.ppermute(to_next[0], axis, _pairs(count, 1))]
        from_next = [lax.ppermute(to_prev[0], axis, _pairs(count, -1))]
        return from_prev, from_next
    from_prev = lax.ppermute(_pack(to_next), axis, _pairs(count, 1))
    from_next = lax.ppermute(_pack(to_prev), axis, _pairs(count, -1))
    return _unpack(from_prev, to_next), _unpack(from_next, to_prev)


def widen(block, hx, hy, dx, dy):
    size_x = block.shape[dx]
    (lo,), (hi,) = swap(
        "gx",
        [lax.slice_in_dim(block, size_x - hx, size_x, axis=dx)],
        [lax.slice_in_dim(block, 0, hx, axis=dx)],
    )
    block = jnp.concatenate([lo, block, hi], axis=dx)
    size_y = block.shape[dy]
    (lo,), (hi,) = swap(
        "gy",
        [lax.slice_in_dim(block, size_y - hy, size_y, axis=dy)],
        [lax.slice_in_dim(block, 0, hy, axis=dy)],
    )
    return jnp.concatenate([lo, block, hi], axis=dy)


def zpad(a):
    return jnp.pad(a, [(0, 0)] * (a.ndim - 1) + [(1, 1)])


def near_sum(wide):
    padded = zpad(wide)
    total = wide[..., 2:, 1:-1, :] + wide[..., :-2, 1:-1, :]
    total = total + wide[..., 1:-1, 2:, :] + wide[..., 1:-1, :-2, :]
    total = total + padded[..., 1:-1, 1:-1, 2:] + padded[..., 1:-1, 1:-1, :-2]
    return total


def lookup(grain_ids, table):
    result = jnp.zeros(grain_ids.shape, jnp.float32)
    for index in range(NMAT):
        result = result + (grain_ids == index).astype(jnp.float32) * table[index]
    return result


def body(magnet, grain_ids, exch_table, sat_table, surface_map, near_list, near_blocks):
    cells_x = magnet.shape[1]
    cells_y = magnet.shape[2]
    cells_z = magnet.shape[3]
    grid_x = cells_x * lax.axis_size("gx")
    grid_y = cells_y * lax.axis_size("gy")
    base_x = lax.axis_index("gx") * cells_x
    base_y = lax.axis_index("gy") * cells_y

    def inside(h):
        xs = base_x - h + jnp.arange(cells_x + 2 * h, dtype=jnp.int32)
        ys = base_y - h + jnp.arange(cells_y + 2 * h, dtype=jnp.int32)
        ok_x = (xs >= 0) & (xs < grid_x)
        ok_y = (ys >= 0) & (ys < grid_y)
        return (ok_x[:, None] & ok_y[None, :])[:, :, None]

    exch_coef = lookup(grain_ids, exch_table)
    sat_coef = lookup(grain_ids, sat_table)

    halo = SWEEPS
    data = jnp.concatenate([magnet, sat_coef[None]], axis=0)
    wide = widen(data, halo, halo, 1, 2)
    m0, m1, m2, sat_w = wide[0], wide[1], wide[2], wide[3]

    hs = halo - 1
    ex = slice(1, 1 + cells_x + 2 * hs)
    ey = slice(1, 1 + cells_y + 2 * hs)
    m2p = zpad(m2[ex, ey])
    diverge = (
        m0[2 : 2 + cells_x + 2 * hs, ey]
        - m0[0 : cells_x + 2 * hs, ey]
        + m1[ex, 2 : 2 + cells_y + 2 * hs]
        - m1[ex, 0 : cells_y + 2 * hs]
        + m2p[:, :, 2:]
        - m2p[:, :, :-2]
    ) * 0.5
    source = -sat_w[ex, ey] * diverge

    scalar = jnp.where(inside(hs), source / DIAG, 0.0)
    for sweep in range(1, SWEEPS):
        h = hs - sweep
        off = hs - h
        src = source[off : off + cells_x + 2 * h, off : off + cells_y + 2 * h]
        value = (near_sum(scalar) + src) / DIAG
        scalar = jnp.where(inside(h), value, 0.0) if h > 0 else value

    mag_1 = wide[0:3, halo - 1 : halo + 1 + cells_x, halo - 1 : halo + 1 + cells_y]
    laplace = near_sum(mag_1) - 6.0 * magnet

    node_map = surface_map[:, 0, :]
    cell_ids = jnp.arange(cells_x * cells_y, dtype=jnp.int32)
    onehot = node_map[:, :, None] == cell_ids[None, None, :]
    face_vals = jnp.stack([scalar[:, :, 0], scalar[:, :, -1]]).reshape(2, cells_x * cells_y)
    panels = jnp.sum(jnp.where(onehot, face_vals[:, None, :], 0.0), axis=2)
    low_panels = panels.astype(jnp.bfloat16)
    local_list = near_list[0]
    blank_pick = jnp.zeros((local_list.shape[0], local_list.shape[1], NODES), jnp.bfloat16)
    piece = lax.all_gather(low_panels, "gy", axis=0, tiled=True)
    valid = (local_list >= 0) & (local_list < piece.shape[0])
    picked = piece[jnp.clip(local_list, 0, piece.shape[0] - 1)]
    chosen = jnp.where(valid[:, :, None], picked, blank_pick)
    double = (
        jnp.einsum("tkij,tkj->ti", near_blocks[0], chosen, preferred_element_type=jnp.float32)
        - 0.5 * panels
    )
    cells = jnp.sum(jnp.where(onehot, double[:, :, None], 0.0), axis=1)
    planes = cells.reshape(2, cells_x, cells_y)

    he = EXT_SWEEPS + 1
    (p_lo, s_lo), (p_hi, s_hi) = swap(
        "gx",
        [planes[:, cells_x - he :], scalar[cells_x - 1 :]],
        [planes[:, :he], scalar[:1]],
    )
    planes_x = jnp.concatenate([p_lo, planes, p_hi], axis=1)
    (q_lo, t_lo), (q_hi, t_hi) = swap(
        "gy",
        [planes_x[:, :, cells_y - he :], scalar[:, cells_y - 1 :]],
        [planes_x[:, :, :he], scalar[:, :1]],
    )
    planes_w = jnp.concatenate([q_lo, planes_x, q_hi], axis=2)

    column = jnp.concatenate([s_lo, scalar, s_hi], axis=0)
    row_pad = ((1, 1), (0, 0), (0, 0))
    scalar_1 = jnp.concatenate([jnp.pad(t_lo, row_pad), column, jnp.pad(t_hi, row_pad)], axis=1)

    z_ids = jnp.arange(cells_z, dtype=jnp.int32)
    bottom = z_ids == 0
    top = z_ids == cells_z - 1
    zero_w = jnp.zeros_like(planes_w[0])

    def reset(values, off, size_x, size_y):
        sub = planes_w[:, off : off + size_x, off : off + size_y]
        zero = zero_w[off : off + size_x, off : off + size_y]
        lower = jnp.stack([sub[0], zero])[..., None]
        upper = jnp.stack([zero, sub[1]])[..., None]
        return jnp.where(bottom, lower, jnp.where(top, upper, values))

    extend = reset(
        jnp.zeros((2,) + planes_w.shape[1:] + (cells_z,), jnp.float32),
        0,
        planes_w.shape[1],
        planes_w.shape[2],
    )
    for sweep in range(EXT_SWEEPS):
        h = he - 1 - sweep
        off = he - h
        value = jnp.where(inside(h), near_sum(extend) / DIAG, 0.0)
        extend = reset(value, off, cells_x + 2 * h, cells_y + 2 * h)

    potential_1 = scalar_1 + extend[0] + extend[1]
    potential = potential_1[1:-1, 1:-1]
    padded = zpad(potential_1)
    grad_x = (potential_1[2:, 1:-1] - potential_1[:-2, 1:-1]) * 0.5
    grad_y = (potential_1[1:-1, 2:] - potential_1[1:-1, :-2]) * 0.5
    grad_z = (padded[1:-1, 1:-1, 2:] - padded[1:-1, 1:-1, :-2]) * 0.5
    field = exch_coef[None] * laplace - jnp.stack([grad_x, grad_y, grad_z])
    return (field, potential)


def solution(mesh):
    return jax.shard_map(
        body,
        mesh=mesh,
        in_specs=(
            P(None, "gx", "gy", None),
            P("gx", "gy", None),
            P(),
            P(),
            P("gx", "gy", None),
            P("gx", "gy", None),
            P("gx", "gy", None, None, None),
        ),
        out_specs=(P(None, "gx", "gy", None), P("gx", "gy", None)),
        check_vma=False,
    )
```

time: 334 us -> 91.3 us (0.27)
  the two profiles are of different devices: /device:TPU:125 before, /device:TPU:130 now
where the time goes in v1:
time: 91.3 us; the launch traced here: 90.8 us
  waiting for transfers between devices  28.4 us (31%)
  starting transfers between devices  22.8 us (25%)
  other arithmetic  15.9 us (17%)
  blocking collectives  15.1 us (17%)
  local copies, waits for them, and re-layouts  7.11 us (8%)
  between operations  1.19 us (1%)
    all_gather x1, blocking collectives, body(): piece = lax.all_gather(low_panels, 'gy', axis=0, tiled=True)  15.1 us
    ppermute x2, waiting for transfers between devices, swap(): from_prev = [lax.ppermute(to_next[0], axis, _pairs(count, 1))]  13.9 us
    ppermute x2, waiting for transfers between devices, swap(): from_prev = lax.ppermute(_pack(to_next), axis, _pairs(count, 1))  10.8 us
    ppermute x2, starting transfers between devices, swap(): from_next = [lax.ppermute(to_prev[0], axis, _pairs(count, -1))]  8.81 us
    ppermute x2, starting transfers between devices, swap(): from_next = lax.ppermute(_pack(to_prev), axis, _pairs(count, -1))  5.84 us
    ppermute x2, starting transfers between devices, swap(): from_prev = lax.ppermute(_pack(to_next), axis, _pairs(count, 1))  4.32 us
    ppermute x2, starting transfers between devices, swap(): from_prev = [lax.ppermute(to_next[0], axis, _pairs(count, 1))]  3.84 us
    ppermute x2, waiting for transfers between devices, swap(): from_next = [lax.ppermute(to_prev[0], axis, _pairs(count, -1))]  3.79 us
  transfers between devices with their start and end apart: 8, of which 6 were waited for; matrix products, arithmetic and copies ran while one was open for 3% of the time, Pallas kernels for 0%

profile of v1, /device:TPU:130, one launch (start us, length us, event | category | flops | bytes accessed | tf_op | source)
XLA Modules:
  0.0 90.8 jit_solution(7165096264012109839)
XLA Ops:
  0.6 1.5 %fusion.94 = (f32[1]{0:T(128)}, f32[1]{0:T(128)}, f32[1]{0:T(128)}, f32[1]{0:T(128)}) fusion(f32[4]{0:T(128)} %param.9), kind=kLoop, calls=%fused_computation.240 | loop fusion | bytes 32 | tf_op jit(solution)/shard_map/slice | solution.py:76
  2.1 1.5 %fusion.93 = (f32[1]{0:T(128)}, f32[1]{0:T(128)}, f32[1]{0:T(128)}, f32[1]{0:T(128)}) fusion(f32[4]{0:T(128)} %param.10), kind=kLoop, calls=%fused_computation.239 | loop fusion | bytes 32 | tf_op jit(solution)/shard_map/slice | solution.py:76
  3.6 3.4 %select_add_fusion = (f32[8,16,128]{2,1,0:T(8,128)S(1)}, pred[8,16,128]{2,1,0:T(8,128)(4,1)S(1)}, pred[8,16,128]{2,1,0:T(8,128)(4,1)S(1)}, pred[8,16,128]{2,1,0:T(8,128)(4,1)S(1)}, pred[8,16,128]{2,1,0:T(8,128)(4,1)S(1)}) fusion(f32[]{:T(128)} %bitcast.3, f32[]{:T(128)} %bitcast.2, f32[]{:T(128)} %bitcast.1, f32[]{:T(128)} %bitcast, s32[8,16,128]{2,1,0:T(8,128)} %param.8), kind=kLoop, calls=%fused_computation.182 | loop fusion | flops 180224 | bytes 196624 | tf_op jit(solution)/shard_map/add | solution.py:76
  7.0 2.6 %add_bitcast_fusion = f32[1,8,16,128]{3,2,1,0:T(8,128)S(1)} fusion(pred[8,16,128]{2,1,0:T(8,128)(4,1)S(1)} %get-tuple-element.8, pred[8,16,128]{2,1,0:T(8,128)(4,1)S(1)} %get-tuple-element.7, pred[8,16,128]{2,1,0:T(8,128)(4,1)S(1)} %get-tuple-element.6, pred[8,16,128]{2,1,0:T(8,128)(4,1)S(1)} %get-tuple-element.5, f32[]{:T(128)} %bitcast.7, f32[]{:T(128)} %bitcast.6, ...), kind=kLoop, calls=%fused_computation.181 | loop fusion | flops 114688 | bytes 131088 | tf_op jit(solution)/shard_map/broadcast_in_dim | solution.py:100
  9.6 0.9 %pad_maximum_fusion.2 = f32[4,8,16,128]{3,2,1,0:T(8,128)S(1)} fusion(f32[1,8,16,128]{3,2,1,0:T(8,128)S(1)} %add_bitcast_fusion, f32[3,8,16,128]{3,2,1,0:T(8,128)} %param.7), kind=kLoop, calls=%fused_computation.90 | loop fusion | flops 65536 | bytes 524288 | tf_op jit(solution)/shard_map/concatenate | solution.py:100
  10.6 3.0 %collective-permute-start = (f32[4,8,16,128]{3,2,1,0:T(8,128)S(1)}, f32[4,8,16,128]{3,2,1,0:T(8,128)S(1)}, u32[]{:S(2)}, u32[]{:S(2)}) collective-permute-start(f32[4,8,16,128]{3,2,1,0:T(8,128)S(1)} %pad_maximum_fusion.2), channel_id=1, source_target_pairs={{8,0},{16,8},{24,16},{32,24},{40,32},{48,40},{56,48},{64,56},{72,6... | collective-permute-start | bytes 786440 | tf_op jit(solution)/shard_map/ppermute | solution.py:37
  13.6 1.9 %collective-permute-start.1 = (f32[4,8,16,128]{3,2,1,0:T(8,128)S(1)}, f32[4,8,16,128]{3,2,1,0:T(8,128)S(1)}, u32[]{:S(2)}, u32[]{:S(2)}) collective-permute-start(f32[4,8,16,128]{3,2,1,0:T(8,128)S(1)} %pad_maximum_fusion.2), channel_id=1, source_target_pairs={{0,8},{8,16},{16,24},{24,32},{32,40},{40,48},{48,56},{56,64},{64,7... | collective-permute-start | bytes 786440 | tf_op jit(solution)/shard_map/ppermute | solution.py:36
  15.7 0.7 compare_select_fusion
  17.0 0.5 collective-permute-done
  17.4 7.4 %collective-permute-done.1 = f32[4,8,16,128]{3,2,1,0:T(8,128)S(1)} collective-permute-done((f32[4,8,16,128]{3,2,1,0:T(8,128)S(1)}, f32[4,8,16,128]{3,2,1,0:T(8,128)S(1)}, u32[]{:S(2)}, u32[]{:S(2)}) %collective-permute-start.1) | collective-permute-done | bytes 262176 | tf_op jit(solution)/shard_map/ppermute | solution.py:36
  24.9 1.0 %pad_maximum_fusion.1 = f32[4,24,16,128]{3,2,1,0:T(8,128)S(1)} fusion(f32[4,8,16,128]{3,2,1,0:T(8,128)S(1)} %collective-permute-done, f32[1,8,16,128]{3,2,1,0:T(8,128)S(1)} %add_bitcast_fusion, f32[3,8,16,128]{3,2,1,0:T(8,128)} %param.7, f32[4,8,16,128]{3,2,1,0:T(8,128)S(1)} %collective-permute-done.1), kind=kLoop, calls=%fused_computation.14 | loop fusion | flops 589824 | bytes 1572864 | tf_op jit(solution)/shard_map/concatenate | solution.py:51
  25.9 5.8 %collective-permute-start.2 = (f32[4,24,8,128]{3,2,1,0:T(8,128)S(1)}, f32[4,24,8,128]{3,2,1,0:T(8,128)S(1)}, u32[]{:S(2)}, u32[]{:S(2)}) collective-permute-start(f32[4,24,8,128]{3,2,1,0:T(8,128)S(1)} %get-tuple-element.18), channel_id=1, source_target_pairs={{1,0},{2,1},{3,2},{4,3},{5,4},{6,5},{7,6},{9,8},{10,9},{11,10},{12... | collective-permute-start | bytes 1179656 | tf_op jit(solution)/shard_map/ppermute | solution.py:37
  31.7 1.9 %collective-permute-start.3 = (f32[4,24,8,128]{3,2,1,0:T(8,128)S(1)}, f32[4,24,8,128]{3,2,1,0:T(8,128)S(1)}, u32[]{:S(2)}, u32[]{:S(2)}) collective-permute-start(f32[4,24,8,128]{3,2,1,0:T(8,128)S(1)} %get-tuple-element.17), channel_id=1, source_target_pairs={{0,1},{1,2},{2,3},{3,4},{4,5},{5,6},{6,7},{8,9},{9,10},{10,11},{11... | collective-permute-start | bytes 1179656 | tf_op jit(solution)/shard_map/ppermute | solution.py:36
  33.8 3.3 %collective-permute-done.2 = f32[4,24,8,128]{3,2,1,0:T(8,128)S(1)} collective-permute-done((f32[4,24,8,128]{3,2,1,0:T(8,128)S(1)}, f32[4,24,8,128]{3,2,1,0:T(8,128)S(1)}, u32[]{:S(2)}, u32[]{:S(2)}) %collective-permute-start.2) | collective-permute-done | bytes 393248 | tf_op jit(solution)/shard_map/ppermute | solution.py:37
  37.1 6.4 %collective-permute-done.3 = f32[4,24,8,128]{3,2,1,0:T(8,128)S(1)} collective-permute-done((f32[4,24,8,128]{3,2,1,0:T(8,128)S(1)}, f32[4,24,8,128]{3,2,1,0:T(8,128)S(1)}, u32[]{:S(2)}, u32[]{:S(2)}) %collective-permute-start.3) | collective-permute-done | bytes 393248 | tf_op jit(solution)/shard_map/ppermute | solution.py:36
  43.7 0.6 copy-done.2
  44.5 0.4 multiply_select_fusion
  47.0 15.1 %all-gather = bf16[8,2,128]{2,1,0:T(2,128)(2,1)S(1)} all-gather(bf16[1,2,128]{2,1,0:T(2,128)(2,1)S(1)} %convert_bitcast_fusion), channel_id=1, replica_groups=mesh['gx'=32,'gy'=8] {'gy'}, dimensions={0}, use_global_device_ids=true | all-gather | bytes 4608 | tf_op jit(solution)/shard_map/all_gather | solution.py:137
  62.1 0.6 gather_fusion
  63.4 1.9 %collective-permute-start.5 = (f32[2208]{0:T(1024)S(1)}, f32[2208]{0:T(1024)S(1)}, u32[]{:S(2)}, u32[]{:S(2)}) collective-permute-start(f32[2208]{0:T(1024)S(1)} %pad_maximum_fusion.18), channel_id=1, source_target_pairs={{8,0},{16,8},{24,16},{32,24},{40,32},{48,40},{56,48},{64,56},{72,6... | collective-permute-start | bytes 26504 | tf_op jit(solution)/shard_map/ppermute | solution.py:40
  65.5 2.4 %collective-permute-start.4 = (f32[2208]{0:T(1024)S(1)}, f32[2208]{0:T(1024)S(1)}, u32[]{:S(2)}, u32[]{:S(2)}) collective-permute-start(f32[2208]{0:T(1024)S(1)} %pad_maximum_fusion.17), channel_id=1, source_target_pairs={{0,8},{8,16},{16,24},{24,32},{32,40},{40,48},{48,56},{56,64},{64,7... | collective-permute-start | bytes 26504 | tf_op jit(solution)/shard_map/ppermute | solution.py:39
  67.9 0.8 slice.580
  68.7 5.3 %collective-permute-done.4 = f32[2208]{0:T(1024)S(1)} collective-permute-done((f32[2208]{0:T(1024)S(1)}, f32[2208]{0:T(1024)S(1)}, u32[]{:S(2)}, u32[]{:S(2)}) %collective-permute-start.4) | collective-permute-done | bytes 8864 | tf_op jit(solution)/shard_map/ppermute | solution.py:39
  74.4 3.9 %collective-permute-start.7 = (f32[1204]{0:T(1024)S(1)}, f32[1204]{0:T(1024)S(1)}, u32[]{:S(2)}, u32[]{:S(2)}) collective-permute-start(f32[1204]{0:T(1024)S(1)} %pad_maximum_fusion.20), channel_id=1, source_target_pairs={{1,0},{2,1},{3,2},{4,3},{5,4},{6,5},{7,6},{9,8},{10,9},{11,10},{12... | collective-permute-start | bytes 14456 | tf_op jit(solution)/shard_map/ppermute | solution.py:40
  78.6 1.9 %collective-permute-start.6 = (f32[1204]{0:T(1024)S(1)}, f32[1204]{0:T(1024)S(1)}, u32[]{:S(2)}, u32[]{:S(2)}) collective-permute-start(f32[1204]{0:T(1024)S(1)} %pad_maximum_fusion.19), channel_id=1, source_target_pairs={{0,1},{1,2},{2,3},{3,4},{4,5},{5,6},{6,7},{8,9},{9,10},{10,11},{11... | collective-permute-start | bytes 14456 | tf_op jit(solution)/shard_map/ppermute | solution.py:39
  80.7 5.5 %collective-permute-done.6 = f32[1204]{0:T(1024)S(1)} collective-permute-done((f32[1204]{0:T(1024)S(1)}, f32[1204]{0:T(1024)S(1)}, u32[]{:S(2)}, u32[]{:S(2)}) %collective-permute-start.6) | collective-permute-done | bytes 4848 | tf_op jit(solution)/shard_map/ppermute | solution.py:39
  86.8 0.4 select_select_fusion
  87.2 0.5 fusion.7
  87.8 0.5 fusion.17
  88.2 0.4 fusion.33
  89.2 0.7 fusion.85
  89.9 0.9 fusion.49
  (106 shorter events, 6.1 us)
Async XLA Ops:
  0.6 62.1 %copy-start = (bf16[1,2,8,128,128]{4,3,2,1,0:T(8,128)(2,1)S(1)}, bf16[1,2,8,128,128]{4,3,2,1,0:T(8,128)(2,1)}, u32[]{:S(2)}) copy-start(bf16[1,2,8,128,128]{4,3,2,1,0:T(8,128)(2,1)} %param.13) | copy-start | bytes 1572868
  10.6 6.9 %collective-permute-start = (f32[4,8,16,128]{3,2,1,0:T(8,128)S(1)}, f32[4,8,16,128]{3,2,1,0:T(8,128)S(1)}, u32[]{:S(2)}, u32[]{:S(2)}) collective-permute-start(f32[4,8,16,128]{3,2,1,0:T(8,128)S(1)} %pad_maximum_fusion.2), channel_id=1, source_target_pairs={{8,0},{16,8},{24,16},{32,24},{40,32},{48,40},{56,48},{64,56},{72,6... | collective-permute-start | bytes 786440 | tf_op jit(solution)/shard_map/ppermute | solution.py:37
  13.6 11.3 %collective-permute-start.1 = (f32[4,8,16,128]{3,2,1,0:T(8,128)S(1)}, f32[4,8,16,128]{3,2,1,0:T(8,128)S(1)}, u32[]{:S(2)}, u32[]{:S(2)}) collective-permute-start(f32[4,8,16,128]{3,2,1,0:T(8,128)S(1)} %pad_maximum_fusion.2), channel_id=1, source_target_pairs={{0,8},{8,16},{16,24},{24,32},{32,40},{40,48},{48,56},{56,64},{64,7... | collective-permute-start | bytes 786440 | tf_op jit(solution)/shard_map/ppermute | solution.py:36
  17.0 16.7 %copy-start.6 = (s32[1,2,8]{2,1,0:T(2,128)S(1)}, s32[1,2,8]{2,1,0:T(2,128)}, u32[]{:S(2)}) copy-start(s32[1,2,8]{2,1,0:T(2,128)} %param.12) | copy-start | bytes 196
  17.0 26.5 %copy-start.1 = (f32[3,8,16,128]{3,2,1,0:T(8,128)S(1)}, f32[3,8,16,128]{3,2,1,0:T(8,128)}, u32[]{:S(2)}) copy-start(f32[3,8,16,128]{3,2,1,0:T(8,128)} %param.7) | copy-start | bytes 589828
  25.9 11.2 %collective-permute-start.2 = (f32[4,24,8,128]{3,2,1,0:T(8,128)S(1)}, f32[4,24,8,128]{3,2,1,0:T(8,128)S(1)}, u32[]{:S(2)}, u32[]{:S(2)}) collective-permute-start(f32[4,24,8,128]{3,2,1,0:T(8,128)S(1)} %get-tuple-element.18), channel_id=1, source_target_pairs={{1,0},{2,1},{3,2},{4,3},{5,4},{6,5},{7,6},{9,8},{10,9},{11,10},{12... | collective-permute-start | bytes 1179656 | tf_op jit(solution)/shard_map/ppermute | solution.py:37
  31.7 11.8 %collective-permute-start.3 = (f32[4,24,8,128]{3,2,1,0:T(8,128)S(1)}, f32[4,24,8,128]{3,2,1,0:T(8,128)S(1)}, u32[]{:S(2)}, u32[]{:S(2)}) collective-permute-start(f32[4,24,8,128]{3,2,1,0:T(8,128)S(1)} %get-tuple-element.17), channel_id=1, source_target_pairs={{0,1},{1,2},{2,3},{3,4},{4,5},{5,6},{6,7},{8,9},{9,10},{10,11},{11... | collective-permute-start | bytes 1179656 | tf_op jit(solution)/shard_map/ppermute | solution.py:36
  43.5 0.8 copy-start.2
  45.9 0.9 copy-start.5
  46.1 40.2 %copy-start.7 = (pred[2]{0:T(512)(128)(4,1)S(1)}, pred[2]{0:T(512)(128)(4,1)}, u32[]{:S(2)}) copy-start(pred[2]{0:T(512)(128)(4,1)} %constant.64.clone.1) | copy-start | bytes 10
  63.4 5.3 %collective-permute-start.5 = (f32[2208]{0:T(1024)S(1)}, f32[2208]{0:T(1024)S(1)}, u32[]{:S(2)}, u32[]{:S(2)}) collective-permute-start(f32[2208]{0:T(1024)S(1)} %pad_maximum_fusion.18), channel_id=1, source_target_pairs={{8,0},{16,8},{24,16},{32,24},{40,32},{48,40},{56,48},{64,56},{72,6... | collective-permute-start | bytes 26504 | tf_op jit(solution)/shard_map/ppermute | solution.py:40
  65.5 8.6 %collective-permute-start.4 = (f32[2208]{0:T(1024)S(1)}, f32[2208]{0:T(1024)S(1)}, u32[]{:S(2)}, u32[]{:S(2)}) collective-permute-start(f32[2208]{0:T(1024)S(1)} %pad_maximum_fusion.17), channel_id=1, source_target_pairs={{0,8},{8,16},{16,24},{24,32},{32,40},{40,48},{48,56},{56,64},{64,7... | collective-permute-start | bytes 26504 | tf_op jit(solution)/shard_map/ppermute | solution.py:39
  74.4 6.2 %collective-permute-start.7 = (f32[1204]{0:T(1024)S(1)}, f32[1204]{0:T(1024)S(1)}, u32[]{:S(2)}, u32[]{:S(2)}) collective-permute-start(f32[1204]{0:T(1024)S(1)} %pad_maximum_fusion.20), channel_id=1, source_target_pairs={{1,0},{2,1},{3,2},{4,3},{5,4},{6,5},{7,6},{9,8},{10,9},{11,10},{12... | collective-permute-start | bytes 14456 | tf_op jit(solution)/shard_map/ppermute | solution.py:40
  78.6 7.7 %collective-permute-start.6 = (f32[1204]{0:T(1024)S(1)}, f32[1204]{0:T(1024)S(1)}, u32[]{:S(2)}, u32[]{:S(2)}) collective-permute-start(f32[1204]{0:T(1024)S(1)} %pad_maximum_fusion.19), channel_id=1, source_target_pairs={{0,1},{1,2},{2,3},{3,4},{4,5},{5,6},{6,7},{8,9},{9,10},{10,11},{11... | collective-permute-start | bytes 14456 | tf_op jit(solution)/shard_map/ppermute | solution.py:39
  88.7 1.2 %copy-start.3 = (f32[4,24,8,128]{3,2,1,0:T(8,128)S(1)}, f32[4,24,8,128]{3,2,1,0:T(8,128)}, u32[]{:S(2)}) copy-start(f32[4,24,8,128]{3,2,1,0:T(8,128)} %copy-done.2) | copy-start | bytes 1179652
  88.7 1.2 %copy-start.4 = (f32[3,10,18,128]{3,2,1,0:T(8,128)S(1)}, f32[3,10,18,128]{3,2,1,0:T(8,128)}, u32[]{:S(2)}) copy-start(f32[3,10,18,128]{3,2,1,0:T(8,128)} %slice.580) | copy-start | bytes 829444

commit v2 on v1

--- a/solution.py
+++ b/solution.py
@@ -93,13 +93,11 @@
         ok_y = (ys >= 0) & (ys < grid_y)
         return (ok_x[:, None] & ok_y[None, :])[:, :, None]
 
+    halo = SWEEPS
+    data = jnp.concatenate([magnet, grain_ids.astype(jnp.float32)[None]], axis=0)
+    wide = widen(data, halo, halo, 1, 2)
+    m0, m1, m2 = wide[0], wide[1], wide[2]
     exch_coef = lookup(grain_ids, exch_table)
-    sat_coef = lookup(grain_ids, sat_table)
-
-    halo = SWEEPS
-    data = jnp.concatenate([magnet, sat_coef[None]], axis=0)
-    wide = widen(data, halo, halo, 1, 2)
-    m0, m1, m2, sat_w = wide[0], wide[1], wide[2], wide[3]
 
     hs = halo - 1
     ex = slice(1, 1 + cells_x + 2 * hs)
@@ -113,7 +111,8 @@
         + m2p[:, :, 2:]
         - m2p[:, :, :-2]
     ) * 0.5
-    source = -sat_w[ex, ey] * diverge
+    sat_w = lookup(wide[3, ex, ey].astype(jnp.int32), sat_table)
+    source = -sat_w * diverge
 
     scalar = jnp.where(inside(hs), source / DIAG, 0.0)
     for sweep in range(1, SWEEPS):
@@ -134,7 +133,9 @@
     low_panels = panels.astype(jnp.bfloat16)
     local_list = near_list[0]
     blank_pick = jnp.zeros((local_list.shape[0], local_list.shape[1], NODES), jnp.bfloat16)
-    piece = lax.all_gather(low_panels, "gy", axis=0, tiled=True)
+    group = lax.axis_size("gy")
+    copies = jnp.broadcast_to(low_panels[None], (group,) + low_panels.shape)
+    piece = lax.all_to_all(copies, "gy", 0, 0, tiled=True).reshape(group * 2, NODES)
     valid = (local_list >= 0) & (local_list < piece.shape[0])
     picked = piece[jnp.clip(local_list, 0, piece.shape[0] - 1)]
     chosen = jnp.where(valid[:, :, None], picked, blank_pick)

time: 91.3 us -> 80.8 us (0.88)
  the two profiles are of different devices: /device:TPU:130 before, /device:TPU:125 now
where the time goes in v2:
time: 80.8 us; the launch traced here: 80.3 us
  starting transfers between devices  38.9 us (48%)
  other arithmetic  16.6 us (21%)
  waiting for transfers between devices  16.5 us (20%)
  local copies, waits for them, and re-layouts  6.81 us (8%)
  between operations  1.17 us (1%)
    ppermute x2, starting transfers between devices, swap(): from_prev = lax.ppermute(_pack(to_next), axis, _pairs(count, 1))  12.7 us
    ppermute x2, starting transfers between devices, swap(): from_prev = [lax.ppermute(to_next[0], axis, _pairs(count, 1))]  11.6 us
    ppermute x2, waiting for transfers between devices, swap(): from_next = lax.ppermute(_pack(to_prev), axis, _pairs(count, -1))  10.1 us
    all_to_all x1, starting transfers between devices, body(): lax.all_to_all(copies, 'gy', 0, 0, tiled=True).reshape(group * 2, NODES)  5.87 us
    ppermute x2, starting transfers between devices, swap(): from_next = [lax.ppermute(to_prev[0], axis, _pairs(count, -1))]  4.96 us
    ppermute x2, starting transfers between devices, swap(): from_next = lax.ppermute(_pack(to_prev), axis, _pairs(count, -1))  3.83 us
    all_to_all x1, waiting for transfers between devices, body(): lax.all_to_all(copies, 'gy', 0, 0, tiled=True).reshape(group * 2, NODES)  3.17 us
    select_n x1, other arithmetic, body(): scalar = jnp.where(inside(hs), source / DIAG, 0.0)  2.92 us
  transfers between devices with their start and end apart: 9, of which 5 were waited for; matrix products, arithmetic and copies ran while one was open for 10% of the time, Pallas kernels for 0%

profile of v2, /device:TPU:125, one launch (start us, length us, event | category | flops | bytes accessed | tf_op | source)
XLA Modules:
  0.0 80.3 jit_solution(10033657809209759453)
XLA Ops:
  0.6 0.9 %convert_bitcast_fusion = f32[1,8,16,128]{3,2,1,0:T(8,128)S(1)} fusion(s32[8,16,128]{2,1,0:T(8,128)} %param.8), kind=kLoop, calls=%fused_computation.180 | loop fusion | flops 16384 | bytes 131072 | tf_op jit(solution)/shard_map/broadcast_in_dim | solution.py:97
  1.5 0.9 %pad_maximum_fusion.2 = f32[4,8,16,128]{3,2,1,0:T(8,128)S(1)} fusion(f32[1,8,16,128]{3,2,1,0:T(8,128)S(1)} %convert_bitcast_fusion, f32[3,8,16,128]{3,2,1,0:T(8,128)} %param.7), kind=kLoop, calls=%fused_computation.89 | loop fusion | flops 65536 | bytes 524288 | tf_op jit(solution)/shard_map/concatenate | solution.py:97
  2.5 2.6 %collective-permute-start = (f32[4,8,16,128]{3,2,1,0:T(8,128)S(1)}, f32[4,8,16,128]{3,2,1,0:T(8,128)S(1)}, u32[]{:S(2)}, u32[]{:S(2)}) collective-permute-start(f32[4,8,16,128]{3,2,1,0:T(8,128)S(1)} %pad_maximum_fusion.2), channel_id=1, source_target_pairs={{8,0},{16,8},{24,16},{32,24},{40,32},{48,40},{56,48},{64,56},{72,6... | collective-permute-start | bytes 786440 | tf_op jit(solution)/shard_map/ppermute | solution.py:37
  5.1 6.6 %collective-permute-start.1 = (f32[4,8,16,128]{3,2,1,0:T(8,128)S(1)}, f32[4,8,16,128]{3,2,1,0:T(8,128)S(1)}, u32[]{:S(2)}, u32[]{:S(2)}) collective-permute-start(f32[4,8,16,128]{3,2,1,0:T(8,128)S(1)} %pad_maximum_fusion.2), channel_id=1, source_target_pairs={{0,8},{8,16},{16,24},{24,32},{32,40},{40,48},{48,56},{56,64},{64,7... | collective-permute-start | bytes 786440 | tf_op jit(solution)/shard_map/ppermute | solution.py:36
  11.7 0.7 compare_select_fusion
  12.4 0.7 and_bitcast_fusion
  13.1 1.4 %fusion.94 = (f32[1]{0:T(128)}, f32[1]{0:T(128)}, f32[1]{0:T(128)}, f32[1]{0:T(128)}) fusion(f32[4]{0:T(128)} %param.10), kind=kLoop, calls=%fused_computation.234 | loop fusion | bytes 32 | tf_op jit(solution)/shard_map/slice | solution.py:76
  15.3 1.0 %pad_maximum_fusion.1 = f32[4,24,16,128]{3,2,1,0:T(8,128)S(1)} fusion(f32[4,8,16,128]{3,2,1,0:T(8,128)S(1)} %collective-permute-done, f32[1,8,16,128]{3,2,1,0:T(8,128)S(1)} %convert_bitcast_fusion, f32[3,8,16,128]{3,2,1,0:T(8,128)} %param.7, f32[4,8,16,128]{3,2,1,0:T(8,128)S(1)} %collective-permute-done.1), kind=kLoop, calls=%fused_computation.14 | loop fusion | flops 589824 | bytes 1572864 | tf_op jit(solution)/shard_map/concatenate | solution.py:51
  16.5 2.4 %collective-permute-start.2 = (f32[4,24,8,128]{3,2,1,0:T(8,128)S(1)}, f32[4,24,8,128]{3,2,1,0:T(8,128)S(1)}, u32[]{:S(2)}, u32[]{:S(2)}) collective-permute-start(f32[4,24,8,128]{3,2,1,0:T(8,128)S(1)} %get-tuple-element.12), channel_id=1, source_target_pairs={{1,0},{2,1},{3,2},{4,3},{5,4},{6,5},{7,6},{9,8},{10,9},{11,10},{12... | collective-permute-start | bytes 1179656 | tf_op jit(solution)/shard_map/ppermute | solution.py:37
  18.8 5.0 %collective-permute-start.3 = (f32[4,24,8,128]{3,2,1,0:T(8,128)S(1)}, f32[4,24,8,128]{3,2,1,0:T(8,128)S(1)}, u32[]{:S(2)}, u32[]{:S(2)}) collective-permute-start(f32[4,24,8,128]{3,2,1,0:T(8,128)S(1)} %get-tuple-element.11), channel_id=1, source_target_pairs={{0,1},{1,2},{2,3},{3,4},{4,5},{5,6},{6,7},{8,9},{9,10},{10,11},{11... | collective-permute-start | bytes 1179656 | tf_op jit(solution)/shard_map/ppermute | solution.py:36
  23.9 0.7 fusion.93
  24.6 2.6 %select_add_fusion = f32[8,16,128]{2,1,0:T(8,128)S(1)} fusion(s32[8,16,128]{2,1,0:T(8,128)S(1)} %copy-done.5, f32[]{:T(128)} %bitcast.3, f32[]{:T(128)} %bitcast.2, f32[]{:T(128)} %bitcast.1, f32[]{:T(128)} %bitcast), kind=kLoop, calls=%fused_computation.181 | loop fusion | flops 180224 | bytes 131088 | tf_op jit(solution)/shard_map/add | solution.py:76
  27.1 2.3 %collective-permute-done.2 = f32[4,24,8,128]{3,2,1,0:T(8,128)S(1)} collective-permute-done((f32[4,24,8,128]{3,2,1,0:T(8,128)S(1)}, f32[4,24,8,128]{3,2,1,0:T(8,128)S(1)}, u32[]{:S(2)}, u32[]{:S(2)}) %collective-permute-start.2) | collective-permute-done | bytes 393248 | tf_op jit(solution)/shard_map/ppermute | solution.py:37
  29.4 0.9 %collective-permute-done.3 = f32[4,24,8,128]{3,2,1,0:T(8,128)S(1)} collective-permute-done((f32[4,24,8,128]{3,2,1,0:T(8,128)S(1)}, f32[4,24,8,128]{3,2,1,0:T(8,128)S(1)}, u32[]{:S(2)}, u32[]{:S(2)}) %collective-permute-start.3) | collective-permute-done | bytes 393248 | tf_op jit(solution)/shard_map/ppermute | solution.py:36
  30.5 0.6 copy-done.2
  31.2 2.9 %multiply_select_fusion = (f32[22,30,128]{2,1,0:T(8,128)S(1)}, f32[22,30,128]{2,1,0:T(8,128)S(1)}) fusion(pred[22,30]{1,0:T(8,128)(4,1)S(1)} %broadcast_and_fusion, f32[22,30,128]{2,1,0:T(8,128)S(1)} %slice.585, f32[24,32,128]{2,1,0:T(8,128)S(1)} %get-tuple-element.10, f32[24,32,128]{2,1,0:T(8,128)S(1)} %get-tuple-element.8, f32[]{:T(128)} %bitcast.10, ...), kind=kLoop, calls=%fused_computation.48 | loop fusion | flops 1858560 | bytes 2704036 | tf_op jit(solution)/shard_map/jit(_where)/select_n | solution.py:117
  36.3 0.6 broadcast_in_dim.343
  36.9 5.9 %all-to-all-start = ((bf16[8,2,128]{2,1,0:T(2,128)(2,1)}), bf16[8,2,128]{2,1,0:T(2,128)(2,1)S(1)}, u32[]{:S(2)}, u32[]{:S(2)}) async-start(bf16[8,2,128]{2,1,0:T(2,128)(2,1)} %broadcast_in_dim.343), calls=%async_computation | async-start | bytes 8192 | tf_op jit(solution)/shard_map/all_to_all | solution.py:138
  42.8 3.2 %all-to-all-done = bf16[8,2,128]{2,1,0:T(2,128)(2,1)S(1)} async-done(((bf16[8,2,128]{2,1,0:T(2,128)(2,1)}), bf16[8,2,128]{2,1,0:T(2,128)(2,1)S(1)}, u32[]{:S(2)}, u32[]{:S(2)}) %all-to-all-start) | async-done | bytes 4128 | tf_op jit(solution)/shard_map/all_to_all | solution.py:138
  45.9 0.6 gather_fusion
  47.2 8.4 %collective-permute-start.4 = (f32[2208]{0:T(1024)S(1)}, f32[2208]{0:T(1024)S(1)}, u32[]{:S(2)}, u32[]{:S(2)}) collective-permute-start(f32[2208]{0:T(1024)S(1)} %pad_maximum_fusion.17), channel_id=1, source_target_pairs={{0,8},{8,16},{16,24},{24,32},{32,40},{40,48},{48,56},{56,64},{64,7... | collective-permute-start | bytes 26504 | tf_op jit(solution)/shard_map/ppermute | solution.py:39
  55.8 1.9 %collective-permute-start.5 = (f32[2208]{0:T(1024)S(1)}, f32[2208]{0:T(1024)S(1)}, u32[]{:S(2)}, u32[]{:S(2)}) collective-permute-start(f32[2208]{0:T(1024)S(1)} %pad_maximum_fusion.18), channel_id=1, source_target_pairs={{8,0},{16,8},{24,16},{32,24},{40,32},{48,40},{56,48},{64,56},{72,6... | collective-permute-start | bytes 26504 | tf_op jit(solution)/shard_map/ppermute | solution.py:40
  57.7 0.8 slice.576
  58.6 5.8 %collective-permute-done.5 = f32[2208]{0:T(1024)S(1)} collective-permute-done((f32[2208]{0:T(1024)S(1)}, f32[2208]{0:T(1024)S(1)}, u32[]{:S(2)}, u32[]{:S(2)}) %collective-permute-start.5) | collective-permute-done | bytes 8864 | tf_op jit(solution)/shard_map/ppermute | solution.py:40
  64.8 4.3 %collective-permute-start.6 = (f32[1204]{0:T(1024)S(1)}, f32[1204]{0:T(1024)S(1)}, u32[]{:S(2)}, u32[]{:S(2)}) collective-permute-start(f32[1204]{0:T(1024)S(1)} %pad_maximum_fusion.19), channel_id=1, source_target_pairs={{0,1},{1,2},{2,3},{3,4},{4,5},{5,6},{6,7},{8,9},{9,10},{10,11},{11... | collective-permute-start | bytes 14456 | tf_op jit(solution)/shard_map/ppermute | solution.py:39
  69.2 1.9 %collective-permute-start.7 = (f32[1204]{0:T(1024)S(1)}, f32[1204]{0:T(1024)S(1)}, u32[]{:S(2)}, u32[]{:S(2)}) collective-permute-start(f32[1204]{0:T(1024)S(1)} %pad_maximum_fusion.20), channel_id=1, source_target_pairs={{1,0},{2,1},{3,2},{4,3},{5,4},{6,5},{7,6},{9,8},{10,9},{11,10},{12... | collective-permute-start | bytes 14456 | tf_op jit(solution)/shard_map/ppermute | solution.py:40
  71.4 4.3 %collective-permute-done.7 = f32[1204]{0:T(1024)S(1)} collective-permute-done((f32[1204]{0:T(1024)S(1)}, f32[1204]{0:T(1024)S(1)}, u32[]{:S(2)}, u32[]{:S(2)}) %collective-permute-start.7) | collective-permute-done | bytes 4848 | tf_op jit(solution)/shard_map/ppermute | solution.py:40
  76.8 0.5 fusion.7
  77.3 0.5 fusion.17
  77.8 0.4 fusion.33
  78.8 0.7 fusion.85
  79.4 0.9 %fusion.49 = f32[3,8,16,128]{3,2,1,0:T(8,128)} fusion(f32[3,10,18,128]{3,2,1,0:T(8,128)S(1)} %copy-done.4, f32[4,24,8,128]{3,2,1,0:T(8,128)S(1)} %copy-done.3, f32[4,8,16,128]{3,2,1,0:T(8,128)S(1)} %collective-permute-done, f32[4,8,16,128]{3,2,1,0:T(8,128)S(1)} %collective-permute-done.1, f32[1,8,16,128]{3,2,1,0:T(8,128)S(1)} %convert_bitcast_fusion, ...), kind=kLoop, calls=%fused_computation.108 | loop fusion | flops 1130496 | bytes 2308096 | tf_op jit(solution)/shard_map/sub | solution.py:197
  (110 shorter events, 6.4 us)
Async XLA Ops:
  0.6 45.9 %copy-start = (bf16[1,2,8,128,128]{4,3,2,1,0:T(8,128)(2,1)S(1)}, bf16[1,2,8,128,128]{4,3,2,1,0:T(8,128)(2,1)}, u32[]{:S(2)}) copy-start(bf16[1,2,8,128,128]{4,3,2,1,0:T(8,128)(2,1)} %param.13) | copy-start | bytes 1572868
  2.5 12.8 %collective-permute-start = (f32[4,8,16,128]{3,2,1,0:T(8,128)S(1)}, f32[4,8,16,128]{3,2,1,0:T(8,128)S(1)}, u32[]{:S(2)}, u32[]{:S(2)}) collective-permute-start(f32[4,8,16,128]{3,2,1,0:T(8,128)S(1)} %pad_maximum_fusion.2), channel_id=1, source_target_pairs={{8,0},{16,8},{24,16},{32,24},{40,32},{48,40},{56,48},{64,56},{72,6... | collective-permute-start | bytes 786440 | tf_op jit(solution)/shard_map/ppermute | solution.py:37
  5.1 10.2 %collective-permute-start.1 = (f32[4,8,16,128]{3,2,1,0:T(8,128)S(1)}, f32[4,8,16,128]{3,2,1,0:T(8,128)S(1)}, u32[]{:S(2)}, u32[]{:S(2)}) collective-permute-start(f32[4,8,16,128]{3,2,1,0:T(8,128)S(1)} %pad_maximum_fusion.2), channel_id=1, source_target_pairs={{0,8},{8,16},{16,24},{24,32},{32,40},{40,48},{48,56},{56,64},{64,7... | collective-permute-start | bytes 786440 | tf_op jit(solution)/shard_map/ppermute | solution.py:36
  15.3 8.6 %copy-start.6 = (f32[4]{0:T(128)S(1)}, f32[4]{0:T(128)}, u32[]{:S(2)}) copy-start(f32[4]{0:T(128)} %param.9) | copy-start | bytes 52
  15.3 9.2 %copy-start.5 = (s32[8,16,128]{2,1,0:T(8,128)S(1)}, s32[8,16,128]{2,1,0:T(8,128)}, u32[]{:S(2)}) copy-start(s32[8,16,128]{2,1,0:T(8,128)} %param.8) | copy-start | bytes 196612
  15.3 15.0 %copy-start.1 = (f32[3,8,16,128]{3,2,1,0:T(8,128)S(1)}, f32[3,8,16,128]{3,2,1,0:T(8,128)}, u32[]{:S(2)}) copy-start(f32[3,8,16,128]{3,2,1,0:T(8,128)} %param.7) | copy-start | bytes 589828
  16.5 13.0 %collective-permute-start.2 = (f32[4,24,8,128]{3,2,1,0:T(8,128)S(1)}, f32[4,24,8,128]{3,2,1,0:T(8,128)S(1)}, u32[]{:S(2)}, u32[]{:S(2)}) collective-permute-start(f32[4,24,8,128]{3,2,1,0:T(8,128)S(1)} %get-tuple-element.12), channel_id=1, source_target_pairs={{1,0},{2,1},{3,2},{4,3},{5,4},{6,5},{7,6},{9,8},{10,9},{11,10},{12... | collective-permute-start | bytes 1179656 | tf_op jit(solution)/shard_map/ppermute | solution.py:37
  18.8 11.5 %collective-permute-start.3 = (f32[4,24,8,128]{3,2,1,0:T(8,128)S(1)}, f32[4,24,8,128]{3,2,1,0:T(8,128)S(1)}, u32[]{:S(2)}, u32[]{:S(2)}) collective-permute-start(f32[4,24,8,128]{3,2,1,0:T(8,128)S(1)} %get-tuple-element.11), channel_id=1, source_target_pairs={{0,1},{1,2},{2,3},{3,4},{4,5},{5,6},{6,7},{8,9},{9,10},{10,11},{11... | collective-permute-start | bytes 1179656 | tf_op jit(solution)/shard_map/ppermute | solution.py:36
  30.3 0.8 copy-start.2
  35.2 0.8 %copy-start.7 = (s32[2,1,128]{2,1,0:T(1,128)S(1)}, s32[2,1,128]{2,1,0:T(1,128)}, u32[]{:S(2)}) copy-start(s32[2,1,128]{2,1,0:T(1,128)} %param.11) | copy-start | bytes 3076
  35.4 40.4 %copy-start.8 = (pred[2]{0:T(512)(128)(4,1)S(1)}, pred[2]{0:T(512)(128)(4,1)}, u32[]{:S(2)}) copy-start(pred[2]{0:T(512)(128)(4,1)} %constant.64.clone.1) | copy-start | bytes 10
  36.9 9.0 %all-to-all-start = ((bf16[8,2,128]{2,1,0:T(2,128)(2,1)}), bf16[8,2,128]{2,1,0:T(2,128)(2,1)S(1)}, u32[]{:S(2)}, u32[]{:S(2)}) async-start(bf16[8,2,128]{2,1,0:T(2,128)(2,1)} %broadcast_in_dim.343), calls=%async_computation | async-start | bytes 8192 | tf_op jit(solution)/shard_map/all_to_all | solution.py:138
  47.2 11.3 %collective-permute-start.4 = (f32[2208]{0:T(1024)S(1)}, f32[2208]{0:T(1024)S(1)}, u32[]{:S(2)}, u32[]{:S(2)}) collective-permute-start(f32[2208]{0:T(1024)S(1)} %pad_maximum_fusion.17), channel_id=1, source_target_pairs={{0,8},{8,16},{16,24},{24,32},{32,40},{40,48},{48,56},{56,64},{64,7... | collective-permute-start | bytes 26504 | tf_op jit(solution)/shard_map/ppermute | solution.py:39
  55.8 8.6 %collective-permute-start.5 = (f32[2208]{0:T(1024)S(1)}, f32[2208]{0:T(1024)S(1)}, u32[]{:S(2)}, u32[]{:S(2)}) collective-permute-start(f32[2208]{0:T(1024)S(1)} %pad_maximum_fusion.18), channel_id=1, source_target_pairs={{8,0},{16,8},{24,16},{32,24},{40,32},{48,40},{56,48},{64,56},{72,6... | collective-permute-start | bytes 26504 | tf_op jit(solution)/shard_map/ppermute | solution.py:40
  64.8 6.6 %collective-permute-start.6 = (f32[1204]{0:T(1024)S(1)}, f32[1204]{0:T(1024)S(1)}, u32[]{:S(2)}, u32[]{:S(2)}) collective-permute-start(f32[1204]{0:T(1024)S(1)} %pad_maximum_fusion.19), channel_id=1, source_target_pairs={{0,1},{1,2},{2,3},{3,4},{4,5},{5,6},{6,7},{8,9},{9,10},{10,11},{11... | collective-permute-start | bytes 14456 | tf_op jit(solution)/shard_map/ppermute | solution.py:39
  69.2 6.5 %collective-permute-start.7 = (f32[1204]{0:T(1024)S(1)}, f32[1204]{0:T(1024)S(1)}, u32[]{:S(2)}, u32[]{:S(2)}) collective-permute-start(f32[1204]{0:T(1024)S(1)} %pad_maximum_fusion.20), channel_id=1, source_target_pairs={{1,0},{2,1},{3,2},{4,3},{5,4},{6,5},{7,6},{9,8},{10,9},{11,10},{12... | collective-permute-start | bytes 14456 | tf_op jit(solution)/shard_map/ppermute | solution.py:40
  78.2 1.2 %copy-start.3 = (f32[4,24,8,128]{3,2,1,0:T(8,128)S(1)}, f32[4,24,8,128]{3,2,1,0:T(8,128)}, u32[]{:S(2)}) copy-start(f32[4,24,8,128]{3,2,1,0:T(8,128)} %copy-done.2) | copy-start | bytes 1179652
  78.2 1.2 %copy-start.4 = (f32[3,10,18,128]{3,2,1,0:T(8,128)S(1)}, f32[3,10,18,128]{3,2,1,0:T(8,128)}, u32[]{:S(2)}) copy-start(f32[3,10,18,128]{3,2,1,0:T(8,128)} %slice.576) | copy-start | bytes 829444

commit v3 on v2

--- a/solution.py
+++ b/solution.py
@@ -94,8 +94,29 @@
         return (ok_x[:, None] & ok_y[None, :])[:, :, None]
 
     halo = SWEEPS
+    he = EXT_SWEEPS + 1
+    node_map = surface_map[:, 0, :]
+    cell_ids = jnp.arange(cells_x * cells_y, dtype=jnp.int32)
+    onehot = node_map[:, :, None] == cell_ids[None, None, :]
+    rows = jnp.einsum(
+        "tnc,tknj->tkcj",
+        onehot.astype(near_blocks.dtype),
+        near_blocks[0],
+        preferred_element_type=jnp.float32,
+    )
+    rows = rows.reshape(rows.shape[0], rows.shape[1], cells_x, cells_y, NODES)
+    local_list = near_list[0]
+    list_f = local_list.astype(jnp.float32)
+
     data = jnp.concatenate([magnet, grain_ids.astype(jnp.float32)[None]], axis=0)
-    wide = widen(data, halo, halo, 1, 2)
+    (lo,), (hi,) = swap("gx", [data[:, cells_x - halo :]], [data[:, :halo]])
+    wide_x = jnp.concatenate([lo, data, hi], axis=1)
+    (lo, rows_lo, list_lo), (hi, rows_hi, list_hi) = swap(
+        "gy",
+        [wide_x[:, :, cells_y - halo :], rows[:, :, :, cells_y - he :], list_f],
+        [wide_x[:, :, :halo], rows[:, :, :, :he], list_f],
+    )
+    wide = jnp.concatenate([lo, wide_x, hi], axis=2)
     m0, m1, m2 = wide[0], wide[1], wide[2]
     exch_coef = lookup(grain_ids, exch_table)
 
@@ -125,44 +146,61 @@
     mag_1 = wide[0:3, halo - 1 : halo + 1 + cells_x, halo - 1 : halo + 1 + cells_y]
     laplace = near_sum(mag_1) - 6.0 * magnet
 
-    node_map = surface_map[:, 0, :]
-    cell_ids = jnp.arange(cells_x * cells_y, dtype=jnp.int32)
-    onehot = node_map[:, :, None] == cell_ids[None, None, :]
-    face_vals = jnp.stack([scalar[:, :, 0], scalar[:, :, -1]]).reshape(2, cells_x * cells_y)
-    panels = jnp.sum(jnp.where(onehot, face_vals[:, None, :], 0.0), axis=2)
-    low_panels = panels.astype(jnp.bfloat16)
-    local_list = near_list[0]
-    blank_pick = jnp.zeros((local_list.shape[0], local_list.shape[1], NODES), jnp.bfloat16)
+    face = jnp.stack([scalar[:, :, 0], scalar[:, :, -1]])
+    face_flat = face.reshape(2, cells_x * cells_y)
+    panels = jnp.sum(jnp.where(onehot, face_flat[:, None, :], 0.0), axis=2)
+
     group = lax.axis_size("gy")
-    copies = jnp.broadcast_to(low_panels[None], (group,) + low_panels.shape)
-    piece = lax.all_to_all(copies, "gy", 0, 0, tiled=True).reshape(group * 2, NODES)
-    valid = (local_list >= 0) & (local_list < piece.shape[0])
-    picked = piece[jnp.clip(local_list, 0, piece.shape[0] - 1)]
-    chosen = jnp.where(valid[:, :, None], picked, blank_pick)
-    double = (
-        jnp.einsum("tkij,tkj->ti", near_blocks[0], chosen, preferred_element_type=jnp.float32)
-        - 0.5 * panels
-    )
-    cells = jnp.sum(jnp.where(onehot, double[:, :, None], 0.0), axis=1)
-    planes = cells.reshape(2, cells_x, cells_y)
-
-    he = EXT_SWEEPS + 1
+    me = lax.axis_index("gy")
+    side_hi = _pack([face[:, :, cells_y - he :], scalar[:, cells_y - 1]])
+    side_lo = _pack([face[:, :, :he], scalar[:, 0]])
+    rel = jnp.arange(group, dtype=jnp.int32)[:, None] - me
+    side = jnp.where(rel == 1, side_hi[None], jnp.where(rel == -1, side_lo[None], 0.0))
+    chunks = jnp.concatenate(
+        [jnp.broadcast_to(panels.reshape(1, -1), (group, panels.size)), side], axis=1
+    )
+    got = lax.all_to_all(chunks, "gy", 0, 0, tiled=True)
+    piece = got[:, : panels.size].reshape(group * 2, NODES).astype(jnp.bfloat16)
+    from_lo = jnp.where(me > 0, got[jnp.maximum(me - 1, 0), panels.size :], 0.0)
+    from_hi = jnp.where(me < group - 1, got[jnp.minimum(me + 1, group - 1), panels.size :], 0.0)
+    like = [face[:, :, :he], scalar[:, 0]]
+    face_lo, t_lo = _unpack(from_lo, like)
+    face_hi, t_hi = _unpack(from_hi, like)
+
+    def double_of(block_rows, lists, faces):
+        lists = lists.astype(jnp.int32)
+        valid = (lists >= 0) & (lists < piece.shape[0])
+        picked = piece[jnp.clip(lists, 0, piece.shape[0] - 1)]
+        chosen = jnp.where(valid[:, :, None], picked, jnp.zeros_like(picked))
+        product = jnp.einsum(
+            "tkxyj,tkj->txy",
+            block_rows.astype(jnp.bfloat16),
+            chosen,
+            preferred_element_type=jnp.float32,
+        )
+        return product - 0.5 * faces
+
+    planes_y = jnp.concatenate(
+        [
+            double_of(rows_lo, list_lo, face_lo),
+            double_of(rows, local_list, face),
+            double_of(rows_hi, list_hi, face_hi),
+        ],
+        axis=2,
+    )
+
     (p_lo, s_lo), (p_hi, s_hi) = swap(
         "gx",
-        [planes[:, cells_x - he :], scalar[cells_x - 1 :]],
-        [planes[:, :he], scalar[:1]],
-    )
-    planes_x = jnp.concatenate([p_lo, planes, p_hi], axis=1)
-    (q_lo, t_lo), (q_hi, t_hi) = swap(
-        "gy",
-        [planes_x[:, :, cells_y - he :], scalar[:, cells_y - 1 :]],
-        [planes_x[:, :, :he], scalar[:, :1]],
-    )
-    planes_w = jnp.concatenate([q_lo, planes_x, q_hi], axis=2)
+        [planes_y[:, cells_x - he :], scalar[cells_x - 1 :]],
+        [planes_y[:, :he], scalar[:1]],
+    )
+    planes_w = jnp.concatenate([p_lo, planes_y, p_hi], axis=1)
 
     column = jnp.concatenate([s_lo, scalar, s_hi], axis=0)
     row_pad = ((1, 1), (0, 0), (0, 0))
-    scalar_1 = jnp.concatenate([jnp.pad(t_lo, row_pad), column, jnp.pad(t_hi, row_pad)], axis=1)
+    t_lo = jnp.pad(t_lo[:, None], row_pad)
+    t_hi = jnp.pad(t_hi[:, None], row_pad)
+    scalar_1 = jnp.concatenate([t_lo, column, t_hi], axis=1)
 
     z_ids = jnp.arange(cells_z, dtype=jnp.int32)
     bottom = z_ids == 0

time: 80.8 us -> 106 us (1.31)
  the two profiles are of different devices: /device:TPU:125 before, /device:TPU:136 now
where the time goes in v3:
time: 106 us; the launch traced here: 105 us
  other arithmetic  31.5 us (30%)
  starting transfers between devices  28.1 us (27%)
  local copies, waits for them, and re-layouts  24.3 us (23%)
  waiting for transfers between devices  16.6 us (16%)
  matrix products  3.05 us (3%)
  between operations  1.44 us (1%)
    ppermute x2, waiting for transfers between devices, swap(): from_prev = lax.ppermute(_pack(to_next), axis, _pairs(count, 1))  14.7 us
    ppermute x2, starting transfers between devices, swap(): from_next = lax.ppermute(_pack(to_prev), axis, _pairs(count, -1))  7.94 us
    ppermute x1, starting transfers between devices, swap(): from_next = [lax.ppermute(to_prev[0], axis, _pairs(count, -1))]  7.26 us
    all_to_all x1, starting transfers between devices, body(): got = lax.all_to_all(chunks, 'gy', 0, 0, tiled=True)  5.56 us
    ppermute x2, starting transfers between devices, swap(): from_prev = lax.ppermute(_pack(to_next), axis, _pairs(count, 1))  5.39 us
    reshape x7, local copies, waits for them, and re-layouts, _pack(): return jnp.concatenate([a.reshape(-1) for a in arrays])  3.48 us
    add x1, other arithmetic, lookup(): result = result + (grain_ids == index).astype(jnp.float32) * table[index]  3.06 us
    slice x6, local copies, waits for them, and re-layouts, _unpack(): out.append(flat[start:start + a.size].reshape(a.shape))  3.03 us
  transfers between devices with their start and end apart: 7, of which 3 were waited for; matrix products, arithmetic and copies ran while one was open for 19% of the time, Pallas kernels for 0%

profile of v3, /device:TPU:136, one launch (start us, length us, event | category | flops | bytes accessed | tf_op | source)
XLA Modules:
  0.0 104.9 jit_solution(17805243702170936964)
XLA Ops:
  0.6 0.9 convert_bitcast_fusion
  1.6 1.7 %pad_maximum_fusion.4 = f32[4,8,16,128]{3,2,1,0:T(8,128)} fusion(f32[1,8,16,128]{3,2,1,0:T(8,128)S(1)} %convert_bitcast_fusion, f32[3,8,16,128]{3,2,1,0:T(8,128)} %param.7), kind=kLoop, calls=%fused_computation.97 | loop fusion | flops 65536 | bytes 524288 | tf_op jit(solution)/shard_map/concatenate | solution.py:111
  3.2 1.9 %collective-permute-start.1 = (f32[4,8,16,128]{3,2,1,0:T(8,128)}, f32[4,8,16,128]{3,2,1,0:T(8,128)S(1)}, u32[]{:S(2)}, u32[]{:S(2)}) collective-permute-start(f32[4,8,16,128]{3,2,1,0:T(8,128)} %pad_maximum_fusion.4), channel_id=1, source_target_pairs={{0,8},{8,16},{16,24},{24,32},{32,40},{40,48},{48,56},{56,64},{64,7... | collective-permute-start | bytes 786440 | tf_op jit(solution)/shard_map/ppermute | solution.py:36
  5.1 7.3 %collective-permute-start = (f32[4,8,16,128]{3,2,1,0:T(8,128)}, f32[4,8,16,128]{3,2,1,0:T(8,128)S(1)}, u32[]{:S(2)}, u32[]{:S(2)}) collective-permute-start(f32[4,8,16,128]{3,2,1,0:T(8,128)} %pad_maximum_fusion.4), channel_id=1, source_target_pairs={{8,0},{16,8},{24,16},{32,24},{40,32},{48,40},{56,48},{64,56},{72,6... | collective-permute-start | bytes 786440 | tf_op jit(solution)/shard_map/ppermute | solution.py:37
  13.0 1.2 %and_bitcast_fusion = pred[2,8]{1,0:T(4,128)(4,1)} fusion(s32[1,2,8]{2,1,0:T(2,128)} %param.12), kind=kLoop, calls=%fused_computation.247 | loop fusion | flops 48 | bytes 80 | tf_op jit(solution)/shard_map/and | solution.py:172
  15.7 1.5 %fusion.118 = (f32[1]{0:T(128)}, f32[1]{0:T(128)}, f32[1]{0:T(128)}, f32[1]{0:T(128)}) fusion(f32[4]{0:T(128)} %param.9), kind=kLoop, calls=%fused_computation.286 | loop fusion | bytes 32 | tf_op jit(solution)/shard_map/slice | solution.py:76
  17.1 1.5 %fusion.119 = (f32[1]{0:T(128)}, f32[1]{0:T(128)}, f32[1]{0:T(128)}, f32[1]{0:T(128)}) fusion(f32[4]{0:T(128)} %param.10), kind=kLoop, calls=%fused_computation.287 | loop fusion | bytes 32 | tf_op jit(solution)/shard_map/slice | solution.py:76
  19.2 1.0 fusion
  20.8 0.8 reshape.583
  23.4 1.0 pad_maximum_fusion.1
  24.4 3.5 %collective-permute-start.3 = (f32[180240]{0:T(1024)}, f32[180240]{0:T(1024)}, u32[]{:S(2)}, u32[]{:S(2)}) collective-permute-start(f32[180240]{0:T(1024)} %get-tuple-element.47), channel_id=1, source_target_pairs={{0,1},{1,2},{2,3},{3,4},{4,5},{5,6},{6,7},{8,9},{9,10},{10,11},{11... | collective-permute-start | bytes 2162888 | tf_op jit(solution)/shard_map/ppermute | solution.py:39
  27.9 3.2 %collective-permute-start.2 = (f32[180240]{0:T(1024)S(1)}, f32[180240]{0:T(1024)S(1)}, u32[]{:S(2)}, u32[]{:S(2)}) collective-permute-start(f32[180240]{0:T(1024)S(1)} %get-tuple-element.48), channel_id=1, source_target_pairs={{1,0},{2,1},{3,2},{4,3},{5,4},{6,5},{7,6},{9,8},{10,9},{11,10},{12... | collective-permute-start | bytes 2162888 | tf_op jit(solution)/shard_map/ppermute | solution.py:40
  31.3 3.1 %select_add_fusion = f32[8,16,128]{2,1,0:T(8,128)} fusion(s32[8,16,128]{2,1,0:T(8,128)S(1)} %copy-done.17, f32[]{:T(128)} %bitcast.3, f32[]{:T(128)} %bitcast.2, f32[]{:T(128)} %bitcast.1, f32[]{:T(128)} %bitcast), kind=kLoop, calls=%fused_computation.190 | loop fusion | flops 180224 | bytes 131088 | tf_op jit(solution)/shard_map/add | solution.py:76
  34.4 8.2 %collective-permute-done.3 = f32[180240]{0:T(1024)} collective-permute-done((f32[180240]{0:T(1024)}, f32[180240]{0:T(1024)}, u32[]{:S(2)}, u32[]{:S(2)}) %collective-permute-start.3) | collective-permute-done | bytes 720992 | tf_op jit(solution)/shard_map/ppermute | solution.py:39
  42.5 1.0 slice.654
  43.5 1.9 %collective-permute-done.2 = f32[180240]{0:T(1024)S(1)} collective-permute-done((f32[180240]{0:T(1024)S(1)}, f32[180240]{0:T(1024)S(1)}, u32[]{:S(2)}, u32[]{:S(2)}) %collective-permute-start.2) | collective-permute-done | bytes 720992 | tf_op jit(solution)/shard_map/ppermute | solution.py:40
  45.5 0.8 copy-done.15
  46.3 1.3 %pad_maximum_fusion = f32[4,24,32,128]{3,2,1,0:T(8,128)S(1)} fusion(f32[4,24,8,128]{3,2,1,0:T(8,128)S(1)} %bitcast.134, f32[4,8,16,128]{3,2,1,0:T(8,128)} %copy-done.7, f32[1,8,16,128]{3,2,1,0:T(8,128)} %copy-done.9, f32[3,8,16,128]{3,2,1,0:T(8,128)} %param.7, f32[4,8,16,128]{3,2,1,0:T(8,128)} %copy-done.5, f32[4,24,8,128]{3,2,1,0:T(8,128)S(1)} %bitcast.132), kind=kLoop, calls=%fused_computation.3 | loop fusion | flops 1966080 | bytes 3145728 | tf_op jit(solution)/shard_map/concatenate | solution.py:119
  47.8 3.0 %multiply_select_fusion = (f32[22,30,128]{2,1,0:T(8,128)S(1)}, f32[22,30,128]{2,1,0:T(8,128)S(1)}) fusion(pred[22,30]{1,0:T(8,128)(4,1)S(1)} %broadcast_and_fusion, f32[22,30,128]{2,1,0:T(8,128)S(1)} %slice.664, f32[24,32,128]{2,1,0:T(8,128)S(1)} %get-tuple-element.12, f32[24,32,128]{2,1,0:T(8,128)S(1)} %get-tuple-element.10, f32[]{:T(128)} %bitcast.19, ...), kind=kLoop, calls=%fused_computation.54 | loop fusion | flops 1858560 | bytes 2704036 | tf_op jit(solution)/shard_map/jit(_where)/select_n | solution.py:138
  53.8 1.2 %fusion.106 = (s32[16]{0:T(128)}, s32[16]{0:T(128)}) fusion(f32[180240]{0:T(1024)} %collective-permute-done.3, f32[180240]{0:T(1024)} %copy-done.15), kind=kLoop, calls=%fused_computation.275 | loop fusion | flops 64 | bytes 256 | tf_op jit(solution)/shard_map/jit(clip)/min | solution.py:173
  56.3 1.3 %reshape.600 = s32[16]{0:T(128)} reshape(s32[2,8,1]{1,0,2:T(2,128)} %compare_select_fusion.2) | data formatting | bytes 128 | tf_op jit(solution)/shard_map/select_n | solution.py:173
  62.7 1.3 %reshape.585 = f32[80]{0:T(128)} reshape(f32[2,8,5]{2,1,0:T(8,128)} %get-tuple-element.37) | data formatting | bytes 640 | tf_op jit(solution)/shard_map/reshape | solution.py:21
  68.1 5.6 %all-to-all-start = ((f32[8,1,1360]{2,1,0:T(1,128)}), f32[8,1,1360]{2,1,0:T(1,128)}, u32[]{:S(2)}, u32[]{:S(2)}) async-start(f32[8,1,1360]{2,1,0:T(1,128)} %all_to_all.8), calls=%async_computation | async-start | bytes 90112 | tf_op jit(solution)/shard_map/all_to_all | solution.py:162
  73.7 1.3 %compare_and_fusion = (pred[16]{0:T(512)(128)(4,1)}, pred[16]{0:T(512)(128)(4,1)}) fusion(f32[180240]{0:T(1024)} %copy-done.15, f32[180240]{0:T(1024)} %collective-permute-done.3), kind=kLoop, calls=%fused_computation.246 | loop fusion | flops 128 | bytes 160 | tf_op jit(solution)/shard_map/and | solution.py:172
  75.6 0.8 slice.655
  76.4 1.0 slice.1145
  79.0 1.0 slice.1144
  80.9 0.8 copy.48
  86.6 4.7 %collective-permute-start.5 = (f32[2308]{0:T(1024)S(1)}, f32[2308]{0:T(1024)S(1)}, u32[]{:S(2)}, u32[]{:S(2)}) collective-permute-start(f32[2308]{0:T(1024)S(1)} %pad_maximum_fusion.20), channel_id=1, source_target_pairs={{8,0},{16,8},{24,16},{32,24},{40,32},{48,40},{56,48},{64,56},{72,6... | collective-permute-start | bytes 27704 | tf_op jit(solution)/shard_map/ppermute | solution.py:40
  91.4 1.9 %collective-permute-start.4 = (f32[2308]{0:T(1024)S(1)}, f32[2308]{0:T(1024)S(1)}, u32[]{:S(2)}, u32[]{:S(2)}) collective-permute-start(f32[2308]{0:T(1024)S(1)} %pad_maximum_fusion.19), channel_id=1, source_target_pairs={{0,8},{8,16},{16,24},{24,32},{32,40},{40,48},{48,56},{56,64},{64,7... | collective-permute-start | bytes 27704 | tf_op jit(solution)/shard_map/ppermute | solution.py:39
  93.5 6.5 %collective-permute-done.4 = f32[2308]{0:T(1024)S(1)} collective-permute-done((f32[2308]{0:T(1024)S(1)}, f32[2308]{0:T(1024)S(1)}, u32[]{:S(2)}, u32[]{:S(2)}) %collective-permute-start.4) | collective-permute-done | bytes 9264 | tf_op jit(solution)/shard_map/ppermute | solution.py:39
  104.1 0.9 fusion.51
  (194 shorter events, 30.6 us)
Async XLA Ops:
  0.6 18.6 %copy-start = (bf16[1,2,8,128,128]{4,3,2,1,0:T(8,128)(2,1)S(1)}, bf16[1,2,8,128,128]{4,3,2,1,0:T(8,128)(2,1)}, u32[]{:S(2)}) copy-start(bf16[1,2,8,128,128]{4,3,2,1,0:T(8,128)(2,1)} %param.13) | copy-start | bytes 1572868
  1.5 20.7 %copy-start.9 = (f32[1,8,16,128]{3,2,1,0:T(8,128)}, f32[1,8,16,128]{3,2,1,0:T(8,128)S(1)}, u32[]{:S(2)}) copy-start(f32[1,8,16,128]{3,2,1,0:T(8,128)S(1)} %convert_bitcast_fusion) | copy-start | bytes 196612
  3.2 19.0 %collective-permute-start.1 = (f32[4,8,16,128]{3,2,1,0:T(8,128)}, f32[4,8,16,128]{3,2,1,0:T(8,128)S(1)}, u32[]{:S(2)}, u32[]{:S(2)}) collective-permute-start(f32[4,8,16,128]{3,2,1,0:T(8,128)} %pad_maximum_fusion.4), channel_id=1, source_target_pairs={{0,8},{8,16},{16,24},{24,32},{32,40},{40,48},{48,56},{56,64},{64,7... | collective-permute-start | bytes 786440 | tf_op jit(solution)/shard_map/ppermute | solution.py:36
  5.1 17.1 %collective-permute-start = (f32[4,8,16,128]{3,2,1,0:T(8,128)}, f32[4,8,16,128]{3,2,1,0:T(8,128)S(1)}, u32[]{:S(2)}, u32[]{:S(2)}) collective-permute-start(f32[4,8,16,128]{3,2,1,0:T(8,128)} %pad_maximum_fusion.4), channel_id=1, source_target_pairs={{8,0},{16,8},{24,16},{32,24},{40,32},{48,40},{56,48},{64,56},{72,6... | collective-permute-start | bytes 786440 | tf_op jit(solution)/shard_map/ppermute | solution.py:37
  19.2 1.5 %copy-start.31 = (s32[1,2,8]{2,1,0:T(2,128)S(1)}, s32[1,2,8]{2,1,0:T(2,128)}, u32[]{:S(2)}) copy-start(s32[1,2,8]{2,1,0:T(2,128)} %param.12) | copy-start | bytes 196
  20.2 2.1 %copy-start.3 = (f32[3,8,16,128]{3,2,1,0:T(8,128)S(1)}, f32[3,8,16,128]{3,2,1,0:T(8,128)}, u32[]{:S(2)}) copy-start(f32[3,8,16,128]{3,2,1,0:T(8,128)} %param.7) | copy-start | bytes 589828
  20.4 31.0 %copy-start.26 = (pred[16,24]{1,0:T(8,128)(4,1)}, pred[16,24]{1,0:T(8,128)(4,1)S(1)}, u32[]{:S(2)}) copy-start(pred[16,24]{1,0:T(8,128)(4,1)S(1)} %broadcast_and_fusion.3) | copy-start | bytes 1156
  20.5 31.1 %copy-start.22 = (pred[14,22]{1,0:T(8,128)(4,1)}, pred[14,22]{1,0:T(8,128)(4,1)S(1)}, u32[]{:S(2)}) copy-start(pred[14,22]{1,0:T(8,128)(4,1)S(1)} %broadcast_and_fusion.4) | copy-start | bytes 928
  20.6 31.3 %copy-start.24 = (pred[12,20]{1,0:T(8,128)(4,1)}, pred[12,20]{1,0:T(8,128)(4,1)S(1)}, u32[]{:S(2)}) copy-start(pred[12,20]{1,0:T(8,128)(4,1)S(1)} %broadcast_and_fusion.5) | copy-start | bytes 724
  20.7 31.4 %copy-start.20 = (pred[10,18]{1,0:T(8,128)(4,1)}, pred[10,18]{1,0:T(8,128)(4,1)S(1)}, u32[]{:S(2)}) copy-start(pred[10,18]{1,0:T(8,128)(4,1)S(1)} %broadcast_and_fusion.6) | copy-start | bytes 544
  23.0 8.2 %copy-start.17 = (s32[8,16,128]{2,1,0:T(8,128)S(1)}, s32[8,16,128]{2,1,0:T(8,128)}, u32[]{:S(2)}) copy-start(s32[8,16,128]{2,1,0:T(8,128)} %param.8) | copy-start | bytes 196612
  24.4 18.1 %collective-permute-start.3 = (f32[180240]{0:T(1024)}, f32[180240]{0:T(1024)}, u32[]{:S(2)}, u32[]{:S(2)}) collective-permute-start(f32[180240]{0:T(1024)} %get-tuple-element.47), channel_id=1, source_target_pairs={{0,1},{1,2},{2,3},{3,4},{4,5},{5,6},{6,7},{8,9},{9,10},{10,11},{11... | collective-permute-start | bytes 2162888 | tf_op jit(solution)/shard_map/ppermute | solution.py:39
  27.9 17.5 %collective-permute-start.2 = (f32[180240]{0:T(1024)S(1)}, f32[180240]{0:T(1024)S(1)}, u32[]{:S(2)}, u32[]{:S(2)}) collective-permute-start(f32[180240]{0:T(1024)S(1)} %get-tuple-element.48), channel_id=1, source_target_pairs={{1,0},{2,1},{3,2},{4,3},{5,4},{6,5},{7,6},{9,8},{10,9},{11,10},{12... | collective-permute-start | bytes 2162888 | tf_op jit(solution)/shard_map/ppermute | solution.py:40
  45.4 2.2 %copy-start.1 = (f32[98304]{0:T(1024)}, f32[98304]{0:T(1024)S(1)}, u32[]{:S(2)}) copy-start(f32[98304]{0:T(1024)S(1)} %slice.651) | copy-start | bytes 1179652
  47.7 3.0 %copy-start.30 = (pred[20,28]{1,0:T(8,128)(4,1)S(1)}, pred[20,28]{1,0:T(8,128)(4,1)}, u32[]{:S(2)}) copy-start(pred[20,28]{1,0:T(8,128)(4,1)} %broadcast_and_fusion.1) | copy-start | bytes 1684
  51.9 9.5 %copy-start.32 = (s32[2,1,128]{2,1,0:T(1,128)S(1)}, s32[2,1,128]{2,1,0:T(1,128)}, u32[]{:S(2)}) copy-start(s32[2,1,128]{2,1,0:T(1,128)} %param.11) | copy-start | bytes 3076
  64.6 19.0 %copy-start.34 = (pred[2,8]{1,0:T(4,128)(4,1)S(1)}, pred[2,8]{1,0:T(4,128)(4,1)}, u32[]{:S(2)}) copy-start(pred[2,8]{1,0:T(4,128)(4,1)} %and_bitcast_fusion) | copy-start | bytes 52
  68.1 11.9 %all-to-all-start = ((f32[8,1,1360]{2,1,0:T(1,128)}), f32[8,1,1360]{2,1,0:T(1,128)}, u32[]{:S(2)}, u32[]{:S(2)}) async-start(f32[8,1,1360]{2,1,0:T(1,128)} %all_to_all.8), calls=%async_computation | async-start | bytes 90112 | tf_op jit(solution)/shard_map/all_to_all | solution.py:162
  77.4 9.1 %copy-start.19 = (f32[2048]{0:T(1024)S(1)}, f32[2048]{0:T(1024)}, u32[]{:S(2)}) copy-start(f32[2048]{0:T(1024)} %get-tuple-element.22) | copy-start | bytes 24580
  77.5 13.8 %copy-start.18 = (f32[2048]{0:T(1024)S(1)}, f32[2048]{0:T(1024)}, u32[]{:S(2)}) copy-start(f32[2048]{0:T(1024)} %get-tuple-element.21) | copy-start | bytes 24580
  77.5 22.6 %copy-start.33 = (pred[2]{0:T(512)(128)(4,1)S(1)}, pred[2]{0:T(512)(128)(4,1)}, u32[]{:S(2)}) copy-start(pred[2]{0:T(512)(128)(4,1)} %constant.69.clone.1) | copy-start | bytes 10
  79.9 20.7 %copy-start.28 = (pred[128]{0:T(512)(128)(4,1)S(1)}, pred[128]{0:T(512)(128)(4,1)}, u32[]{:S(2)}) copy-start(pred[128]{0:T(512)(128)(4,1)} %get-tuple-element.59) | copy-start | bytes 388
  80.0 20.7 %copy-start.29 = (pred[128]{0:T(512)(128)(4,1)S(1)}, pred[128]{0:T(512)(128)(4,1)}, u32[]{:S(2)}) copy-start(pred[128]{0:T(512)(128)(4,1)} %get-tuple-element.60) | copy-start | bytes 388
  83.7 17.3 %copy-start.27 = (pred[16,24]{1,0:T(8,128)(4,1)S(1)}, pred[16,24]{1,0:T(8,128)(4,1)}, u32[]{:S(2)}) copy-start(pred[16,24]{1,0:T(8,128)(4,1)} %copy-done.26) | copy-start | bytes 1156
  86.6 6.8 %collective-permute-start.5 = (f32[2308]{0:T(1024)S(1)}, f32[2308]{0:T(1024)S(1)}, u32[]{:S(2)}, u32[]{:S(2)}) collective-permute-start(f32[2308]{0:T(1024)S(1)} %pad_maximum_fusion.20), channel_id=1, source_target_pairs={{8,0},{16,8},{24,16},{32,24},{40,32},{48,40},{56,48},{64,56},{72,6... | collective-permute-start | bytes 27704 | tf_op jit(solution)/shard_map/ppermute | solution.py:40
  91.4 8.6 %collective-permute-start.4 = (f32[2308]{0:T(1024)S(1)}, f32[2308]{0:T(1024)S(1)}, u32[]{:S(2)}, u32[]{:S(2)}) collective-permute-start(f32[2308]{0:T(1024)S(1)} %pad_maximum_fusion.19), channel_id=1, source_target_pairs={{0,8},{8,16},{16,24},{24,32},{32,40},{40,48},{48,56},{56,64},{64,7... | collective-permute-start | bytes 27704 | tf_op jit(solution)/shard_map/ppermute | solution.py:39
  102.7 1.3 %copy-start.2 = (f32[98304]{0:T(1024)S(1)}, f32[98304]{0:T(1024)}, u32[]{:S(2)}) copy-start(f32[98304]{0:T(1024)} %copy-done.1) | copy-start | bytes 1179652
  102.7 1.3 %copy-start.4 = (f32[3,8,16,128]{3,2,1,0:T(8,128)S(1)}, f32[3,8,16,128]{3,2,1,0:T(8,128)}, u32[]{:S(2)}) copy-start(f32[3,8,16,128]{3,2,1,0:T(8,128)} %param.7) | copy-start | bytes 589828
  102.7 1.3 %copy-start.6 = (f32[4,8,16,128]{3,2,1,0:T(8,128)S(1)}, f32[4,8,16,128]{3,2,1,0:T(8,128)}, u32[]{:S(2)}) copy-start(f32[4,8,16,128]{3,2,1,0:T(8,128)} %copy-done.5) | copy-start | bytes 786436
  102.7 1.3 %copy-start.8 = (f32[4,8,16,128]{3,2,1,0:T(8,128)S(1)}, f32[4,8,16,128]{3,2,1,0:T(8,128)}, u32[]{:S(2)}) copy-start(f32[4,8,16,128]{3,2,1,0:T(8,128)} %copy-done.7) | copy-start | bytes 786436
  102.7 1.3 %copy-start.11 = (f32[3,10,18,128]{3,2,1,0:T(8,128)S(1)}, f32[3,10,18,128]{3,2,1,0:T(8,128)}, u32[]{:S(2)}) copy-start(f32[3,10,18,128]{3,2,1,0:T(8,128)} %slice.655) | copy-start | bytes 829444
  102.7 1.3 %copy-start.16 = (f32[8,16,128]{2,1,0:T(8,128)S(1)}, f32[8,16,128]{2,1,0:T(8,128)}, u32[]{:S(2)}) copy-start(f32[8,16,128]{2,1,0:T(8,128)} %select_add_fusion) | copy-start | bytes 196612
  (10 other events, 9.3 us)

commit v4 on v2

--- a/solution.py
+++ b/solution.py
@@ -42,20 +42,20 @@
 
 
 def widen(block, hx, hy, dx, dy):
+    size_y = block.shape[dy]
+    (lo,), (hi,) = swap(
+        "gy",
+        [lax.slice_in_dim(block, size_y - hy, size_y, axis=dy)],
+        [lax.slice_in_dim(block, 0, hy, axis=dy)],
+    )
+    block = jnp.concatenate([lo, block, hi], axis=dy)
     size_x = block.shape[dx]
     (lo,), (hi,) = swap(
         "gx",
         [lax.slice_in_dim(block, size_x - hx, size_x, axis=dx)],
         [lax.slice_in_dim(block, 0, hx, axis=dx)],
     )
-    block = jnp.concatenate([lo, block, hi], axis=dx)
-    size_y = block.shape[dy]
-    (lo,), (hi,) = swap(
-        "gy",
-        [lax.slice_in_dim(block, size_y - hy, size_y, axis=dy)],
-        [lax.slice_in_dim(block, 0, hy, axis=dy)],
-    )
-    return jnp.concatenate([lo, block, hi], axis=dy)
+    return jnp.concatenate([lo, block, hi], axis=dx)
 
 
 def zpad(a):

time: 80.8 us -> 88.1 us (1.090)
  other arithmetic: 16.6 us -> 24.3 us
  local copies, waits for them, and re-layouts: 6.81 us -> 11.6 us
  waiting for transfers between devices: 16.5 us -> 13.5 us
  starting transfers between devices: 38.9 us -> 36.2 us
    ppermute x2, starting transfers between devices: 11.6 us -> 8.52 us  [swap(): from_prev = [lax.ppermute(to_next[0], axis, _pairs(count, 1))]]
    ppermute x2, waiting for transfers between devices: 10.1 us -> 7.43 us  [swap(): from_next = lax.ppermute(_pack(to_prev), axis, _pairs(count, -1))]
    reshape x6, local copies, waits for them, and re-layouts: 0.52 us -> 1.93 us  [_unpack(): out.append(flat[start:start + a.size].reshape(a.shape))]
    select_n x5, other arithmetic: 2.14 us -> 3.51 us  [reset(): return jnp.where(bottom, lower, jnp.where(top, upper, values))]
    concatenate x4, other arithmetic: 0.3 us -> 1.66 us  [_pack(): return jnp.concatenate([a.reshape(-1) for a in arrays])]
    and x7, other arithmetic: 0.52 us -> 1.68 us  [inside(): return (ok_x[:, None] & ok_y[None, :])[:, :, None]]
    unnamed x18 -> x32, local copies, waits for them, and re-layouts: 0.63 us -> 1.78 us
    all_to_all x1, starting transfers between devices: 5.87 us -> 4.76 us  [body(): lax.all_to_all(copies, 'gy', 0, 0, tiled=True).reshape(group * 2, NODES)]
  transfers between devices with their start and end apart: 9 -> 9, of which waited for: 5 -> 5; matrix products, arithmetic and copies ran while one was open for 10% -> 18% of each run, Pallas kernels for 0% -> 0%
where the time goes in v4:
time: 88.1 us; the launch traced here: 87.1 us
  starting transfers between devices  36.2 us (41%)
  other arithmetic  24.3 us (28%)
  waiting for transfers between devices  13.5 us (15%)
  local copies, waits for them, and re-layouts  11.6 us (13%)
  between operations  1.22 us (1%)
    ppermute x2, starting transfers between devices, swap(): from_prev = lax.ppermute(_pack(to_next), axis, _pairs(count, 1))  13.2 us
    ppermute x2, starting transfers between devices, swap(): from_prev = [lax.ppermute(to_next[0], axis, _pairs(count, 1))]  8.52 us
    ppermute x2, waiting for transfers between devices, swap(): from_next = lax.ppermute(_pack(to_prev), axis, _pairs(count, -1))  7.43 us
    ppermute x2, starting transfers between devices, swap(): from_next = [lax.ppermute(to_prev[0], axis, _pairs(count, -1))]  5.94 us
    all_to_all x1, starting transfers between devices, body(): lax.all_to_all(copies, 'gy', 0, 0, tiled=True).reshape(group * 2, NODES)  4.76 us
    ppermute x2, starting transfers between devices, swap(): from_next = lax.ppermute(_pack(to_prev), axis, _pairs(count, -1))  3.82 us
    select_n x5, other arithmetic, reset(): return jnp.where(bottom, lower, jnp.where(top, upper, values))  3.51 us
    all_to_all x1, waiting for transfers between devices, body(): lax.all_to_all(copies, 'gy', 0, 0, tiled=True).reshape(group * 2, NODES)  3.17 us
  transfers between devices with their start and end apart: 9, of which 5 were waited for; matrix products, arithmetic and copies ran while one was open for 18% of the time, Pallas kernels for 0%

profile of v4, /device:TPU:125, one launch (start us, length us, event | category | flops | bytes accessed | tf_op | source)
XLA Modules:
  0.0 87.1 jit_solution(1840414897658465762)
XLA Ops:
  0.7 0.9 %convert_bitcast_fusion = f32[1,8,16,128]{3,2,1,0:T(8,128)S(1)} fusion(s32[8,16,128]{2,1,0:T(8,128)} %param.8), kind=kLoop, calls=%fused_computation.183 | loop fusion | flops 16384 | bytes 131072 | tf_op jit(solution)/shard_map/broadcast_in_dim | solution.py:97
  1.6 1.0 %fusion.63 = (f32[4,8,8,128]{3,2,1,0:T(8,128)S(1)}, f32[4,8,8,128]{3,2,1,0:T(8,128)S(1)}) fusion(f32[3,8,16,128]{3,2,1,0:T(8,128)} %param.7, f32[1,8,16,128]{3,2,1,0:T(8,128)S(1)} %convert_bitcast_fusion), kind=kLoop, calls=%fused_computation.144 | loop fusion | flops 65536 | bytes 524288 | tf_op jit(solution)/shard_map/concatenate | solution.py:97
  2.5 2.5 %collective-permute-start = (f32[4,8,8,128]{3,2,1,0:T(8,128)S(1)}, f32[4,8,8,128]{3,2,1,0:T(8,128)S(1)}, u32[]{:S(2)}, u32[]{:S(2)}) collective-permute-start(f32[4,8,8,128]{3,2,1,0:T(8,128)S(1)} %get-tuple-element.11), channel_id=1, source_target_pairs={{0,1},{1,2},{2,3},{3,4},{4,5},{5,6},{6,7},{8,9},{9,10},{10,11},{11... | collective-permute-start | bytes 393224 | tf_op jit(solution)/shard_map/ppermute | solution.py:36
  5.0 2.8 %collective-permute-start.1 = (f32[4,8,8,128]{3,2,1,0:T(8,128)S(1)}, f32[4,8,8,128]{3,2,1,0:T(8,128)S(1)}, u32[]{:S(2)}, u32[]{:S(2)}) collective-permute-start(f32[4,8,8,128]{3,2,1,0:T(8,128)S(1)} %get-tuple-element.12), channel_id=1, source_target_pairs={{1,0},{2,1},{3,2},{4,3},{5,4},{6,5},{7,6},{9,8},{10,9},{11,10},{12... | collective-permute-start | bytes 393224 | tf_op jit(solution)/shard_map/ppermute | solution.py:37
  8.5 1.3 %and_bitcast_fusion = pred[2,8]{1,0:T(4,128)(4,1)} fusion(s32[1,2,8]{2,1,0:T(2,128)} %param.12), kind=kLoop, calls=%fused_computation.222 | loop fusion | flops 48 | bytes 80 | tf_op jit(solution)/shard_map/and | solution.py:139
  10.4 1.5 %fusion.94 = (f32[1]{0:T(128)}, f32[1]{0:T(128)}, f32[1]{0:T(128)}, f32[1]{0:T(128)}) fusion(f32[4]{0:T(128)} %param.10), kind=kLoop, calls=%fused_computation.236 | loop fusion | bytes 32 | tf_op jit(solution)/shard_map/slice | solution.py:76
  14.3 1.5 %fusion.93 = (f32[1]{0:T(128)}, f32[1]{0:T(128)}, f32[1]{0:T(128)}, f32[1]{0:T(128)}) fusion(f32[4]{0:T(128)} %param.9), kind=kLoop, calls=%fused_computation.235 | loop fusion | bytes 32 | tf_op jit(solution)/shard_map/slice | solution.py:76
  16.5 1.0 %pad_maximum_fusion.1 = f32[4,8,32,128]{3,2,1,0:T(8,128)S(1)} fusion(f32[4,8,8,128]{3,2,1,0:T(8,128)S(1)} %collective-permute-done.1, f32[1,8,16,128]{3,2,1,0:T(8,128)S(1)} %convert_bitcast_fusion, f32[3,8,16,128]{3,2,1,0:T(8,128)} %param.7, f32[4,8,8,128]{3,2,1,0:T(8,128)S(1)} %collective-permute-done), kind=kLoop, calls=%fused_computation.21 | loop fusion | flops 393216 | bytes 1048576 | tf_op jit(solution)/shard_map/concatenate | solution.py:51
  17.4 3.1 %collective-permute-start.2 = (f32[4,8,32,128]{3,2,1,0:T(8,128)S(1)}, f32[4,8,32,128]{3,2,1,0:T(8,128)S(1)}, u32[]{:S(2)}, u32[]{:S(2)}) collective-permute-start(f32[4,8,32,128]{3,2,1,0:T(8,128)S(1)} %pad_maximum_fusion.1), channel_id=1, source_target_pairs={{8,0},{16,8},{24,16},{32,24},{40,32},{48,40},{56,48},{64,56},{72,6... | collective-permute-start | bytes 1572872 | tf_op jit(solution)/shard_map/ppermute | solution.py:37
  20.6 6.0 %collective-permute-start.3 = (f32[4,8,32,128]{3,2,1,0:T(8,128)S(1)}, f32[4,8,32,128]{3,2,1,0:T(8,128)S(1)}, u32[]{:S(2)}, u32[]{:S(2)}) collective-permute-start(f32[4,8,32,128]{3,2,1,0:T(8,128)S(1)} %pad_maximum_fusion.1), channel_id=1, source_target_pairs={{0,8},{8,16},{16,24},{24,32},{32,40},{40,48},{48,56},{56,64},{64,7... | collective-permute-start | bytes 1572872 | tf_op jit(solution)/shard_map/ppermute | solution.py:36
  26.7 3.1 %select_add_fusion = f32[8,16,128]{2,1,0:T(8,128)} fusion(s32[8,16,128]{2,1,0:T(8,128)S(1)} %copy-done.8, f32[]{:T(128)} %bitcast.3, f32[]{:T(128)} %bitcast.2, f32[]{:T(128)} %bitcast.1, f32[]{:T(128)} %bitcast), kind=kLoop, calls=%fused_computation.184 | loop fusion | flops 180224 | bytes 131088 | tf_op jit(solution)/shard_map/add | solution.py:76
  29.9 1.8 %collective-permute-done.2 = f32[4,8,32,128]{3,2,1,0:T(8,128)S(1)} collective-permute-done((f32[4,8,32,128]{3,2,1,0:T(8,128)S(1)}, f32[4,8,32,128]{3,2,1,0:T(8,128)S(1)}, u32[]{:S(2)}, u32[]{:S(2)}) %collective-permute-start.2) | collective-permute-done | bytes 524320 | tf_op jit(solution)/shard_map/ppermute | solution.py:37
  31.7 1.1 %collective-permute-done.3 = f32[4,8,32,128]{3,2,1,0:T(8,128)S(1)} collective-permute-done((f32[4,8,32,128]{3,2,1,0:T(8,128)S(1)}, f32[4,8,32,128]{3,2,1,0:T(8,128)S(1)}, u32[]{:S(2)}, u32[]{:S(2)}) %collective-permute-start.3) | collective-permute-done | bytes 524320 | tf_op jit(solution)/shard_map/ppermute | solution.py:36
  32.8 1.1 %pad_maximum_fusion = f32[4,24,32,128]{3,2,1,0:T(8,128)S(1)} fusion(f32[4,8,32,128]{3,2,1,0:T(8,128)S(1)} %collective-permute-done.2, f32[4,8,8,128]{3,2,1,0:T(8,128)} %copy-done.5, f32[1,8,16,128]{3,2,1,0:T(8,128)S(1)} %convert_bitcast_fusion, f32[3,8,16,128]{3,2,1,0:T(8,128)S(1)} %copy-done.1, f32[4,8,8,128]{3,2,1,0:T(8,128)S(1)} %collective-permute-done, ...), kind=kLoop, calls=%fused_computation.1 | loop fusion | flops 1966080 | bytes 3145728 | tf_op jit(solution)/shard_map/concatenate | solution.py:58
  34.6 2.9 %multiply_select_fusion = (f32[22,30,128]{2,1,0:T(8,128)S(1)}, f32[22,30,128]{2,1,0:T(8,128)S(1)}) fusion(pred[22,30]{1,0:T(8,128)(4,1)S(1)} %copy-done.12, f32[22,30,128]{2,1,0:T(8,128)S(1)} %slice.585, f32[24,32,128]{2,1,0:T(8,128)S(1)} %get-tuple-element.10, f32[24,32,128]{2,1,0:T(8,128)S(1)} %get-tuple-element.8, f32[]{:T(128)} %bitcast.10, f32[]{:T(128)} %bitcast.9, ...), kind=kLoop, calls=%fused_computation.48 | loop fusion | flops 1858560 | bytes 2704036 | tf_op jit(solution)/shard_map/jit(_where)/select_n | solution.py:117
  40.2 4.8 %all-to-all-start = ((bf16[8,2,128]{2,1,0:T(2,128)(2,1)}), bf16[8,2,128]{2,1,0:T(2,128)(2,1)S(1)}, u32[]{:S(2)}, u32[]{:S(2)}) async-start(bf16[8,2,128]{2,1,0:T(2,128)(2,1)} %broadcast_in_dim.343), calls=%async_computation | async-start | bytes 8192 | tf_op jit(solution)/shard_map/all_to_all | solution.py:138
  45.0 3.2 %all-to-all-done = bf16[8,2,128]{2,1,0:T(2,128)(2,1)S(1)} async-done(((bf16[8,2,128]{2,1,0:T(2,128)(2,1)}), bf16[8,2,128]{2,1,0:T(2,128)(2,1)S(1)}, u32[]{:S(2)}, u32[]{:S(2)}) %all-to-all-start) | async-done | bytes 4128 | tf_op jit(solution)/shard_map/all_to_all | solution.py:138
  49.6 8.9 %collective-permute-start.4 = (f32[2208]{0:T(1024)S(1)}, f32[2208]{0:T(1024)}, u32[]{:S(2)}, u32[]{:S(2)}) collective-permute-start(f32[2208]{0:T(1024)S(1)} %pad_maximum_fusion.17), channel_id=1, source_target_pairs={{0,8},{8,16},{16,24},{24,32},{32,40},{40,48},{48,56},{56,64},{64,7... | collective-permute-start | bytes 26504 | tf_op jit(solution)/shard_map/ppermute | solution.py:39
  58.7 1.9 %collective-permute-start.5 = (f32[2208]{0:T(1024)S(1)}, f32[2208]{0:T(1024)S(1)}, u32[]{:S(2)}, u32[]{:S(2)}) collective-permute-start(f32[2208]{0:T(1024)S(1)} %pad_maximum_fusion.18), channel_id=1, source_target_pairs={{8,0},{16,8},{24,16},{32,24},{40,32},{48,40},{56,48},{64,56},{72,6... | collective-permute-start | bytes 26504 | tf_op jit(solution)/shard_map/ppermute | solution.py:40
  61.2 0.8 slice.576
  62.8 4.5 %collective-permute-done.5 = f32[2208]{0:T(1024)S(1)} collective-permute-done((f32[2208]{0:T(1024)S(1)}, f32[2208]{0:T(1024)S(1)}, u32[]{:S(2)}, u32[]{:S(2)}) %collective-permute-start.5) | collective-permute-done | bytes 8864 | tf_op jit(solution)/shard_map/ppermute | solution.py:40
  68.1 0.7 pad_maximum_fusion.19
  68.8 4.3 %collective-permute-start.6 = (f32[1204]{0:T(1024)S(1)}, f32[1204]{0:T(1024)S(1)}, u32[]{:S(2)}, u32[]{:S(2)}) collective-permute-start(f32[1204]{0:T(1024)S(1)} %pad_maximum_fusion.19), channel_id=1, source_target_pairs={{0,1},{1,2},{2,3},{3,4},{4,5},{5,6},{6,7},{8,9},{9,10},{10,11},{11... | collective-permute-start | bytes 14456 | tf_op jit(solution)/shard_map/ppermute | solution.py:39
  73.2 0.8 pad_maximum_fusion.20
  74.0 1.9 %collective-permute-start.7 = (f32[1204]{0:T(1024)S(1)}, f32[1204]{0:T(1024)S(1)}, u32[]{:S(2)}, u32[]{:S(2)}) collective-permute-start(f32[1204]{0:T(1024)S(1)} %pad_maximum_fusion.20), channel_id=1, source_target_pairs={{1,0},{2,1},{3,2},{4,3},{5,4},{6,5},{7,6},{9,8},{10,9},{11,10},{12... | collective-permute-start | bytes 14456 | tf_op jit(solution)/shard_map/ppermute | solution.py:40
  75.9 0.8 slice_bitcast_fusion.6
  76.7 0.8 slice_bitcast_fusion.5
  77.6 2.9 %collective-permute-done.7 = f32[1204]{0:T(1024)S(1)} collective-permute-done((f32[1204]{0:T(1024)S(1)}, f32[1204]{0:T(1024)S(1)}, u32[]{:S(2)}, u32[]{:S(2)}) %collective-permute-start.7) | collective-permute-done | bytes 4848 | tf_op jit(solution)/shard_map/ppermute | solution.py:40
  80.6 0.7 broadcast_select_fusion
  81.8 1.1 %select_select_fusion = f32[2,18,26,128]{3,2,1,0:T(8,128)S(1)} fusion(f32[2,18,26]{2,1,0:T(8,128)S(1)} %stack.61, f32[2,18,26]{2,1,0:T(8,128)S(1)} %get-tuple-element.4, pred[128]{0:T(512)(128)(4,1)} %get-tuple-element.41, pred[128]{0:T(512)(128)(4,1)} %get-tuple-element.42), kind=kLoop, calls=%fused_computation.20 | loop fusion | flops 239616 | bytes 486976 | tf_op jit(solution)/shard_map/jit(_where)/select_n | solution.py:177
  82.9 1.2 %fusion.7 = f32[2,16,24,128]{3,2,1,0:T(8,128)S(1)} fusion(f32[2,18,26,128]{3,2,1,0:T(8,128)S(1)} %select_select_fusion, f32[2,16,24]{2,1,0:T(8,128)S(1)} %stack.59, f32[2,16,24]{2,1,0:T(8,128)S(1)} %stack.58, pred[16,24]{1,0:T(8,128)(4,1)S(1)} %broadcast_and_fusion.3, pred[128]{0:T(512)(128)(4,1)} %get-tuple-element.41, pred[128]{0:T(512)(128)(4,1)} %get-tuple-element.42), kind=kLoop, calls=%fused_computation.33 | loop fusion | flops 884736 | bytes 2590976 | tf_op jit(solution)/shard_map/jit(_where)/select_n | solution.py:177
  86.3 0.9 fusion.49
  (123 shorter events, 14.3 us)
Async XLA Ops:
  0.6 48.3 %copy-start = (bf16[1,2,8,128,128]{4,3,2,1,0:T(8,128)(2,1)S(1)}, bf16[1,2,8,128,128]{4,3,2,1,0:T(8,128)(2,1)}, u32[]{:S(2)}) copy-start(bf16[1,2,8,128,128]{4,3,2,1,0:T(8,128)(2,1)} %param.13) | copy-start | bytes 1572868
  0.6 26.1 %copy-start.8 = (s32[8,16,128]{2,1,0:T(8,128)S(1)}, s32[8,16,128]{2,1,0:T(8,128)}, u32[]{:S(2)}) copy-start(s32[8,16,128]{2,1,0:T(8,128)} %param.8) | copy-start | bytes 196612
  0.7 32.1 %copy-start.1 = (f32[3,8,16,128]{3,2,1,0:T(8,128)S(1)}, f32[3,8,16,128]{3,2,1,0:T(8,128)}, u32[]{:S(2)}) copy-start(f32[3,8,16,128]{3,2,1,0:T(8,128)} %param.7) | copy-start | bytes 589828
  2.5 13.2 %collective-permute-start = (f32[4,8,8,128]{3,2,1,0:T(8,128)S(1)}, f32[4,8,8,128]{3,2,1,0:T(8,128)S(1)}, u32[]{:S(2)}, u32[]{:S(2)}) collective-permute-start(f32[4,8,8,128]{3,2,1,0:T(8,128)S(1)} %get-tuple-element.11), channel_id=1, source_target_pairs={{0,1},{1,2},{2,3},{3,4},{4,5},{5,6},{6,7},{8,9},{9,10},{10,11},{11... | collective-permute-start | bytes 393224 | tf_op jit(solution)/shard_map/ppermute | solution.py:36
  5.0 10.7 %collective-permute-start.1 = (f32[4,8,8,128]{3,2,1,0:T(8,128)S(1)}, f32[4,8,8,128]{3,2,1,0:T(8,128)S(1)}, u32[]{:S(2)}, u32[]{:S(2)}) collective-permute-start(f32[4,8,8,128]{3,2,1,0:T(8,128)S(1)} %get-tuple-element.12), channel_id=1, source_target_pairs={{1,0},{2,1},{3,2},{4,3},{5,4},{6,5},{7,6},{9,8},{10,9},{11,10},{12... | collective-permute-start | bytes 393224 | tf_op jit(solution)/shard_map/ppermute | solution.py:37
  15.8 18.1 %copy-start.3 = (f32[4,8,8,128]{3,2,1,0:T(8,128)}, f32[4,8,8,128]{3,2,1,0:T(8,128)S(1)}, u32[]{:S(2)}) copy-start(f32[4,8,8,128]{3,2,1,0:T(8,128)S(1)} %collective-permute-done) | copy-start | bytes 393220
  15.8 0.7 copy-start.5
  17.4 14.2 %collective-permute-start.2 = (f32[4,8,32,128]{3,2,1,0:T(8,128)S(1)}, f32[4,8,32,128]{3,2,1,0:T(8,128)S(1)}, u32[]{:S(2)}, u32[]{:S(2)}) collective-permute-start(f32[4,8,32,128]{3,2,1,0:T(8,128)S(1)} %pad_maximum_fusion.1), channel_id=1, source_target_pairs={{8,0},{16,8},{24,16},{32,24},{40,32},{48,40},{56,48},{64,56},{72,6... | collective-permute-start | bytes 1572872 | tf_op jit(solution)/shard_map/ppermute | solution.py:37
  20.6 12.2 %collective-permute-start.3 = (f32[4,8,32,128]{3,2,1,0:T(8,128)S(1)}, f32[4,8,32,128]{3,2,1,0:T(8,128)S(1)}, u32[]{:S(2)}, u32[]{:S(2)}) collective-permute-start(f32[4,8,32,128]{3,2,1,0:T(8,128)S(1)} %pad_maximum_fusion.1), channel_id=1, source_target_pairs={{0,8},{8,16},{16,24},{24,32},{32,40},{40,48},{48,56},{56,64},{64,7... | collective-permute-start | bytes 1572872 | tf_op jit(solution)/shard_map/ppermute | solution.py:36
  33.9 0.7 copy-start.12
  34.0 3.5 %copy-start.11 = (pred[20,28]{1,0:T(8,128)(4,1)S(1)}, pred[20,28]{1,0:T(8,128)(4,1)}, u32[]{:S(2)}) copy-start(pred[20,28]{1,0:T(8,128)(4,1)} %broadcast_and_fusion.1) | copy-start | bytes 1684
  38.6 0.8 copy-start.14
  38.6 10.3 %copy-start.15 = (pred[2,8]{1,0:T(4,128)(4,1)S(1)}, pred[2,8]{1,0:T(4,128)(4,1)}, u32[]{:S(2)}) copy-start(pred[2,8]{1,0:T(4,128)(4,1)} %and_bitcast_fusion) | copy-start | bytes 52
  40.2 7.9 %all-to-all-start = ((bf16[8,2,128]{2,1,0:T(2,128)(2,1)}), bf16[8,2,128]{2,1,0:T(2,128)(2,1)S(1)}, u32[]{:S(2)}, u32[]{:S(2)}) async-start(bf16[8,2,128]{2,1,0:T(2,128)(2,1)} %broadcast_in_dim.343), calls=%async_computation | async-start | bytes 8192 | tf_op jit(solution)/shard_map/all_to_all | solution.py:138
  49.6 12.4 %collective-permute-start.4 = (f32[2208]{0:T(1024)S(1)}, f32[2208]{0:T(1024)}, u32[]{:S(2)}, u32[]{:S(2)}) collective-permute-start(f32[2208]{0:T(1024)S(1)} %pad_maximum_fusion.17), channel_id=1, source_target_pairs={{0,8},{8,16},{16,24},{24,32},{32,40},{40,48},{48,56},{56,64},{64,7... | collective-permute-start | bytes 26504 | tf_op jit(solution)/shard_map/ppermute | solution.py:39
  58.7 8.6 %collective-permute-start.5 = (f32[2208]{0:T(1024)S(1)}, f32[2208]{0:T(1024)S(1)}, u32[]{:S(2)}, u32[]{:S(2)}) collective-permute-start(f32[2208]{0:T(1024)S(1)} %pad_maximum_fusion.18), channel_id=1, source_target_pairs={{8,0},{16,8},{24,16},{32,24},{40,32},{48,40},{56,48},{64,56},{72,6... | collective-permute-start | bytes 26504 | tf_op jit(solution)/shard_map/ppermute | solution.py:40
  67.3 0.6 copy-start.13
  68.8 8.7 %collective-permute-start.6 = (f32[1204]{0:T(1024)S(1)}, f32[1204]{0:T(1024)S(1)}, u32[]{:S(2)}, u32[]{:S(2)}) collective-permute-start(f32[1204]{0:T(1024)S(1)} %pad_maximum_fusion.19), channel_id=1, source_target_pairs={{0,1},{1,2},{2,3},{3,4},{4,5},{5,6},{6,7},{8,9},{9,10},{10,11},{11... | collective-permute-start | bytes 14456 | tf_op jit(solution)/shard_map/ppermute | solution.py:39
  74.0 6.5 %collective-permute-start.7 = (f32[1204]{0:T(1024)S(1)}, f32[1204]{0:T(1024)S(1)}, u32[]{:S(2)}, u32[]{:S(2)}) collective-permute-start(f32[1204]{0:T(1024)S(1)} %pad_maximum_fusion.20), channel_id=1, source_target_pairs={{1,0},{2,1},{3,2},{4,3},{5,4},{6,5},{7,6},{9,8},{10,9},{11,10},{12... | collective-permute-start | bytes 14456 | tf_op jit(solution)/shard_map/ppermute | solution.py:40
  81.8 2.3 %copy-start.9 = (pred[128]{0:T(512)(128)(4,1)S(1)}, pred[128]{0:T(512)(128)(4,1)}, u32[]{:S(2)}) copy-start(pred[128]{0:T(512)(128)(4,1)} %get-tuple-element.41) | copy-start | bytes 388
  81.8 2.3 %copy-start.10 = (pred[128]{0:T(512)(128)(4,1)S(1)}, pred[128]{0:T(512)(128)(4,1)}, u32[]{:S(2)}) copy-start(pred[128]{0:T(512)(128)(4,1)} %get-tuple-element.42) | copy-start | bytes 388
  85.0 1.3 %copy-start.2 = (f32[3,10,18,128]{3,2,1,0:T(8,128)S(1)}, f32[3,10,18,128]{3,2,1,0:T(8,128)}, u32[]{:S(2)}) copy-start(f32[3,10,18,128]{3,2,1,0:T(8,128)} %slice.576) | copy-start | bytes 829444
  85.0 1.3 %copy-start.4 = (f32[4,8,8,128]{3,2,1,0:T(8,128)S(1)}, f32[4,8,8,128]{3,2,1,0:T(8,128)}, u32[]{:S(2)}) copy-start(f32[4,8,8,128]{3,2,1,0:T(8,128)} %copy-done.3) | copy-start | bytes 393220
  85.0 1.2 %copy-start.6 = (f32[4,8,8,128]{3,2,1,0:T(8,128)S(1)}, f32[4,8,8,128]{3,2,1,0:T(8,128)}, u32[]{:S(2)}) copy-start(f32[4,8,8,128]{3,2,1,0:T(8,128)} %copy-done.5) | copy-start | bytes 393220
  85.0 1.2 %copy-start.7 = (f32[8,16,128]{2,1,0:T(8,128)S(1)}, f32[8,16,128]{2,1,0:T(8,128)}, u32[]{:S(2)}) copy-start(f32[8,16,128]{2,1,0:T(8,128)} %select_add_fusion) | copy-start | bytes 196612

commit v5 on v2

--- a/solution.py
+++ b/solution.py
@@ -41,7 +41,7 @@
     return _unpack(from_prev, to_next), _unpack(from_next, to_prev)
 
 
-def widen(block, hx, hy, dx, dy):
+def widen(block, hx, hy, dx, dy, trim=0):
     size_x = block.shape[dx]
     (lo,), (hi,) = swap(
         "gx",
@@ -50,12 +50,16 @@
     )
     block = jnp.concatenate([lo, block, hi], axis=dx)
     size_y = block.shape[dy]
+    width = block.shape[dx]
+    inner = lax.slice_in_dim(block, trim, width - trim, axis=dx)
     (lo,), (hi,) = swap(
         "gy",
-        [lax.slice_in_dim(block, size_y - hy, size_y, axis=dy)],
-        [lax.slice_in_dim(block, 0, hy, axis=dy)],
-    )
-    return jnp.concatenate([lo, block, hi], axis=dy)
+        [lax.slice_in_dim(inner, size_y - hy, size_y, axis=dy)],
+        [lax.slice_in_dim(inner, 0, hy, axis=dy)],
+    )
+    pad = [(0, 0)] * block.ndim
+    pad[dx] = (trim, trim)
+    return jnp.concatenate([jnp.pad(lo, pad), block, jnp.pad(hi, pad)], axis=dy)
 
 
 def zpad(a):
@@ -95,7 +99,7 @@
 
     halo = SWEEPS
     data = jnp.concatenate([magnet, grain_ids.astype(jnp.float32)[None]], axis=0)
-    wide = widen(data, halo, halo, 1, 2)
+    wide = widen(data, halo, halo, 1, 2, trim=1)
     m0, m1, m2 = wide[0], wide[1], wide[2]
     exch_coef = lookup(grain_ids, exch_table)
 
@@ -147,18 +151,18 @@
     planes = cells.reshape(2, cells_x, cells_y)
 
     he = EXT_SWEEPS + 1
+    (q_lo, t_lo), (q_hi, t_hi) = swap(
+        "gy",
+        [planes[:, :, cells_y - he :], scalar[:, cells_y - 1 :]],
+        [planes[:, :, :he], scalar[:, :1]],
+    )
+    planes_y = jnp.concatenate([q_lo, planes, q_hi], axis=2)
     (p_lo, s_lo), (p_hi, s_hi) = swap(
         "gx",
-        [planes[:, cells_x - he :], scalar[cells_x - 1 :]],
-        [planes[:, :he], scalar[:1]],
-    )
-    planes_x = jnp.concatenate([p_lo, planes, p_hi], axis=1)
-    (q_lo, t_lo), (q_hi, t_hi) = swap(
-        "gy",
-        [planes_x[:, :, cells_y - he :], scalar[:, cells_y - 1 :]],
-        [planes_x[:, :, :he], scalar[:, :1]],
-    )
-    planes_w = jnp.concatenate([q_lo, planes_x, q_hi], axis=2)
+        [planes_y[:, cells_x - he :], scalar[cells_x - 1 :]],
+        [planes_y[:, :he], scalar[:1]],
+    )
+    planes_w = jnp.concatenate([p_lo, planes_y, p_hi], axis=1)
 
     column = jnp.concatenate([s_lo, scalar, s_hi], axis=0)
     row_pad = ((1, 1), (0, 0), (0, 0))

time: 80.8 us -> 104 us (1.29); the launches traced: 80.3 us -> 102 us
  local copies, waits for them, and re-layouts: 6.81 us -> 22.5 us
  other arithmetic: 16.6 us -> 27.6 us
  waiting for transfers between devices: 16.5 us -> 11.4 us
    concatenate x4, other arithmetic: 0.3 us -> 5.46 us  [_pack(): return jnp.concatenate([a.reshape(-1) for a in arrays])]
    slice x6, local copies, waits for them, and re-layouts: 0.15 us -> 5.29 us  [_unpack(): out.append(flat[start:start + a.size].reshape(a.shape))]
    reshape x5, local copies, waits for them, and re-layouts: 0.38 us -> 5.21 us  [_pack(): return jnp.concatenate([a.reshape(-1) for a in arrays])]
    ppermute x2, waiting for transfers between devices: 10.1 us -> 5.75 us  [swap(): from_next = lax.ppermute(_pack(to_prev), axis, _pairs(count, -1))]
    reshape x6, local copies, waits for them, and re-layouts: 0.52 us -> 3.76 us  [_unpack(): out.append(flat[start:start + a.size].reshape(a.shape))]
    select_n x5, other arithmetic: 2.14 us -> 3.5 us  [reset(): return jnp.where(bottom, lower, jnp.where(top, upper, values))]
    slice x3 -> x2, local copies, waits for them, and re-layouts: 0.13 us -> 1.29 us  [the longest x1 0.69 us: body(): planes[:, :, cells_y - he:]]
  transfers between devices with their start and end apart: 9 -> 9, of which waited for: 5 -> 5; matrix products, arithmetic and copies ran while one was open for 10% -> 18% of each run, Pallas kernels for 0% -> 0%
where the time goes in v5:
time: 104 us; the launch traced here: 102 us
  starting transfers between devices  39.1 us (38%)
  other arithmetic  27.6 us (27%)
  local copies, waits for them, and re-layouts  22.5 us (22%)
  waiting for transfers between devices  11.4 us (11%)
  between operations  1.24 us (1%)
    ppermute x2, starting transfers between devices, swap(): from_prev = lax.ppermute(_pack(to_next), axis, _pairs(count, 1))  12.9 us
    ppermute x2, starting transfers between devices, swap(): from_prev = [lax.ppermute(to_next[0], axis, _pairs(count, 1))]  11.6 us
    all_to_all x1, starting transfers between devices, body(): lax.all_to_all(copies, 'gy', 0, 0, tiled=True).reshape(group * 2, NODES)  5.87 us
    ppermute x2, waiting for transfers between devices, swap(): from_next = lax.ppermute(_pack(to_prev), axis, _pairs(count, -1))  5.75 us
    concatenate x4, other arithmetic, _pack(): return jnp.concatenate([a.reshape(-1) for a in arrays])  5.46 us
    slice x6, local copies, waits for them, and re-layouts, _unpack(): out.append(flat[start:start + a.size].reshape(a.shape))  5.29 us
    reshape x5, local copies, waits for them, and re-layouts, _pack(): return jnp.concatenate([a.reshape(-1) for a in arrays])  5.21 us
    ppermute x2, starting transfers between devices, swap(): from_next = [lax.ppermute(to_prev[0], axis, _pairs(count, -1))]  4.96 us
  transfers between devices with their start and end apart: 9, of which 5 were waited for; matrix products, arithmetic and copies ran while one was open for 18% of the time, Pallas kernels for 0%

profile of v5, /device:TPU:125, one launch (start us, length us, event | category | flops | bytes accessed | tf_op | source)
XLA Modules:
  0.0 102.1 jit_solution(5435317485422908854)
XLA Ops:
  0.7 0.9 convert_bitcast_fusion
  1.6 0.9 pad_maximum_fusion.5
  2.5 2.6 %collective-permute-start = (f32[4,8,16,128]{3,2,1,0:T(8,128)S(1)}, f32[4,8,16,128]{3,2,1,0:T(8,128)S(1)}, u32[]{:S(2)}, u32[]{:S(2)}) collective-permute-start(f32[4,8,16,128]{3,2,1,0:T(8,128)S(1)} %pad_maximum_fusion.5), channel_id=1, source_target_pairs={{8,0},{16,8},{24,16},{32,24},{40,32},{48,40},{56,48},{64,56},{72,6... | collective-permute-start | bytes 786440 | tf_op jit(solution)/shard_map/ppermute | solution.py:37
  5.1 6.6 %collective-permute-start.1 = (f32[4,8,16,128]{3,2,1,0:T(8,128)S(1)}, f32[4,8,16,128]{3,2,1,0:T(8,128)S(1)}, u32[]{:S(2)}, u32[]{:S(2)}) collective-permute-start(f32[4,8,16,128]{3,2,1,0:T(8,128)S(1)} %pad_maximum_fusion.5), channel_id=1, source_target_pairs={{0,8},{8,16},{16,24},{24,32},{32,40},{40,48},{48,56},{56,64},{64,7... | collective-permute-start | bytes 786440 | tf_op jit(solution)/shard_map/ppermute | solution.py:36
  12.4 1.2 %and_bitcast_fusion = pred[2,8]{1,0:T(4,128)(4,1)} fusion(s32[1,2,8]{2,1,0:T(2,128)} %param.12), kind=kLoop, calls=%fused_computation.222 | loop fusion | flops 48 | bytes 80 | tf_op jit(solution)/shard_map/and | solution.py:143
  13.6 1.4 %fusion.93 = (f32[1]{0:T(128)}, f32[1]{0:T(128)}, f32[1]{0:T(128)}, f32[1]{0:T(128)}) fusion(f32[4]{0:T(128)} %param.10), kind=kLoop, calls=%fused_computation.236 | loop fusion | bytes 32 | tf_op jit(solution)/shard_map/slice | solution.py:80
  15.9 1.1 %pad_maximum_fusion.1 = (f32[4,22,8,128]{3,2,1,0:T(8,128)S(1)}, f32[4,22,8,128]{3,2,1,0:T(8,128)S(1)}) fusion(f32[4,8,16,128]{3,2,1,0:T(8,128)S(1)} %collective-permute-done, f32[4,8,16,128]{3,2,1,0:T(8,128)S(1)} %collective-permute-done.1, f32[1,8,16,128]{3,2,1,0:T(8,128)S(1)} %convert_bitcast_fusion, f32[3,8,16,128]{3,2,1,0:T(8,128)} %param.7), kind=kLoop, calls=%fused_computation.47 | loop fusion | flops 540672 | bytes 1507328 | tf_op jit(solution)/shard_map/concatenate | solution.py:51
  17.0 2.4 %collective-permute-start.2 = (f32[4,22,8,128]{3,2,1,0:T(8,128)S(1)}, f32[4,22,8,128]{3,2,1,0:T(8,128)S(1)}, u32[]{:S(2)}, u32[]{:S(2)}) collective-permute-start(f32[4,22,8,128]{3,2,1,0:T(8,128)S(1)} %get-tuple-element.12), channel_id=1, source_target_pairs={{1,0},{2,1},{3,2},{4,3},{5,4},{6,5},{7,6},{9,8},{10,9},{11,10},{12... | collective-permute-start | bytes 1081352 | tf_op jit(solution)/shard_map/ppermute | solution.py:37
  19.4 5.0 %collective-permute-start.3 = (f32[4,22,8,128]{3,2,1,0:T(8,128)S(1)}, f32[4,22,8,128]{3,2,1,0:T(8,128)S(1)}, u32[]{:S(2)}, u32[]{:S(2)}) collective-permute-start(f32[4,22,8,128]{3,2,1,0:T(8,128)S(1)} %get-tuple-element.11), channel_id=1, source_target_pairs={{0,1},{1,2},{2,3},{3,4},{4,5},{5,6},{6,7},{8,9},{9,10},{10,11},{11... | collective-permute-start | bytes 1081352 | tf_op jit(solution)/shard_map/ppermute | solution.py:36
  25.1 2.4 %select_add_fusion = f32[8,16,128]{2,1,0:T(8,128)S(1)} fusion(s32[8,16,128]{2,1,0:T(8,128)S(1)} %copy-done.6, f32[]{:T(128)} %bitcast.3, f32[]{:T(128)} %bitcast.2, f32[]{:T(128)} %bitcast.1, f32[]{:T(128)} %bitcast), kind=kLoop, calls=%fused_computation.184 | loop fusion | flops 180224 | bytes 131088 | tf_op jit(solution)/shard_map/add | solution.py:80
  27.5 2.2 %collective-permute-done.2 = f32[4,22,8,128]{3,2,1,0:T(8,128)S(1)} collective-permute-done((f32[4,22,8,128]{3,2,1,0:T(8,128)S(1)}, f32[4,22,8,128]{3,2,1,0:T(8,128)S(1)}, u32[]{:S(2)}, u32[]{:S(2)}) %collective-permute-start.2) | collective-permute-done | bytes 360480 | tf_op jit(solution)/shard_map/ppermute | solution.py:37
  31.0 3.0 %multiply_select_fusion = (f32[22,30,128]{2,1,0:T(8,128)S(1)}, f32[22,30,128]{2,1,0:T(8,128)S(1)}) fusion(pred[22,30]{1,0:T(8,128)(4,1)S(1)} %broadcast_and_fusion, f32[22,30,128]{2,1,0:T(8,128)S(1)} %slice.586, f32[24,32,128]{2,1,0:T(8,128)S(1)} %get-tuple-element.10, f32[24,32,128]{2,1,0:T(8,128)S(1)} %get-tuple-element.8, f32[]{:T(128)} %bitcast.10, ...), kind=kLoop, calls=%fused_computation.51 | loop fusion | flops 1858560 | bytes 2704036 | tf_op jit(solution)/shard_map/jit(_where)/select_n | solution.py:121
  38.5 5.9 %all-to-all-start = ((bf16[8,2,128]{2,1,0:T(2,128)(2,1)}), bf16[8,2,128]{2,1,0:T(2,128)(2,1)S(1)}, u32[]{:S(2)}, u32[]{:S(2)}) async-start(bf16[8,2,128]{2,1,0:T(2,128)(2,1)} %broadcast_in_dim.343), calls=%async_computation | async-start | bytes 8192 | tf_op jit(solution)/shard_map/all_to_all | solution.py:142
  44.9 2.6 %all-to-all-done = bf16[8,2,128]{2,1,0:T(2,128)(2,1)S(1)} async-done(((bf16[8,2,128]{2,1,0:T(2,128)(2,1)}), bf16[8,2,128]{2,1,0:T(2,128)(2,1)S(1)}, u32[]{:S(2)}, u32[]{:S(2)}) %all-to-all-start) | async-done | bytes 4128 | tf_op jit(solution)/shard_map/all_to_all | solution.py:142
  50.5 1.3 %reshape.426 = f32[80]{0:T(128)} reshape(f32[2,8,5]{2,1,0:T(8,128)} %get-tuple-element.31) | data formatting | bytes 640 | tf_op jit(solution)/shard_map/reshape | solution.py:21
  51.8 1.4 %pad_maximum_fusion.21 = f32[1104]{0:T(1024)} fusion(f32[1024]{0:T(1024)} %bitcast.72, f32[80]{0:T(128)} %reshape.426), kind=kLoop, calls=%fused_computation.193 | loop fusion | flops 1104 | bytes 8832 | tf_op jit(solution)/shard_map/concatenate | solution.py:21
  53.2 3.7 %collective-permute-start.4 = (f32[1104]{0:T(1024)}, f32[1104]{0:T(1024)}, u32[]{:S(2)}, u32[]{:S(2)}) collective-permute-start(f32[1104]{0:T(1024)} %pad_maximum_fusion.21), channel_id=1, source_target_pairs={{0,1},{1,2},{2,3},{3,4},{4,5},{5,6},{6,7},{8,9},{9,10},{10,11},{11... | collective-permute-start | bytes 13256 | tf_op jit(solution)/shard_map/ppermute | solution.py:39
  57.5 1.4 %pad_maximum_fusion.22 = f32[1104]{0:T(1024)} fusion(f32[1024]{0:T(1024)} %bitcast.71, f32[80]{0:T(128)} %reshape.430), kind=kLoop, calls=%fused_computation.194 | loop fusion | flops 1104 | bytes 8832 | tf_op jit(solution)/shard_map/concatenate | solution.py:21
  58.8 1.9 %collective-permute-start.5 = (f32[1104]{0:T(1024)}, f32[1104]{0:T(1024)}, u32[]{:S(2)}, u32[]{:S(2)}) collective-permute-start(f32[1104]{0:T(1024)} %pad_maximum_fusion.22), channel_id=1, source_target_pairs={{1,0},{2,1},{3,2},{4,3},{5,4},{6,5},{7,6},{9,8},{10,9},{11,10},{12... | collective-permute-start | bytes 13256 | tf_op jit(solution)/shard_map/ppermute | solution.py:40
  61.4 1.2 %slice.627 = f32[80]{0:T(128)} slice(f32[1104]{0:T(1024)} %collective-permute-done.4), slice={[0:80]} | slice | bytes 640 | tf_op jit(solution)/shard_map/slice | solution.py:28
  63.3 2.4 %collective-permute-done.5 = f32[1104]{0:T(1024)} collective-permute-done((f32[1104]{0:T(1024)}, f32[1104]{0:T(1024)}, u32[]{:S(2)}, u32[]{:S(2)}) %collective-permute-start.5) | collective-permute-done | bytes 4448 | tf_op jit(solution)/shard_map/ppermute | solution.py:40
  65.6 1.2 %slice.630 = f32[80]{0:T(128)} slice(f32[1104]{0:T(1024)} %collective-permute-done.5), slice={[0:80]} | slice | bytes 640 | tf_op jit(solution)/shard_map/slice | solution.py:28
  66.8 1.3 %reshape.432 = f32[2,8,5]{2,1,0:T(8,128)} reshape(f32[80]{0:T(128)} %slice.630) | data formatting | bytes 640 | tf_op jit(solution)/shard_map/reshape | solution.py:28
  69.5 1.3 %reshape.433 = f32[260]{0:T(512)} reshape(f32[2,5,26]{2,1,0:T(8,128)} %get-tuple-element.29) | data formatting | bytes 2080 | tf_op jit(solution)/shard_map/reshape | solution.py:21
  70.9 1.4 %pad_maximum_fusion.19 = f32[2308]{0:T(1024)} fusion(f32[2048]{0:T(1024)} %get-tuple-element.17, f32[260]{0:T(512)} %reshape.433), kind=kLoop, calls=%fused_computation.186 | loop fusion | flops 2308 | bytes 18464 | tf_op jit(solution)/shard_map/concatenate | solution.py:21
  72.3 9.2 %collective-permute-start.6 = (f32[2308]{0:T(1024)}, f32[2308]{0:T(1024)}, u32[]{:S(2)}, u32[]{:S(2)}) collective-permute-start(f32[2308]{0:T(1024)} %pad_maximum_fusion.19), channel_id=1, source_target_pairs={{0,8},{8,16},{16,24},{24,32},{32,40},{40,48},{48,56},{56,64},{64,7... | collective-permute-start | bytes 27704 | tf_op jit(solution)/shard_map/ppermute | solution.py:39
  81.5 1.4 %reshape.436 = f32[260]{0:T(512)} reshape(f32[2,5,26]{2,1,0:T(8,128)} %get-tuple-element.30) | data formatting | bytes 2080 | tf_op jit(solution)/shard_map/reshape | solution.py:21
  82.8 1.4 %pad_maximum_fusion.20 = f32[2308]{0:T(1024)} fusion(f32[2048]{0:T(1024)} %get-tuple-element.18, f32[260]{0:T(512)} %reshape.436), kind=kLoop, calls=%fused_computation.187 | loop fusion | flops 2308 | bytes 18464 | tf_op jit(solution)/shard_map/concatenate | solution.py:21
  84.2 1.9 %collective-permute-start.7 = (f32[2308]{0:T(1024)}, f32[2308]{0:T(1024)}, u32[]{:S(2)}, u32[]{:S(2)}) collective-permute-start(f32[2308]{0:T(1024)} %pad_maximum_fusion.20), channel_id=1, source_target_pairs={{8,0},{16,8},{24,16},{32,24},{40,32},{48,40},{56,48},{64,56},{72,6... | collective-permute-start | bytes 27704 | tf_op jit(solution)/shard_map/ppermute | solution.py:40
  89.7 3.4 %collective-permute-done.7 = f32[2308]{0:T(1024)} collective-permute-done((f32[2308]{0:T(1024)}, f32[2308]{0:T(1024)}, u32[]{:S(2)}, u32[]{:S(2)}) %collective-permute-start.7) | collective-permute-done | bytes 9264 | tf_op jit(solution)/shard_map/ppermute | solution.py:40
  95.1 1.1 %select_select_fusion = f32[2,18,26,128]{3,2,1,0:T(8,128)S(1)} fusion(f32[2,18,26]{2,1,0:T(8,128)S(1)} %stack.61, f32[2,18,26]{2,1,0:T(8,128)S(1)} %get-tuple-element.4, pred[128]{0:T(512)(128)(4,1)} %get-tuple-element.41, pred[128]{0:T(512)(128)(4,1)} %get-tuple-element.42), kind=kLoop, calls=%fused_computation.20 | loop fusion | flops 239616 | bytes 486976 | tf_op jit(solution)/shard_map/jit(_where)/select_n | solution.py:181
  96.2 1.2 %fusion.7 = f32[2,16,24,128]{3,2,1,0:T(8,128)S(1)} fusion(f32[2,18,26,128]{3,2,1,0:T(8,128)S(1)} %select_select_fusion, f32[2,16,24]{2,1,0:T(8,128)S(1)} %stack.59, f32[2,16,24]{2,1,0:T(8,128)S(1)} %stack.58, pred[16,24]{1,0:T(8,128)(4,1)} %copy-done.13, pred[128]{0:T(512)(128)(4,1)} %get-tuple-element.41, pred[128]{0:T(512)(128)(4,1)} %get-tuple-element.42), kind=kLoop, calls=%fused_computation.32 | loop fusion | flops 884736 | bytes 2589312 | tf_op jit(solution)/shard_map/jit(_where)/select_n | solution.py:181
  (131 shorter events, 24.7 us)
Async XLA Ops:
  0.6 48.1 %copy-start = (bf16[1,2,8,128,128]{4,3,2,1,0:T(8,128)(2,1)S(1)}, bf16[1,2,8,128,128]{4,3,2,1,0:T(8,128)(2,1)}, u32[]{:S(2)}) copy-start(bf16[1,2,8,128,128]{4,3,2,1,0:T(8,128)(2,1)} %param.13) | copy-start | bytes 1572868
  0.6 24.4 %copy-start.6 = (s32[8,16,128]{2,1,0:T(8,128)S(1)}, s32[8,16,128]{2,1,0:T(8,128)}, u32[]{:S(2)}) copy-start(s32[8,16,128]{2,1,0:T(8,128)} %param.8) | copy-start | bytes 196612
  0.7 23.8 %copy-start.16 = (f32[4]{0:T(128)S(1)}, f32[4]{0:T(128)}, u32[]{:S(2)}) copy-start(f32[4]{0:T(128)} %param.9) | copy-start | bytes 52
  2.5 13.3 %collective-permute-start = (f32[4,8,16,128]{3,2,1,0:T(8,128)S(1)}, f32[4,8,16,128]{3,2,1,0:T(8,128)S(1)}, u32[]{:S(2)}, u32[]{:S(2)}) collective-permute-start(f32[4,8,16,128]{3,2,1,0:T(8,128)S(1)} %pad_maximum_fusion.5), channel_id=1, source_target_pairs={{8,0},{16,8},{24,16},{32,24},{40,32},{48,40},{56,48},{64,56},{72,6... | collective-permute-start | bytes 786440 | tf_op jit(solution)/shard_map/ppermute | solution.py:37
  5.1 10.7 %collective-permute-start.1 = (f32[4,8,16,128]{3,2,1,0:T(8,128)S(1)}, f32[4,8,16,128]{3,2,1,0:T(8,128)S(1)}, u32[]{:S(2)}, u32[]{:S(2)}) collective-permute-start(f32[4,8,16,128]{3,2,1,0:T(8,128)S(1)} %pad_maximum_fusion.5), channel_id=1, source_target_pairs={{0,8},{8,16},{16,24},{24,32},{32,40},{40,48},{48,56},{56,64},{64,7... | collective-permute-start | bytes 786440 | tf_op jit(solution)/shard_map/ppermute | solution.py:36
  15.5 19.2 %copy-start.13 = (pred[16,24]{1,0:T(8,128)(4,1)}, pred[16,24]{1,0:T(8,128)(4,1)S(1)}, u32[]{:S(2)}) copy-start(pred[16,24]{1,0:T(8,128)(4,1)S(1)} %broadcast_and_fusion.3) | copy-start | bytes 1156
  15.5 19.4 %copy-start.9 = (pred[14,22]{1,0:T(8,128)(4,1)}, pred[14,22]{1,0:T(8,128)(4,1)S(1)}, u32[]{:S(2)}) copy-start(pred[14,22]{1,0:T(8,128)(4,1)S(1)} %broadcast_and_fusion.4) | copy-start | bytes 928
  15.6 19.5 %copy-start.11 = (pred[12,20]{1,0:T(8,128)(4,1)}, pred[12,20]{1,0:T(8,128)(4,1)S(1)}, u32[]{:S(2)}) copy-start(pred[12,20]{1,0:T(8,128)(4,1)S(1)} %broadcast_and_fusion.5) | copy-start | bytes 724
  15.7 19.7 %copy-start.7 = (pred[10,18]{1,0:T(8,128)(4,1)}, pred[10,18]{1,0:T(8,128)(4,1)S(1)}, u32[]{:S(2)}) copy-start(pred[10,18]{1,0:T(8,128)(4,1)S(1)} %broadcast_and_fusion.6) | copy-start | bytes 544
  15.9 14.8 %copy-start.1 = (f32[3,8,16,128]{3,2,1,0:T(8,128)S(1)}, f32[3,8,16,128]{3,2,1,0:T(8,128)}, u32[]{:S(2)}) copy-start(f32[3,8,16,128]{3,2,1,0:T(8,128)} %param.7) | copy-start | bytes 589828
  15.9 11.7 %copy-start.2 = (f32[4,8,16,128]{3,2,1,0:T(8,128)}, f32[4,8,16,128]{3,2,1,0:T(8,128)S(1)}, u32[]{:S(2)}) copy-start(f32[4,8,16,128]{3,2,1,0:T(8,128)S(1)} %collective-permute-done.1) | copy-start | bytes 786436
  17.0 12.8 %collective-permute-start.2 = (f32[4,22,8,128]{3,2,1,0:T(8,128)S(1)}, f32[4,22,8,128]{3,2,1,0:T(8,128)S(1)}, u32[]{:S(2)}, u32[]{:S(2)}) collective-permute-start(f32[4,22,8,128]{3,2,1,0:T(8,128)S(1)} %get-tuple-element.12), channel_id=1, source_target_pairs={{1,0},{2,1},{3,2},{4,3},{5,4},{6,5},{7,6},{9,8},{10,9},{11,10},{12... | collective-permute-start | bytes 1081352 | tf_op jit(solution)/shard_map/ppermute | solution.py:37
  19.4 11.3 %collective-permute-start.3 = (f32[4,22,8,128]{3,2,1,0:T(8,128)S(1)}, f32[4,22,8,128]{3,2,1,0:T(8,128)S(1)}, u32[]{:S(2)}, u32[]{:S(2)}) collective-permute-start(f32[4,22,8,128]{3,2,1,0:T(8,128)S(1)} %get-tuple-element.11), channel_id=1, source_target_pairs={{0,1},{1,2},{2,3},{3,4},{4,5},{5,6},{6,7},{8,9},{9,10},{10,11},{11... | collective-permute-start | bytes 1081352 | tf_op jit(solution)/shard_map/ppermute | solution.py:36
  29.8 1.0 copy-start.3
  35.1 2.5 %copy-start.17 = (s32[2,1,128]{2,1,0:T(1,128)S(1)}, s32[2,1,128]{2,1,0:T(1,128)}, u32[]{:S(2)}) copy-start(s32[2,1,128]{2,1,0:T(1,128)} %param.11) | copy-start | bytes 3076
  37.8 0.6 copy-start.18
  38.5 9.0 %all-to-all-start = ((bf16[8,2,128]{2,1,0:T(2,128)(2,1)}), bf16[8,2,128]{2,1,0:T(2,128)(2,1)S(1)}, u32[]{:S(2)}, u32[]{:S(2)}) async-start(bf16[8,2,128]{2,1,0:T(2,128)(2,1)} %broadcast_in_dim.343), calls=%async_computation | async-start | bytes 8192 | tf_op jit(solution)/shard_map/all_to_all | solution.py:142
  53.2 8.2 %collective-permute-start.4 = (f32[1104]{0:T(1024)}, f32[1104]{0:T(1024)}, u32[]{:S(2)}, u32[]{:S(2)}) collective-permute-start(f32[1104]{0:T(1024)} %pad_maximum_fusion.21), channel_id=1, source_target_pairs={{0,1},{1,2},{2,3},{3,4},{4,5},{5,6},{6,7},{8,9},{9,10},{10,11},{11... | collective-permute-start | bytes 13256 | tf_op jit(solution)/shard_map/ppermute | solution.py:39
  58.8 6.8 %collective-permute-start.5 = (f32[1104]{0:T(1024)}, f32[1104]{0:T(1024)}, u32[]{:S(2)}, u32[]{:S(2)}) collective-permute-start(f32[1104]{0:T(1024)} %pad_maximum_fusion.22), channel_id=1, source_target_pairs={{1,0},{2,1},{3,2},{4,3},{5,4},{6,5},{7,6},{9,8},{10,9},{11,10},{12... | collective-permute-start | bytes 13256 | tf_op jit(solution)/shard_map/ppermute | solution.py:40
  72.3 16.7 %collective-permute-start.6 = (f32[2308]{0:T(1024)}, f32[2308]{0:T(1024)}, u32[]{:S(2)}, u32[]{:S(2)}) collective-permute-start(f32[2308]{0:T(1024)} %pad_maximum_fusion.19), channel_id=1, source_target_pairs={{0,8},{8,16},{16,24},{24,32},{32,40},{40,48},{48,56},{56,64},{64,7... | collective-permute-start | bytes 27704 | tf_op jit(solution)/shard_map/ppermute | solution.py:39
  84.2 8.9 %collective-permute-start.7 = (f32[2308]{0:T(1024)}, f32[2308]{0:T(1024)}, u32[]{:S(2)}, u32[]{:S(2)}) collective-permute-start(f32[2308]{0:T(1024)} %pad_maximum_fusion.20), channel_id=1, source_target_pairs={{8,0},{16,8},{24,16},{32,24},{40,32},{48,40},{56,48},{64,56},{72,6... | collective-permute-start | bytes 27704 | tf_op jit(solution)/shard_map/ppermute | solution.py:40
  95.1 2.3 %copy-start.10 = (pred[14,22]{1,0:T(8,128)(4,1)S(1)}, pred[14,22]{1,0:T(8,128)(4,1)}, u32[]{:S(2)}) copy-start(pred[14,22]{1,0:T(8,128)(4,1)} %copy-done.9) | copy-start | bytes 928
  95.1 2.3 %copy-start.14 = (pred[128]{0:T(512)(128)(4,1)S(1)}, pred[128]{0:T(512)(128)(4,1)}, u32[]{:S(2)}) copy-start(pred[128]{0:T(512)(128)(4,1)} %get-tuple-element.41) | copy-start | bytes 388
  95.1 2.3 %copy-start.15 = (pred[128]{0:T(512)(128)(4,1)S(1)}, pred[128]{0:T(512)(128)(4,1)}, u32[]{:S(2)}) copy-start(pred[128]{0:T(512)(128)(4,1)} %get-tuple-element.42) | copy-start | bytes 388
  97.5 0.7 copy-start.12
  97.5 1.1 %copy-start.8 = (pred[10,18]{1,0:T(8,128)(4,1)S(1)}, pred[10,18]{1,0:T(8,128)(4,1)}, u32[]{:S(2)}) copy-start(pred[10,18]{1,0:T(8,128)(4,1)} %copy-done.7) | copy-start | bytes 544
  98.6 2.7 %copy-start.4 = (f32[4,8,16,128]{3,2,1,0:T(8,128)S(1)}, f32[4,8,16,128]{3,2,1,0:T(8,128)}, u32[]{:S(2)}) copy-start(f32[4,8,16,128]{3,2,1,0:T(8,128)} %copy-done.2) | copy-start | bytes 786436
  98.6 2.6 %copy-start.5 = (f32[3,10,18,128]{3,2,1,0:T(8,128)S(1)}, f32[3,10,18,128]{3,2,1,0:T(8,128)}, u32[]{:S(2)}) copy-start(f32[3,10,18,128]{3,2,1,0:T(8,128)} %slice.577) | copy-start | bytes 829444

commit v6 on v5

--- a/solution.py
+++ b/solution.py
@@ -41,7 +41,7 @@
     return _unpack(from_prev, to_next), _unpack(from_next, to_prev)
 
 
-def widen(block, hx, hy, dx, dy, trim=0):
+def widen(block, hx, hy, dx, dy):
     size_x = block.shape[dx]
     (lo,), (hi,) = swap(
         "gx",
@@ -50,16 +50,12 @@
     )
     block = jnp.concatenate([lo, block, hi], axis=dx)
     size_y = block.shape[dy]
-    width = block.shape[dx]
-    inner = lax.slice_in_dim(block, trim, width - trim, axis=dx)
     (lo,), (hi,) = swap(
         "gy",
-        [lax.slice_in_dim(inner, size_y - hy, size_y, axis=dy)],
-        [lax.slice_in_dim(inner, 0, hy, axis=dy)],
-    )
-    pad = [(0, 0)] * block.ndim
-    pad[dx] = (trim, trim)
-    return jnp.concatenate([jnp.pad(lo, pad), block, jnp.pad(hi, pad)], axis=dy)
+        [lax.slice_in_dim(block, size_y - hy, size_y, axis=dy)],
+        [lax.slice_in_dim(block, 0, hy, axis=dy)],
+    )
+    return jnp.concatenate([lo, block, hi], axis=dy)
 
 
 def zpad(a):
@@ -99,7 +95,7 @@
 
     halo = SWEEPS
     data = jnp.concatenate([magnet, grain_ids.astype(jnp.float32)[None]], axis=0)
-    wide = widen(data, halo, halo, 1, 2, trim=1)
+    wide = widen(data, halo, halo, 1, 2)
     m0, m1, m2 = wide[0], wide[1], wide[2]
     exch_coef = lookup(grain_ids, exch_table)
 

time: 104 us -> 81.6 us (0.78); the launches traced: 102 us -> 81.1 us
  local copies, waits for them, and re-layouts: 22.5 us -> 6.74 us
  other arithmetic: 27.6 us -> 16.7 us
  waiting for transfers between devices: 11.4 us -> 16.5 us
    concatenate x4, other arithmetic: 5.46 us -> 0.3 us  [_pack(): return jnp.concatenate([a.reshape(-1) for a in arrays])]
    slice x6, local copies, waits for them, and re-layouts: 5.29 us -> 0.15 us  [_unpack(): out.append(flat[start:start + a.size].reshape(a.shape))]
    reshape x5, local copies, waits for them, and re-layouts: 5.21 us -> 0.35 us  [_pack(): return jnp.concatenate([a.reshape(-1) for a in arrays])]
    ppermute x2, waiting for transfers between devices: 5.75 us -> 10.1 us  [swap(): from_next = lax.ppermute(_pack(to_prev), axis, _pairs(count, -1))]
    reshape x6, local copies, waits for them, and re-layouts: 3.76 us -> 0.47 us  [_unpack(): out.append(flat[start:start + a.size].reshape(a.shape))]
    select_n x5, other arithmetic: 3.5 us -> 2.14 us  [reset(): return jnp.where(bottom, lower, jnp.where(top, upper, values))]
  transfers between devices with their start and end apart: 9 -> 9, of which waited for: 5 -> 5; matrix products, arithmetic and copies ran while one was open for 18% -> 10% of each run, Pallas kernels for 0% -> 0%
where the time goes in v6:
time: 81.6 us; the launch traced here: 81.1 us
  starting transfers between devices  39.8 us (49%)
  other arithmetic  16.7 us (20%)
  waiting for transfers between devices  16.5 us (20%)
  local copies, waits for them, and re-layouts  6.74 us (8%)
  between operations  1.17 us (1%)
    ppermute x2, starting transfers between devices, swap(): from_prev = lax.ppermute(_pack(to_next), axis, _pairs(count, 1))  13.5 us
    ppermute x2, starting transfers between devices, swap(): from_prev = [lax.ppermute(to_next[0], axis, _pairs(count, 1))]  11.6 us
    ppermute x2, waiting for transfers between devices, swap(): from_next = lax.ppermute(_pack(to_prev), axis, _pairs(count, -1))  10.1 us
    all_to_all x1, starting transfers between devices, body(): lax.all_to_all(copies, 'gy', 0, 0, tiled=True).reshape(group * 2, NODES)  5.87 us
    ppermute x2, starting transfers between devices, swap(): from_next = [lax.ppermute(to_prev[0], axis, _pairs(count, -1))]  4.96 us
    ppermute x2, starting transfers between devices, swap(): from_next = lax.ppermute(_pack(to_prev), axis, _pairs(count, -1))  3.83 us
    all_to_all x1, waiting for transfers between devices, body(): lax.all_to_all(copies, 'gy', 0, 0, tiled=True).reshape(group * 2, NODES)  3.16 us
    select_n x1, other arithmetic, body(): scalar = jnp.where(inside(hs), source / DIAG, 0.0)  2.92 us
  transfers between devices with their start and end apart: 9, of which 5 were waited for; matrix products, arithmetic and copies ran while one was open for 10% of the time, Pallas kernels for 0%

profile of v6, /device:TPU:125, one launch (start us, length us, event | category | flops | bytes accessed | tf_op | source)
XLA Modules:
  0.0 81.1 jit_solution(17668336940106286162)
XLA Ops:
  0.6 0.9 %convert_bitcast_fusion = f32[1,8,16,128]{3,2,1,0:T(8,128)S(1)} fusion(s32[8,16,128]{2,1,0:T(8,128)} %param.8), kind=kLoop, calls=%fused_computation.180 | loop fusion | flops 16384 | bytes 131072 | tf_op jit(solution)/shard_map/broadcast_in_dim | solution.py:97
  1.5 0.9 %pad_maximum_fusion.2 = f32[4,8,16,128]{3,2,1,0:T(8,128)S(1)} fusion(f32[1,8,16,128]{3,2,1,0:T(8,128)S(1)} %convert_bitcast_fusion, f32[3,8,16,128]{3,2,1,0:T(8,128)} %param.7), kind=kLoop, calls=%fused_computation.89 | loop fusion | flops 65536 | bytes 524288 | tf_op jit(solution)/shard_map/concatenate | solution.py:97
  2.5 2.6 %collective-permute-start = (f32[4,8,16,128]{3,2,1,0:T(8,128)S(1)}, f32[4,8,16,128]{3,2,1,0:T(8,128)S(1)}, u32[]{:S(2)}, u32[]{:S(2)}) collective-permute-start(f32[4,8,16,128]{3,2,1,0:T(8,128)S(1)} %pad_maximum_fusion.2), channel_id=1, source_target_pairs={{8,0},{16,8},{24,16},{32,24},{40,32},{48,40},{56,48},{64,56},{72,6... | collective-permute-start | bytes 786440 | tf_op jit(solution)/shard_map/ppermute | solution.py:37
  5.1 6.6 %collective-permute-start.1 = (f32[4,8,16,128]{3,2,1,0:T(8,128)S(1)}, f32[4,8,16,128]{3,2,1,0:T(8,128)S(1)}, u32[]{:S(2)}, u32[]{:S(2)}) collective-permute-start(f32[4,8,16,128]{3,2,1,0:T(8,128)S(1)} %pad_maximum_fusion.2), channel_id=1, source_target_pairs={{0,8},{8,16},{16,24},{24,32},{32,40},{40,48},{48,56},{56,64},{64,7... | collective-permute-start | bytes 786440 | tf_op jit(solution)/shard_map/ppermute | solution.py:36
  11.7 0.7 compare_select_fusion
  12.4 0.7 and_bitcast_fusion
  13.1 1.4 %fusion.94 = (f32[1]{0:T(128)}, f32[1]{0:T(128)}, f32[1]{0:T(128)}, f32[1]{0:T(128)}) fusion(f32[4]{0:T(128)} %param.10), kind=kLoop, calls=%fused_computation.234 | loop fusion | bytes 32 | tf_op jit(solution)/shard_map/slice | solution.py:76
  15.3 1.0 %pad_maximum_fusion.1 = f32[4,24,16,128]{3,2,1,0:T(8,128)S(1)} fusion(f32[4,8,16,128]{3,2,1,0:T(8,128)S(1)} %collective-permute-done, f32[1,8,16,128]{3,2,1,0:T(8,128)S(1)} %convert_bitcast_fusion, f32[3,8,16,128]{3,2,1,0:T(8,128)} %param.7, f32[4,8,16,128]{3,2,1,0:T(8,128)S(1)} %collective-permute-done.1), kind=kLoop, calls=%fused_computation.14 | loop fusion | flops 589824 | bytes 1572864 | tf_op jit(solution)/shard_map/concatenate | solution.py:51
  16.4 2.4 %collective-permute-start.2 = (f32[4,24,8,128]{3,2,1,0:T(8,128)S(1)}, f32[4,24,8,128]{3,2,1,0:T(8,128)S(1)}, u32[]{:S(2)}, u32[]{:S(2)}) collective-permute-start(f32[4,24,8,128]{3,2,1,0:T(8,128)S(1)} %get-tuple-element.12), channel_id=1, source_target_pairs={{1,0},{2,1},{3,2},{4,3},{5,4},{6,5},{7,6},{9,8},{10,9},{11,10},{12... | collective-permute-start | bytes 1179656 | tf_op jit(solution)/shard_map/ppermute | solution.py:37
  18.8 5.0 %collective-permute-start.3 = (f32[4,24,8,128]{3,2,1,0:T(8,128)S(1)}, f32[4,24,8,128]{3,2,1,0:T(8,128)S(1)}, u32[]{:S(2)}, u32[]{:S(2)}) collective-permute-start(f32[4,24,8,128]{3,2,1,0:T(8,128)S(1)} %get-tuple-element.11), channel_id=1, source_target_pairs={{0,1},{1,2},{2,3},{3,4},{4,5},{5,6},{6,7},{8,9},{9,10},{10,11},{11... | collective-permute-start | bytes 1179656 | tf_op jit(solution)/shard_map/ppermute | solution.py:36
  23.9 0.7 fusion.93
  24.6 2.6 %select_add_fusion = f32[8,16,128]{2,1,0:T(8,128)S(1)} fusion(s32[8,16,128]{2,1,0:T(8,128)S(1)} %copy-done.5, f32[]{:T(128)} %bitcast.3, f32[]{:T(128)} %bitcast.2, f32[]{:T(128)} %bitcast.1, f32[]{:T(128)} %bitcast), kind=kLoop, calls=%fused_computation.181 | loop fusion | flops 180224 | bytes 131088 | tf_op jit(solution)/shard_map/add | solution.py:76
  27.1 2.3 %collective-permute-done.2 = f32[4,24,8,128]{3,2,1,0:T(8,128)S(1)} collective-permute-done((f32[4,24,8,128]{3,2,1,0:T(8,128)S(1)}, f32[4,24,8,128]{3,2,1,0:T(8,128)S(1)}, u32[]{:S(2)}, u32[]{:S(2)}) %collective-permute-start.2) | collective-permute-done | bytes 393248 | tf_op jit(solution)/shard_map/ppermute | solution.py:37
  29.4 0.9 %collective-permute-done.3 = f32[4,24,8,128]{3,2,1,0:T(8,128)S(1)} collective-permute-done((f32[4,24,8,128]{3,2,1,0:T(8,128)S(1)}, f32[4,24,8,128]{3,2,1,0:T(8,128)S(1)}, u32[]{:S(2)}, u32[]{:S(2)}) %collective-permute-start.3) | collective-permute-done | bytes 393248 | tf_op jit(solution)/shard_map/ppermute | solution.py:36
  30.5 0.6 copy-done.2
  31.2 2.9 %multiply_select_fusion = (f32[22,30,128]{2,1,0:T(8,128)S(1)}, f32[22,30,128]{2,1,0:T(8,128)S(1)}) fusion(pred[22,30]{1,0:T(8,128)(4,1)S(1)} %broadcast_and_fusion, f32[22,30,128]{2,1,0:T(8,128)S(1)} %slice.585, f32[24,32,128]{2,1,0:T(8,128)S(1)} %get-tuple-element.10, f32[24,32,128]{2,1,0:T(8,128)S(1)} %get-tuple-element.8, f32[]{:T(128)} %bitcast.10, ...), kind=kLoop, calls=%fused_computation.48 | loop fusion | flops 1858560 | bytes 2704036 | tf_op jit(solution)/shard_map/jit(_where)/select_n | solution.py:117
  36.3 0.6 broadcast_in_dim.343
  36.9 5.9 %all-to-all-start = ((bf16[8,2,128]{2,1,0:T(2,128)(2,1)}), bf16[8,2,128]{2,1,0:T(2,128)(2,1)S(1)}, u32[]{:S(2)}, u32[]{:S(2)}) async-start(bf16[8,2,128]{2,1,0:T(2,128)(2,1)} %broadcast_in_dim.343), calls=%async_computation | async-start | bytes 8192 | tf_op jit(solution)/shard_map/all_to_all | solution.py:138
  42.7 3.2 %all-to-all-done = bf16[8,2,128]{2,1,0:T(2,128)(2,1)S(1)} async-done(((bf16[8,2,128]{2,1,0:T(2,128)(2,1)}), bf16[8,2,128]{2,1,0:T(2,128)(2,1)S(1)}, u32[]{:S(2)}, u32[]{:S(2)}) %all-to-all-start) | async-done | bytes 4128 | tf_op jit(solution)/shard_map/all_to_all | solution.py:138
  45.9 0.6 gather_fusion
  47.3 3.7 %collective-permute-start.4 = (f32[1104]{0:T(1024)S(1)}, f32[1104]{0:T(1024)S(1)}, u32[]{:S(2)}, u32[]{:S(2)}) collective-permute-start(f32[1104]{0:T(1024)S(1)} %pad_maximum_fusion.18), channel_id=1, source_target_pairs={{0,1},{1,2},{2,3},{3,4},{4,5},{5,6},{6,7},{8,9},{9,10},{10,11},{11... | collective-permute-start | bytes 13256 | tf_op jit(solution)/shard_map/ppermute | solution.py:39
  51.2 1.9 %collective-permute-start.5 = (f32[1104]{0:T(1024)S(1)}, f32[1104]{0:T(1024)S(1)}, u32[]{:S(2)}, u32[]{:S(2)}) collective-permute-start(f32[1104]{0:T(1024)S(1)} %pad_maximum_fusion.19), channel_id=1, source_target_pairs={{1,0},{2,1},{3,2},{4,3},{5,4},{6,5},{7,6},{9,8},{10,9},{11,10},{12... | collective-permute-start | bytes 13256 | tf_op jit(solution)/shard_map/ppermute | solution.py:40
  53.2 4.5 %collective-permute-done.5 = f32[1104]{0:T(1024)S(1)} collective-permute-done((f32[1104]{0:T(1024)S(1)}, f32[1104]{0:T(1024)S(1)}, u32[]{:S(2)}, u32[]{:S(2)}) %collective-permute-start.5) | collective-permute-done | bytes 4448 | tf_op jit(solution)/shard_map/ppermute | solution.py:40
  58.0 9.8 %collective-permute-start.6 = (f32[2308]{0:T(1024)S(1)}, f32[2308]{0:T(1024)S(1)}, u32[]{:S(2)}, u32[]{:S(2)}) collective-permute-start(f32[2308]{0:T(1024)S(1)} %pad_maximum_fusion.16), channel_id=1, source_target_pairs={{0,8},{8,16},{16,24},{24,32},{32,40},{40,48},{48,56},{56,64},{64,7... | collective-permute-start | bytes 27704 | tf_op jit(solution)/shard_map/ppermute | solution.py:39
  68.0 1.9 %collective-permute-start.7 = (f32[2308]{0:T(1024)S(1)}, f32[2308]{0:T(1024)S(1)}, u32[]{:S(2)}, u32[]{:S(2)}) collective-permute-start(f32[2308]{0:T(1024)S(1)} %pad_maximum_fusion.17), channel_id=1, source_target_pairs={{8,0},{16,8},{24,16},{32,24},{40,32},{48,40},{56,48},{64,56},{72,6... | collective-permute-start | bytes 27704 | tf_op jit(solution)/shard_map/ppermute | solution.py:40
  69.9 0.8 slice.576
  70.9 5.7 %collective-permute-done.7 = f32[2308]{0:T(1024)S(1)} collective-permute-done((f32[2308]{0:T(1024)S(1)}, f32[2308]{0:T(1024)S(1)}, u32[]{:S(2)}, u32[]{:S(2)}) %collective-permute-start.7) | collective-permute-done | bytes 9264 | tf_op jit(solution)/shard_map/ppermute | solution.py:40
  77.6 0.5 fusion.7
  78.1 0.5 fusion.17
  78.6 0.4 fusion.33
  79.6 0.7 fusion.85
  80.3 0.9 %fusion.49 = f32[3,8,16,128]{3,2,1,0:T(8,128)} fusion(f32[3,10,18,128]{3,2,1,0:T(8,128)S(1)} %copy-done.4, f32[4,24,8,128]{3,2,1,0:T(8,128)S(1)} %copy-done.3, f32[4,8,16,128]{3,2,1,0:T(8,128)S(1)} %collective-permute-done, f32[4,8,16,128]{3,2,1,0:T(8,128)S(1)} %collective-permute-done.1, f32[1,8,16,128]{3,2,1,0:T(8,128)S(1)} %convert_bitcast_fusion, ...), kind=kLoop, calls=%fused_computation.108 | loop fusion | flops 1130496 | bytes 2308096 | tf_op jit(solution)/shard_map/sub | solution.py:197
  (110 shorter events, 6.3 us)
Async XLA Ops:
  0.6 45.9 %copy-start = (bf16[1,2,8,128,128]{4,3,2,1,0:T(8,128)(2,1)S(1)}, bf16[1,2,8,128,128]{4,3,2,1,0:T(8,128)(2,1)}, u32[]{:S(2)}) copy-start(bf16[1,2,8,128,128]{4,3,2,1,0:T(8,128)(2,1)} %param.13) | copy-start | bytes 1572868
  2.5 12.8 %collective-permute-start = (f32[4,8,16,128]{3,2,1,0:T(8,128)S(1)}, f32[4,8,16,128]{3,2,1,0:T(8,128)S(1)}, u32[]{:S(2)}, u32[]{:S(2)}) collective-permute-start(f32[4,8,16,128]{3,2,1,0:T(8,128)S(1)} %pad_maximum_fusion.2), channel_id=1, source_target_pairs={{8,0},{16,8},{24,16},{32,24},{40,32},{48,40},{56,48},{64,56},{72,6... | collective-permute-start | bytes 786440 | tf_op jit(solution)/shard_map/ppermute | solution.py:37
  5.1 10.2 %collective-permute-start.1 = (f32[4,8,16,128]{3,2,1,0:T(8,128)S(1)}, f32[4,8,16,128]{3,2,1,0:T(8,128)S(1)}, u32[]{:S(2)}, u32[]{:S(2)}) collective-permute-start(f32[4,8,16,128]{3,2,1,0:T(8,128)S(1)} %pad_maximum_fusion.2), channel_id=1, source_target_pairs={{0,8},{8,16},{16,24},{24,32},{32,40},{40,48},{48,56},{56,64},{64,7... | collective-permute-start | bytes 786440 | tf_op jit(solution)/shard_map/ppermute | solution.py:36
  15.3 8.6 %copy-start.6 = (f32[4]{0:T(128)S(1)}, f32[4]{0:T(128)}, u32[]{:S(2)}) copy-start(f32[4]{0:T(128)} %param.9) | copy-start | bytes 52
  15.3 9.2 %copy-start.5 = (s32[8,16,128]{2,1,0:T(8,128)S(1)}, s32[8,16,128]{2,1,0:T(8,128)}, u32[]{:S(2)}) copy-start(s32[8,16,128]{2,1,0:T(8,128)} %param.8) | copy-start | bytes 196612
  15.3 15.0 %copy-start.1 = (f32[3,8,16,128]{3,2,1,0:T(8,128)S(1)}, f32[3,8,16,128]{3,2,1,0:T(8,128)}, u32[]{:S(2)}) copy-start(f32[3,8,16,128]{3,2,1,0:T(8,128)} %param.7) | copy-start | bytes 589828
  16.4 13.0 %collective-permute-start.2 = (f32[4,24,8,128]{3,2,1,0:T(8,128)S(1)}, f32[4,24,8,128]{3,2,1,0:T(8,128)S(1)}, u32[]{:S(2)}, u32[]{:S(2)}) collective-permute-start(f32[4,24,8,128]{3,2,1,0:T(8,128)S(1)} %get-tuple-element.12), channel_id=1, source_target_pairs={{1,0},{2,1},{3,2},{4,3},{5,4},{6,5},{7,6},{9,8},{10,9},{11,10},{12... | collective-permute-start | bytes 1179656 | tf_op jit(solution)/shard_map/ppermute | solution.py:37
  18.8 11.5 %collective-permute-start.3 = (f32[4,24,8,128]{3,2,1,0:T(8,128)S(1)}, f32[4,24,8,128]{3,2,1,0:T(8,128)S(1)}, u32[]{:S(2)}, u32[]{:S(2)}) collective-permute-start(f32[4,24,8,128]{3,2,1,0:T(8,128)S(1)} %get-tuple-element.11), channel_id=1, source_target_pairs={{0,1},{1,2},{2,3},{3,4},{4,5},{5,6},{6,7},{8,9},{9,10},{10,11},{11... | collective-permute-start | bytes 1179656 | tf_op jit(solution)/shard_map/ppermute | solution.py:36
  30.3 0.8 copy-start.2
  35.2 0.8 %copy-start.7 = (s32[2,1,128]{2,1,0:T(1,128)S(1)}, s32[2,1,128]{2,1,0:T(1,128)}, u32[]{:S(2)}) copy-start(s32[2,1,128]{2,1,0:T(1,128)} %param.11) | copy-start | bytes 3076
  35.4 41.3 %copy-start.8 = (pred[2]{0:T(512)(128)(4,1)S(1)}, pred[2]{0:T(512)(128)(4,1)}, u32[]{:S(2)}) copy-start(pred[2]{0:T(512)(128)(4,1)} %constant.64.clone.1) | copy-start | bytes 10
  36.9 9.0 %all-to-all-start = ((bf16[8,2,128]{2,1,0:T(2,128)(2,1)}), bf16[8,2,128]{2,1,0:T(2,128)(2,1)S(1)}, u32[]{:S(2)}, u32[]{:S(2)}) async-start(bf16[8,2,128]{2,1,0:T(2,128)(2,1)} %broadcast_in_dim.343), calls=%async_computation | async-start | bytes 8192 | tf_op jit(solution)/shard_map/all_to_all | solution.py:138
  47.3 5.8 %collective-permute-start.4 = (f32[1104]{0:T(1024)S(1)}, f32[1104]{0:T(1024)S(1)}, u32[]{:S(2)}, u32[]{:S(2)}) collective-permute-start(f32[1104]{0:T(1024)S(1)} %pad_maximum_fusion.18), channel_id=1, source_target_pairs={{0,1},{1,2},{2,3},{3,4},{4,5},{5,6},{6,7},{8,9},{9,10},{10,11},{11... | collective-permute-start | bytes 13256 | tf_op jit(solution)/shard_map/ppermute | solution.py:39
  51.2 6.5 %collective-permute-start.5 = (f32[1104]{0:T(1024)S(1)}, f32[1104]{0:T(1024)S(1)}, u32[]{:S(2)}, u32[]{:S(2)}) collective-permute-start(f32[1104]{0:T(1024)S(1)} %pad_maximum_fusion.19), channel_id=1, source_target_pairs={{1,0},{2,1},{3,2},{4,3},{5,4},{6,5},{7,6},{9,8},{10,9},{11,10},{12... | collective-permute-start | bytes 13256 | tf_op jit(solution)/shard_map/ppermute | solution.py:40
  58.0 12.8 %collective-permute-start.6 = (f32[2308]{0:T(1024)S(1)}, f32[2308]{0:T(1024)S(1)}, u32[]{:S(2)}, u32[]{:S(2)}) collective-permute-start(f32[2308]{0:T(1024)S(1)} %pad_maximum_fusion.16), channel_id=1, source_target_pairs={{0,8},{8,16},{16,24},{24,32},{32,40},{40,48},{48,56},{56,64},{64,7... | collective-permute-start | bytes 27704 | tf_op jit(solution)/shard_map/ppermute | solution.py:39
  68.0 8.6 %collective-permute-start.7 = (f32[2308]{0:T(1024)S(1)}, f32[2308]{0:T(1024)S(1)}, u32[]{:S(2)}, u32[]{:S(2)}) collective-permute-start(f32[2308]{0:T(1024)S(1)} %pad_maximum_fusion.17), channel_id=1, source_target_pairs={{8,0},{16,8},{24,16},{32,24},{40,32},{48,40},{56,48},{64,56},{72,6... | collective-permute-start | bytes 27704 | tf_op jit(solution)/shard_map/ppermute | solution.py:40
  79.0 1.2 %copy-start.3 = (f32[4,24,8,128]{3,2,1,0:T(8,128)S(1)}, f32[4,24,8,128]{3,2,1,0:T(8,128)}, u32[]{:S(2)}) copy-start(f32[4,24,8,128]{3,2,1,0:T(8,128)} %copy-done.2) | copy-start | bytes 1179652
  79.0 1.2 %copy-start.4 = (f32[3,10,18,128]{3,2,1,0:T(8,128)S(1)}, f32[3,10,18,128]{3,2,1,0:T(8,128)}, u32[]{:S(2)}) copy-start(f32[3,10,18,128]{3,2,1,0:T(8,128)} %slice.576) | copy-start | bytes 829444

commit v7 on v3

--- a/solution.py
+++ b/solution.py
@@ -93,30 +93,24 @@
         ok_y = (ys >= 0) & (ys < grid_y)
         return (ok_x[:, None] & ok_y[None, :])[:, :, None]
 
-    halo = SWEEPS
     he = EXT_SWEEPS + 1
     node_map = surface_map[:, 0, :]
     cell_ids = jnp.arange(cells_x * cells_y, dtype=jnp.int32)
     onehot = node_map[:, :, None] == cell_ids[None, None, :]
+    y_major = (cell_ids % cells_x) * cells_y + cell_ids // cells_x
+    onehot_y = node_map[:, :, None] == y_major[None, None, :]
     rows = jnp.einsum(
         "tnc,tknj->tkcj",
-        onehot.astype(near_blocks.dtype),
+        onehot_y.astype(near_blocks.dtype),
         near_blocks[0],
         preferred_element_type=jnp.float32,
-    )
-    rows = rows.reshape(rows.shape[0], rows.shape[1], cells_x, cells_y, NODES)
-    local_list = near_list[0]
-    list_f = local_list.astype(jnp.float32)
-
+    ).astype(near_blocks.dtype)
+    rows = rows.reshape(rows.shape[0], rows.shape[1], cells_y, cells_x, NODES)
+    (rows_lo,), (rows_hi,) = swap("gy", [rows[:, :, cells_y - he :]], [rows[:, :, :he]])
+
+    halo = SWEEPS
     data = jnp.concatenate([magnet, grain_ids.astype(jnp.float32)[None]], axis=0)
-    (lo,), (hi,) = swap("gx", [data[:, cells_x - halo :]], [data[:, :halo]])
-    wide_x = jnp.concatenate([lo, data, hi], axis=1)
-    (lo, rows_lo, list_lo), (hi, rows_hi, list_hi) = swap(
-        "gy",
-        [wide_x[:, :, cells_y - halo :], rows[:, :, :, cells_y - he :], list_f],
-        [wide_x[:, :, :halo], rows[:, :, :, :he], list_f],
-    )
-    wide = jnp.concatenate([lo, wide_x, hi], axis=2)
+    wide = widen(data, halo, halo, 1, 2)
     m0, m1, m2 = wide[0], wide[1], wide[2]
     exch_coef = lookup(grain_ids, exch_table)
 
@@ -149,11 +143,13 @@
     face = jnp.stack([scalar[:, :, 0], scalar[:, :, -1]])
     face_flat = face.reshape(2, cells_x * cells_y)
     panels = jnp.sum(jnp.where(onehot, face_flat[:, None, :], 0.0), axis=2)
+    local_list = near_list[0]
 
     group = lax.axis_size("gy")
     me = lax.axis_index("gy")
-    side_hi = _pack([face[:, :, cells_y - he :], scalar[:, cells_y - 1]])
-    side_lo = _pack([face[:, :, :he], scalar[:, 0]])
+    list_f = local_list.astype(jnp.float32)
+    side_hi = _pack([list_f, face[:, :, cells_y - he :], scalar[:, cells_y - 1]])
+    side_lo = _pack([list_f, face[:, :, :he], scalar[:, 0]])
     rel = jnp.arange(group, dtype=jnp.int32)[:, None] - me
     side = jnp.where(rel == 1, side_hi[None], jnp.where(rel == -1, side_lo[None], 0.0))
     chunks = jnp.concatenate(
@@ -163,9 +159,9 @@
     piece = got[:, : panels.size].reshape(group * 2, NODES).astype(jnp.bfloat16)
     from_lo = jnp.where(me > 0, got[jnp.maximum(me - 1, 0), panels.size :], 0.0)
     from_hi = jnp.where(me < group - 1, got[jnp.minimum(me + 1, group - 1), panels.size :], 0.0)
-    like = [face[:, :, :he], scalar[:, 0]]
-    face_lo, t_lo = _unpack(from_lo, like)
-    face_hi, t_hi = _unpack(from_hi, like)
+    like = [list_f, face[:, :, :he], scalar[:, 0]]
+    list_lo, face_lo, t_lo = _unpack(from_lo, like)
+    list_hi, face_hi, t_hi = _unpack(from_hi, like)
 
     def double_of(block_rows, lists, faces):
         lists = lists.astype(jnp.int32)
@@ -173,10 +169,7 @@
         picked = piece[jnp.clip(lists, 0, piece.shape[0] - 1)]
         chosen = jnp.where(valid[:, :, None], picked, jnp.zeros_like(picked))
         product = jnp.einsum(
-            "tkxyj,tkj->txy",
-            block_rows.astype(jnp.bfloat16),
-            chosen,
-            preferred_element_type=jnp.float32,
+            "tkyxj,tkj->txy", block_rows, chosen, preferred_element_type=jnp.float32
         )
         return product - 0.5 * faces
 
@@ -195,12 +188,12 @@
         [planes_y[:, :he], scalar[:1]],
     )
     planes_w = jnp.concatenate([p_lo, planes_y, p_hi], axis=1)
+    t_lo = t_lo[:, None]
+    t_hi = t_hi[:, None]
 
     column = jnp.concatenate([s_lo, scalar, s_hi], axis=0)
     row_pad = ((1, 1), (0, 0), (0, 0))
-    t_lo = jnp.pad(t_lo[:, None], row_pad)
-    t_hi = jnp.pad(t_hi[:, None], row_pad)
-    scalar_1 = jnp.concatenate([t_lo, column, t_hi], axis=1)
+    scalar_1 = jnp.concatenate([jnp.pad(t_lo, row_pad), column, jnp.pad(t_hi, row_pad)], axis=1)
 
     z_ids = jnp.arange(cells_z, dtype=jnp.int32)
     bottom = z_ids == 0

time: 106 us -> 109 us (1.028)
  the two profiles are of different devices: /device:TPU:136 before, /device:TPU:128 now
where the time goes in v7:
time: 109 us
  starting transfers between devices  32.3 us (30%)
  other arithmetic  30.8 us (28%)
  local copies, waits for them, and re-layouts  22.9 us (21%)
  waiting for transfers between devices  16.3 us (15%)
  matrix products  4.92 us (5%)
  between operations  1.27 us (1%)
    select_n x6, other arithmetic, body(): scalar = jnp.where(inside(h), value, 0.0) if h > 0 else value  12 us
    ppermute x3, starting transfers between devices, swap(): from_prev = [lax.ppermute(to_next[0], axis, _pairs(count, 1))]  11.7 us
    unnamed x31, local copies, waits for them, and re-layouts  10.3 us
    all_to_all x1, starting transfers between devices, body(): got = lax.all_to_all(chunks, 'gy', 0, 0, tiled=True)  9.79 us
    select_n x1, other arithmetic, body(): scalar = jnp.where(inside(hs), source / DIAG, 0.0)  7.77 us
    ppermute x3, starting transfers between devices, swap(): from_next = [lax.ppermute(to_prev[0], axis, _pairs(count, -1))]  6.49 us
    ppermute x1, waiting for transfers between devices, swap(): from_prev = lax.ppermute(_pack(to_next), axis, _pairs(count, 1))  6.04 us
    all_to_all x1, waiting for transfers between devices, body(): got = lax.all_to_all(chunks, 'gy', 0, 0, tiled=True)  4.8 us
  transfers between devices with their start and end apart: 9, of which 4 were waited for; matrix products, arithmetic and copies ran while one was open for 44% of the time, Pallas kernels for 0%

profile of v7, /device:TPU:128, one launch (start us, length us, event | category | flops | bytes accessed | tf_op | source)
XLA Modules:
  0.0 108.5 jit_solution(17744876468644719770)
XLA Ops:
  2.5 3.9 %collective-permute-start = (f32[4,8,16,128]{3,2,1,0:T(8,128)S(1)}, f32[4,8,16,128]{3,2,1,0:T(8,128)S(1)}, u32[]{:S(2)}, u32[]{:S(2)}) collective-permute-start(f32[4,8,16,128]{3,2,1,0:T(8,128)S(1)} %pad_maximum_fusion.2), channel_id=1, source_target_pairs={{8,0},{16,8},{24,16},{32,24},{40,32},{48,40},{56,48},{64,56},{72,6... | collective-permute-start | bytes 786440 | tf_op jit(solution)/shard_map/ppermute | solution.py:37
  6.5 1.9 %collective-permute-start.1 = (f32[4,8,16,128]{3,2,1,0:T(8,128)S(1)}, f32[4,8,16,128]{3,2,1,0:T(8,128)S(1)}, u32[]{:S(2)}, u32[]{:S(2)}) collective-permute-start(f32[4,8,16,128]{3,2,1,0:T(8,128)S(1)} %pad_maximum_fusion.2), channel_id=1, source_target_pairs={{0,8},{8,16},{16,24},{24,32},{32,40},{40,48},{48,56},{56,64},{64,7... | collective-permute-start | bytes 786440 | tf_op jit(solution)/shard_map/ppermute | solution.py:36
  8.4 1.0 fusion.12
  11.0 1.3 %collective-permute-start.5 = (bf16[2,8,5,8,128]{4,3,2,1,0:T(8,128)(2,1)}, bf16[2,8,5,8,128]{4,3,2,1,0:T(8,128)(2,1)}, u32[]{:S(2)}, u32[]{:S(2)}) collective-permute-start(bf16[2,8,5,8,128]{4,3,2,1,0:T(8,128)(2,1)} %get-tuple-element.18), channel_id=1, source_target_pairs={{1,0},{2,1},{3,2},{4,3},{5,4},{6,5},{7,6},{9,8},{10,9},{11,10},{12... | collective-permute-start | bytes 491528 | tf_op jit(solution)/shard_map/ppermute | solution.py:37
  12.3 5.2 %collective-permute-start.4 = (bf16[2,8,5,8,128]{4,3,2,1,0:T(8,128)(2,1)}, bf16[2,8,5,8,128]{4,3,2,1,0:T(8,128)(2,1)}, u32[]{:S(2)}, u32[]{:S(2)}) collective-permute-start(bf16[2,8,5,8,128]{4,3,2,1,0:T(8,128)(2,1)} %get-tuple-element.17), channel_id=1, source_target_pairs={{0,1},{1,2},{2,3},{3,4},{4,5},{5,6},{6,7},{8,9},{9,10},{10,11},{11... | collective-permute-start | bytes 491528 | tf_op jit(solution)/shard_map/ppermute | solution.py:36
  19.2 1.3 %collective-permute-start.2 = (f32[4,24,8,128]{3,2,1,0:T(8,128)S(1)}, f32[4,24,8,128]{3,2,1,0:T(8,128)S(1)}, u32[]{:S(2)}, u32[]{:S(2)}) collective-permute-start(f32[4,24,8,128]{3,2,1,0:T(8,128)S(1)} %get-tuple-element.14), channel_id=1, source_target_pairs={{1,0},{2,1},{3,2},{4,3},{5,4},{6,5},{7,6},{9,8},{10,9},{11,10},{12... | collective-permute-start | bytes 1179656 | tf_op jit(solution)/shard_map/ppermute | solution.py:37
  20.5 4.6 %collective-permute-start.3 = (f32[4,24,8,128]{3,2,1,0:T(8,128)S(1)}, f32[4,24,8,128]{3,2,1,0:T(8,128)S(1)}, u32[]{:S(2)}, u32[]{:S(2)}) collective-permute-start(f32[4,24,8,128]{3,2,1,0:T(8,128)S(1)} %get-tuple-element.13), channel_id=1, source_target_pairs={{0,1},{1,2},{2,3},{3,4},{4,5},{5,6},{6,7},{8,9},{9,10},{10,11},{11... | collective-permute-start | bytes 1179656 | tf_op jit(solution)/shard_map/ppermute | solution.py:36
  25.9 2.5 %select_add_fusion = f32[8,16,128]{2,1,0:T(8,128)S(1)} fusion(s32[8,16,128]{2,1,0:T(8,128)S(1)} %copy-done.7, f32[]{:T(128)} %bitcast.3, f32[]{:T(128)} %bitcast.2, f32[]{:T(128)} %bitcast.1, f32[]{:T(128)} %bitcast), kind=kLoop, calls=%fused_computation.178 | loop fusion | flops 180224 | bytes 131088 | tf_op jit(solution)/shard_map/add | solution.py:76
  28.4 4.3 %collective-permute-done.2 = f32[4,24,8,128]{3,2,1,0:T(8,128)S(1)} collective-permute-done((f32[4,24,8,128]{3,2,1,0:T(8,128)S(1)}, f32[4,24,8,128]{3,2,1,0:T(8,128)S(1)}, u32[]{:S(2)}, u32[]{:S(2)}) %collective-permute-start.2) | collective-permute-done | bytes 393248 | tf_op jit(solution)/shard_map/ppermute | solution.py:37
  32.7 1.2 %collective-permute-done.3 = f32[4,24,8,128]{3,2,1,0:T(8,128)S(1)} collective-permute-done((f32[4,24,8,128]{3,2,1,0:T(8,128)S(1)}, f32[4,24,8,128]{3,2,1,0:T(8,128)S(1)}, u32[]{:S(2)}, u32[]{:S(2)}) %collective-permute-start.3) | collective-permute-done | bytes 393248 | tf_op jit(solution)/shard_map/ppermute | solution.py:36
  34.6 1.1 %fusion.104 = (f32[1,24,32,128]{3,2,1,0:T(8,128)}, f32[1,24,32,128]{3,2,1,0:T(8,128)}, f32[1,24,32,128]{3,2,1,0:T(8,128)}) fusion(f32[4,24,32,128]{3,2,1,0:T(8,128)S(1)} %pad_maximum_fusion), kind=kLoop, calls=%fused_computation.268 | loop fusion | bytes 2359296 | tf_op jit(solution)/shard_map/slice | solution.py:114
  36.9 1.5 %copy.56 = f32[1,24,32,128]{2,1,3,0:T(8,128)S(1)} copy(f32[1,24,32,128]{3,2,1,0:T(8,128)} %get-tuple-element.12) | data formatting | bytes 786432
  38.5 1.6 %slice.618 = f32[22,30,128]{1,0,2:T(8,128)} slice(f32[24,32,128]{1,0,2:T(8,128)S(1)} %bitcast.112), slice={[1:23], [1:31], [0:128]} | slice | bytes 675840 | tf_op jit(solution)/shard_map/slice | solution.py:120
  40.1 1.5 %copy.55 = f32[1,24,32,128]{2,1,3,0:T(8,128)S(1)} copy(f32[1,24,32,128]{3,2,1,0:T(8,128)} %get-tuple-element.11) | data formatting | bytes 786432
  41.6 2.6 %copy.54 = f32[1,24,32,128]{2,1,3,0:T(8,128)} copy(f32[1,24,32,128]{3,2,1,0:T(8,128)} %get-tuple-element.10) | data formatting | bytes 786432
  44.3 2.7 %copy.53 = f32[1,22,30,128]{2,1,3,0:T(8,128)} copy(f32[1,22,30,128]{3,2,1,0:T(8,128)} %slice.610) | data formatting | bytes 675840
  46.9 7.8 %multiply_select_fusion = (f32[22,30,128]{1,0,2:T(8,128)S(1)}, f32[22,30,128]{1,0,2:T(8,128)S(1)}) fusion(pred[22,30]{1,0:T(8,128)(4,1)S(1)} %broadcast_and_fusion, f32[22,30,128]{1,0,2:T(8,128)} %slice.618, f32[24,32,128]{1,0,2:T(8,128)S(1)} %bitcast.110, f32[24,32,128]{1,0,2:T(8,128)} %bitcast.111, f32[]{:T(128)} %bitcast.9, f32[]{:T(128)} %bitcast.8, ...), kind=kLoop, calls=%fused_computation.27 | loop fusion | flops 1858560 | bytes 2704036 | tf_op jit(solution)/shard_map/jit(_where)/select_n | solution.py:132
  54.7 2.5 %fusion.5 = f32[20,28,128]{1,0,2:T(8,128)S(1)} fusion(f32[22,30,128]{1,0,2:T(8,128)S(1)} %get-tuple-element.9, f32[22,30,128]{1,0,2:T(8,128)S(1)} %get-tuple-element.8, pred[20,28]{1,0:T(8,128)(4,1)S(1)} %broadcast_and_fusion.1), kind=kLoop, calls=%fused_computation.13 | loop fusion | flops 573440 | bytes 9726976 | tf_op jit(solution)/shard_map/jit(_where)/select_n | solution.py:138
  57.2 2.5 %fusion.1 = f32[18,26,128]{1,0,2:T(8,128)S(1)} fusion(f32[22,30,128]{1,0,2:T(8,128)S(1)} %get-tuple-element.9, f32[20,28,128]{1,0,2:T(8,128)S(1)} %fusion.5, pred[18,26]{1,0:T(8,128)(4,1)S(1)} %broadcast_and_fusion.2), kind=kLoop, calls=%fused_computation.5 | loop fusion | flops 479232 | bytes 9679872 | tf_op jit(solution)/shard_map/jit(_where)/select_n | solution.py:138
  59.7 1.7 %fusion.17 = f32[16,24,128]{1,0,2:T(8,128)S(1)} fusion(f32[18,26,128]{1,0,2:T(8,128)S(1)} %fusion.1, f32[22,30,128]{1,0,2:T(8,128)S(1)} %get-tuple-element.9, pred[16,24]{1,0:T(8,128)(4,1)S(1)} %broadcast_and_fusion.3), kind=kLoop, calls=%fused_computation.42 | loop fusion | flops 393216 | bytes 7014400 | tf_op jit(solution)/shard_map/jit(_where)/select_n | solution.py:138
  61.5 1.9 %fusion.27 = f32[14,22,128]{1,0,2:T(8,128)S(1)} fusion(f32[22,30,128]{1,0,2:T(8,128)S(1)} %get-tuple-element.9, f32[16,24,128]{1,0,2:T(8,128)S(1)} %fusion.17, pred[14,22]{1,0:T(8,128)(4,1)S(1)} %broadcast_and_fusion.4), kind=kLoop, calls=%fused_computation.61 | loop fusion | flops 315392 | bytes 6451200 | tf_op jit(solution)/shard_map/jit(_where)/select_n | solution.py:138
  63.3 1.7 %fusion.23 = f32[12,20,128]{1,0,2:T(8,128)S(1)} fusion(f32[22,30,128]{1,0,2:T(8,128)S(1)} %get-tuple-element.9, f32[14,22,128]{1,0,2:T(8,128)S(1)} %fusion.27, pred[12,20]{1,0:T(8,128)(4,1)S(1)} %broadcast_and_fusion.5), kind=kLoop, calls=%fused_computation.53 | loop fusion | flops 245760 | bytes 6416384 | tf_op jit(solution)/shard_map/jit(_where)/select_n | solution.py:138
  65.0 1.7 %fusion.19 = f32[10,18,128]{1,0,2:T(8,128)S(1)} fusion(f32[22,30,128]{1,0,2:T(8,128)S(1)} %get-tuple-element.9, f32[12,20,128]{1,0,2:T(8,128)S(1)} %fusion.23, pred[10,18]{1,0:T(8,128)(4,1)S(1)} %broadcast_and_fusion.6), kind=kLoop, calls=%fused_computation.45 | loop fusion | flops 184320 | bytes 6385664 | tf_op jit(solution)/shard_map/jit(_where)/select_n | solution.py:138
  69.8 9.8 %all-to-all-start = ((f32[8,1,1376]{2,1,0:T(1,128)}), f32[8,1,1376]{2,1,0:T(1,128)S(1)}, u32[]{:S(2)}, u32[]{:S(2)}) async-start(f32[8,1,1376]{2,1,0:T(1,128)} %all_to_all.8), calls=%async_computation | async-start | bytes 90112 | tf_op jit(solution)/shard_map/all_to_all | solution.py:158
  79.6 1.1 slice.609
  81.0 4.8 %all-to-all-done = f32[8,1,1376]{2,1,0:T(1,128)S(1)} async-done(((f32[8,1,1376]{2,1,0:T(1,128)}), f32[8,1,1376]{2,1,0:T(1,128)S(1)}, u32[]{:S(2)}, u32[]{:S(2)}) %all-to-all-start) | async-done | bytes 44064 | tf_op jit(solution)/shard_map/all_to_all | solution.py:158
  87.1 1.3 %fusion.69 = f32[2,1,5,8,1]{3,1,4,2,0:T(1,128)S(1)} fusion(bf16[2,8,5,8,128]{4,3,2,1,0:T(8,128)(2,1)} %collective-permute-done.5, bf16[2,8,128,1,1]{2,1,0,3,4:T(8,128)(2,1)S(1)} %fusion.94), kind=kOutput, calls=%fused_computation.151 | convolution fusion | flops 163840 | bytes 168256 | tf_op jit(solution)/shard_map/tkyxj,tkj->txy/dot_general | solution.py:171
  89.2 1.2 %fusion.35 = f32[2,1,16,8,1]{3,1,4,2,0:T(1,128)S(1)} fusion(bf16[2,8,16,8,128]{4,3,2,1,0:T(8,128)(2,1)S(1)} %copy-done.6, bf16[2,8,128,1,1]{2,1,0,3,4:T(8,128)(2,1)S(1)} %fusion.95), kind=kOutput, calls=%fused_computation.90 | convolution fusion | flops 524288 | bytes 529408 | tf_op jit(solution)/shard_map/tkyxj,tkj->txy/dot_general | solution.py:171
  91.6 1.3 %fusion.71 = f32[2,1,5,8,1]{3,1,4,2,0:T(1,128)S(1)} fusion(bf16[2,8,5,8,128]{4,3,2,1,0:T(8,128)(2,1)} %collective-permute-done.4, bf16[2,8,128,1,1]{2,1,0,3,4:T(8,128)(2,1)S(1)} %fusion.96), kind=kOutput, calls=%fused_computation.153 | convolution fusion | flops 163840 | bytes 168256 | tf_op jit(solution)/shard_map/tkyxj,tkj->txy/dot_general | solution.py:171
  93.3 1.9 %collective-permute-start.7 = (f32[2308]{0:T(1024)S(1)}, f32[2308]{0:T(1024)S(1)}, u32[]{:S(2)}, u32[]{:S(2)}) collective-permute-start(f32[2308]{0:T(1024)S(1)} %pad_maximum_fusion.18), channel_id=1, source_target_pairs={{8,0},{16,8},{24,16},{32,24},{40,32},{48,40},{56,48},{64,56},{72,6... | collective-permute-start | bytes 27704 | tf_op jit(solution)/shard_map/ppermute | solution.py:40
  95.4 2.4 %collective-permute-start.6 = (f32[2308]{0:T(1024)S(1)}, f32[2308]{0:T(1024)S(1)}, u32[]{:S(2)}, u32[]{:S(2)}) collective-permute-start(f32[2308]{0:T(1024)S(1)} %pad_maximum_fusion.17), channel_id=1, source_target_pairs={{0,8},{8,16},{16,24},{24,32},{32,40},{40,48},{48,56},{56,64},{64,7... | collective-permute-start | bytes 27704 | tf_op jit(solution)/shard_map/ppermute | solution.py:39
  97.9 6.0 %collective-permute-done.6 = f32[2308]{0:T(1024)S(1)} collective-permute-done((f32[2308]{0:T(1024)S(1)}, f32[2308]{0:T(1024)S(1)}, u32[]{:S(2)}, u32[]{:S(2)}) %collective-permute-start.6) | collective-permute-done | bytes 9264 | tf_op jit(solution)/shard_map/ppermute | solution.py:39
  (161 shorter events, 19.2 us)
Async XLA Ops:
  0.6 7.8 %copy-start = (bf16[1,2,8,128,128]{4,3,2,1,0:T(8,128)(2,1)S(1)}, bf16[1,2,8,128,128]{4,3,2,1,0:T(8,128)(2,1)}, u32[]{:S(2)}) copy-start(bf16[1,2,8,128,128]{4,3,2,1,0:T(8,128)(2,1)} %param.13) | copy-start | bytes 1572868
  0.6 18.4 %copy-start.2 = (f32[3,8,16,128]{3,2,1,0:T(8,128)S(1)}, f32[3,8,16,128]{3,2,1,0:T(8,128)}, u32[]{:S(2)}) copy-start(f32[3,8,16,128]{3,2,1,0:T(8,128)} %param.7) | copy-start | bytes 589828
  0.7 16.9 %copy-start.11 = (s32[1,2,8]{2,1,0:T(2,128)S(1)}, s32[1,2,8]{2,1,0:T(2,128)}, u32[]{:S(2)}) copy-start(s32[1,2,8]{2,1,0:T(2,128)} %param.12) | copy-start | bytes 196
  0.7 16.9 %copy-start.8 = (f32[4]{0:T(128)S(1)}, f32[4]{0:T(128)}, u32[]{:S(2)}) copy-start(f32[4]{0:T(128)} %param.10) | copy-start | bytes 52
  2.5 16.5 %collective-permute-start = (f32[4,8,16,128]{3,2,1,0:T(8,128)S(1)}, f32[4,8,16,128]{3,2,1,0:T(8,128)S(1)}, u32[]{:S(2)}, u32[]{:S(2)}) collective-permute-start(f32[4,8,16,128]{3,2,1,0:T(8,128)S(1)} %pad_maximum_fusion.2), channel_id=1, source_target_pairs={{8,0},{16,8},{24,16},{32,24},{40,32},{48,40},{56,48},{64,56},{72,6... | collective-permute-start | bytes 786440 | tf_op jit(solution)/shard_map/ppermute | solution.py:37
  6.5 12.6 %collective-permute-start.1 = (f32[4,8,16,128]{3,2,1,0:T(8,128)S(1)}, f32[4,8,16,128]{3,2,1,0:T(8,128)S(1)}, u32[]{:S(2)}, u32[]{:S(2)}) collective-permute-start(f32[4,8,16,128]{3,2,1,0:T(8,128)S(1)} %pad_maximum_fusion.2), channel_id=1, source_target_pairs={{0,8},{8,16},{16,24},{24,32},{32,40},{40,48},{48,56},{56,64},{64,7... | collective-permute-start | bytes 786440 | tf_op jit(solution)/shard_map/ppermute | solution.py:36
  9.4 0.8 copy-start.5
  11.0 76.1 %collective-permute-start.5 = (bf16[2,8,5,8,128]{4,3,2,1,0:T(8,128)(2,1)}, bf16[2,8,5,8,128]{4,3,2,1,0:T(8,128)(2,1)}, u32[]{:S(2)}, u32[]{:S(2)}) collective-permute-start(bf16[2,8,5,8,128]{4,3,2,1,0:T(8,128)(2,1)} %get-tuple-element.18), channel_id=1, source_target_pairs={{1,0},{2,1},{3,2},{4,3},{5,4},{6,5},{7,6},{9,8},{10,9},{11,10},{12... | collective-permute-start | bytes 491528 | tf_op jit(solution)/shard_map/ppermute | solution.py:37
  12.3 79.3 %collective-permute-start.4 = (bf16[2,8,5,8,128]{4,3,2,1,0:T(8,128)(2,1)}, bf16[2,8,5,8,128]{4,3,2,1,0:T(8,128)(2,1)}, u32[]{:S(2)}, u32[]{:S(2)}) collective-permute-start(bf16[2,8,5,8,128]{4,3,2,1,0:T(8,128)(2,1)} %get-tuple-element.17), channel_id=1, source_target_pairs={{0,1},{1,2},{2,3},{3,4},{4,5},{5,6},{6,7},{8,9},{9,10},{10,11},{11... | collective-permute-start | bytes 491528 | tf_op jit(solution)/shard_map/ppermute | solution.py:36
  19.1 6.2 %copy-start.9 = (f32[4]{0:T(128)S(1)}, f32[4]{0:T(128)}, u32[]{:S(2)}) copy-start(f32[4]{0:T(128)} %param.9) | copy-start | bytes 52
  19.1 6.8 %copy-start.7 = (s32[8,16,128]{2,1,0:T(8,128)S(1)}, s32[8,16,128]{2,1,0:T(8,128)}, u32[]{:S(2)}) copy-start(s32[8,16,128]{2,1,0:T(8,128)} %param.8) | copy-start | bytes 196612
  19.2 13.5 %collective-permute-start.2 = (f32[4,24,8,128]{3,2,1,0:T(8,128)S(1)}, f32[4,24,8,128]{3,2,1,0:T(8,128)S(1)}, u32[]{:S(2)}, u32[]{:S(2)}) collective-permute-start(f32[4,24,8,128]{3,2,1,0:T(8,128)S(1)} %get-tuple-element.14), channel_id=1, source_target_pairs={{1,0},{2,1},{3,2},{4,3},{5,4},{6,5},{7,6},{9,8},{10,9},{11,10},{12... | collective-permute-start | bytes 1179656 | tf_op jit(solution)/shard_map/ppermute | solution.py:37
  20.5 13.4 %collective-permute-start.3 = (f32[4,24,8,128]{3,2,1,0:T(8,128)S(1)}, f32[4,24,8,128]{3,2,1,0:T(8,128)S(1)}, u32[]{:S(2)}, u32[]{:S(2)}) collective-permute-start(f32[4,24,8,128]{3,2,1,0:T(8,128)S(1)} %get-tuple-element.13), channel_id=1, source_target_pairs={{0,1},{1,2},{2,3},{3,4},{4,5},{5,6},{6,7},{8,9},{9,10},{10,11},{11... | collective-permute-start | bytes 1179656 | tf_op jit(solution)/shard_map/ppermute | solution.py:36
  33.9 0.7 copy-start.3
  34.6 1.5 %copy-start.1 = (f32[4,24,32,128]{3,2,1,0:T(8,128)}, f32[4,24,32,128]{3,2,1,0:T(8,128)S(1)}, u32[]{:S(2)}) copy-start(f32[4,24,32,128]{3,2,1,0:T(8,128)S(1)} %pad_maximum_fusion) | copy-start | bytes 4718596
  67.6 1.1 %copy-start.10 = (s32[2,1,128]{2,1,0:T(1,128)S(1)}, s32[2,1,128]{2,1,0:T(1,128)}, u32[]{:S(2)}) copy-start(s32[2,1,128]{2,1,0:T(1,128)} %param.11) | copy-start | bytes 3076
  68.3 20.9 %copy-start.6 = (bf16[2,8,16,8,128]{4,3,2,1,0:T(8,128)(2,1)S(1)}, bf16[2,8,16,8,128]{4,3,2,1,0:T(8,128)(2,1)}, u32[]{:S(2)}) copy-start(bf16[2,8,16,8,128]{4,3,2,1,0:T(8,128)(2,1)} %copy-done.5) | copy-start | bytes 1572868
  69.8 16.1 %all-to-all-start = ((f32[8,1,1376]{2,1,0:T(1,128)}), f32[8,1,1376]{2,1,0:T(1,128)S(1)}, u32[]{:S(2)}, u32[]{:S(2)}) async-start(f32[8,1,1376]{2,1,0:T(1,128)} %all_to_all.8), calls=%async_computation | async-start | bytes 90112 | tf_op jit(solution)/shard_map/all_to_all | solution.py:158
  79.6 24.4 %copy-start.12 = (pred[2]{0:T(512)(128)(4,1)S(1)}, pred[2]{0:T(512)(128)(4,1)}, u32[]{:S(2)}) copy-start(pred[2]{0:T(512)(128)(4,1)} %constant.173.clone.1) | copy-start | bytes 10
  93.3 4.6 %collective-permute-start.7 = (f32[2308]{0:T(1024)S(1)}, f32[2308]{0:T(1024)S(1)}, u32[]{:S(2)}, u32[]{:S(2)}) collective-permute-start(f32[2308]{0:T(1024)S(1)} %pad_maximum_fusion.18), channel_id=1, source_target_pairs={{8,0},{16,8},{24,16},{32,24},{40,32},{48,40},{56,48},{64,56},{72,6... | collective-permute-start | bytes 27704 | tf_op jit(solution)/shard_map/ppermute | solution.py:40
  95.4 8.6 %collective-permute-start.6 = (f32[2308]{0:T(1024)S(1)}, f32[2308]{0:T(1024)S(1)}, u32[]{:S(2)}, u32[]{:S(2)}) collective-permute-start(f32[2308]{0:T(1024)S(1)} %pad_maximum_fusion.17), channel_id=1, source_target_pairs={{0,8},{8,16},{16,24},{24,32},{32,40},{40,48},{48,56},{56,64},{64,7... | collective-permute-start | bytes 27704 | tf_op jit(solution)/shard_map/ppermute | solution.py:39
  106.4 1.2 %copy-start.4 = (f32[4,24,8,128]{3,2,1,0:T(8,128)S(1)}, f32[4,24,8,128]{3,2,1,0:T(8,128)}, u32[]{:S(2)}) copy-start(f32[4,24,8,128]{3,2,1,0:T(8,128)} %copy-done.3) | copy-start | bytes 1179652

commit v8 on v2

--- a/solution.py
+++ b/solution.py
@@ -71,9 +71,9 @@
 
 
 def lookup(grain_ids, table):
-    result = jnp.zeros(grain_ids.shape, jnp.float32)
-    for index in range(NMAT):
-        result = result + (grain_ids == index).astype(jnp.float32) * table[index]
+    result = jnp.full(grain_ids.shape, table[NMAT - 1], jnp.float32)
+    for index in range(NMAT - 2, -1, -1):
+        result = jnp.where(grain_ids == index, table[index], result)
     return result
 
 
@@ -167,17 +167,13 @@
     z_ids = jnp.arange(cells_z, dtype=jnp.int32)
     bottom = z_ids == 0
     top = z_ids == cells_z - 1
-    zero_w = jnp.zeros_like(planes_w[0])
 
     def reset(values, off, size_x, size_y):
         sub = planes_w[:, off : off + size_x, off : off + size_y]
-        zero = zero_w[off : off + size_x, off : off + size_y]
-        lower = jnp.stack([sub[0], zero])[..., None]
-        upper = jnp.stack([zero, sub[1]])[..., None]
-        return jnp.where(bottom, lower, jnp.where(top, upper, values))
+        return jnp.where(bottom, sub[0][..., None], jnp.where(top, sub[1][..., None], values))
 
     extend = reset(
-        jnp.zeros((2,) + planes_w.shape[1:] + (cells_z,), jnp.float32),
+        jnp.zeros(planes_w.shape[1:] + (cells_z,), jnp.float32),
         0,
         planes_w.shape[1],
         planes_w.shape[2],
@@ -188,7 +184,7 @@
         value = jnp.where(inside(h), near_sum(extend) / DIAG, 0.0)
         extend = reset(value, off, cells_x + 2 * h, cells_y + 2 * h)
 
-    potential_1 = scalar_1 + extend[0] + extend[1]
+    potential_1 = scalar_1 + extend
     potential = potential_1[1:-1, 1:-1]
     padded = zpad(potential_1)
     grad_x = (potential_1[2:, 1:-1] - potential_1[:-2, 1:-1]) * 0.5

time: 80.8 us -> 79.8 us (0.988)
  other arithmetic: 16.6 us -> 15.7 us
    add x2 -> x1, other arithmetic: 2.61 us -> 0.23 us  [body(): potential_1 = scalar_1 + extend]
    select_n x5, other arithmetic: 2.14 us -> 3.61 us  [the longest x1 2.52 us: lookup(): result = jnp.where(grain_ids == index, table[index], result)]
    slice x7 -> x2, local copies, waits for them, and re-layouts: 2.37 us -> 2.13 us  [lookup(): result = jnp.where(grain_ids == index, table[index], result)]
where the time goes in v8:
time: 79.8 us; the launch traced here: 79.3 us
  starting transfers between devices  38.8 us (49%)
  waiting for transfers between devices  16.6 us (21%)
  other arithmetic  15.7 us (20%)
  local copies, waits for them, and re-layouts  6.81 us (9%)
  between operations  1.09 us (1%)
    ppermute x2, starting transfers between devices, swap(): from_prev = lax.ppermute(_pack(to_next), axis, _pairs(count, 1))  12.6 us
    ppermute x2, starting transfers between devices, swap(): from_prev = [lax.ppermute(to_next[0], axis, _pairs(count, 1))]  11.6 us
    ppermute x2, waiting for transfers between devices, swap(): from_next = lax.ppermute(_pack(to_prev), axis, _pairs(count, -1))  10.1 us
    all_to_all x1, starting transfers between devices, body(): lax.all_to_all(copies, 'gy', 0, 0, tiled=True).reshape(group * 2, NODES)  5.87 us
    ppermute x2, starting transfers between devices, swap(): from_next = [lax.ppermute(to_prev[0], axis, _pairs(count, -1))]  4.96 us
    ppermute x2, starting transfers between devices, swap(): from_next = lax.ppermute(_pack(to_prev), axis, _pairs(count, -1))  3.83 us
    all_to_all x1, waiting for transfers between devices, body(): lax.all_to_all(copies, 'gy', 0, 0, tiled=True).reshape(group * 2, NODES)  3.17 us
    select_n x1, other arithmetic, body(): scalar = jnp.where(inside(hs), source / DIAG, 0.0)  2.91 us
  transfers between devices with their start and end apart: 9, of which 5 were waited for; matrix products, arithmetic and copies ran while one was open for 10% of the time, Pallas kernels for 0%

profile of v8, /device:TPU:125, one launch (start us, length us, event | category | flops | bytes accessed | tf_op | source)
XLA Modules:
  0.0 79.3 jit_solution(11778796828154569415)
XLA Ops:
  0.6 0.9 %convert_bitcast_fusion = f32[1,8,16,128]{3,2,1,0:T(8,128)S(1)} fusion(s32[8,16,128]{2,1,0:T(8,128)} %param.8), kind=kLoop, calls=%fused_computation.177 | loop fusion | flops 16384 | bytes 131072 | tf_op jit(solution)/shard_map/broadcast_in_dim | solution.py:97
  1.5 0.9 %pad_maximum_fusion.2 = f32[4,8,16,128]{3,2,1,0:T(8,128)S(1)} fusion(f32[1,8,16,128]{3,2,1,0:T(8,128)S(1)} %convert_bitcast_fusion, f32[3,8,16,128]{3,2,1,0:T(8,128)} %param.7), kind=kLoop, calls=%fused_computation.62 | loop fusion | flops 65536 | bytes 524288 | tf_op jit(solution)/shard_map/concatenate | solution.py:97
  2.5 2.6 %collective-permute-start = (f32[4,8,16,128]{3,2,1,0:T(8,128)S(1)}, f32[4,8,16,128]{3,2,1,0:T(8,128)S(1)}, u32[]{:S(2)}, u32[]{:S(2)}) collective-permute-start(f32[4,8,16,128]{3,2,1,0:T(8,128)S(1)} %pad_maximum_fusion.2), channel_id=1, source_target_pairs={{8,0},{16,8},{24,16},{32,24},{40,32},{48,40},{56,48},{64,56},{72,6... | collective-permute-start | bytes 786440 | tf_op jit(solution)/shard_map/ppermute | solution.py:37
  5.1 6.6 %collective-permute-start.1 = (f32[4,8,16,128]{3,2,1,0:T(8,128)S(1)}, f32[4,8,16,128]{3,2,1,0:T(8,128)S(1)}, u32[]{:S(2)}, u32[]{:S(2)}) collective-permute-start(f32[4,8,16,128]{3,2,1,0:T(8,128)S(1)} %pad_maximum_fusion.2), channel_id=1, source_target_pairs={{0,8},{8,16},{16,24},{24,32},{32,40},{40,48},{48,56},{56,64},{64,7... | collective-permute-start | bytes 786440 | tf_op jit(solution)/shard_map/ppermute | solution.py:36
  11.7 0.7 compare_select_fusion
  12.4 0.7 and_bitcast_fusion
  13.1 1.5 %fusion.89 = (f32[1]{0:T(128)}, f32[1]{0:T(128)}, f32[1]{0:T(128)}, f32[1]{0:T(128)}) fusion(f32[4]{0:T(128)} %param.10), kind=kLoop, calls=%fused_computation.236 | loop fusion | bytes 32 | tf_op jit(solution)/shard_map/slice | solution.py:76
  15.4 1.0 %pad_maximum_fusion.1 = f32[4,24,16,128]{3,2,1,0:T(8,128)S(1)} fusion(f32[4,8,16,128]{3,2,1,0:T(8,128)S(1)} %collective-permute-done, f32[1,8,16,128]{3,2,1,0:T(8,128)S(1)} %convert_bitcast_fusion, f32[3,8,16,128]{3,2,1,0:T(8,128)} %param.7, f32[4,8,16,128]{3,2,1,0:T(8,128)S(1)} %collective-permute-done.1), kind=kLoop, calls=%fused_computation.8 | loop fusion | flops 589824 | bytes 1572864 | tf_op jit(solution)/shard_map/concatenate | solution.py:51
  16.5 2.4 %collective-permute-start.2 = (f32[4,24,8,128]{3,2,1,0:T(8,128)S(1)}, f32[4,24,8,128]{3,2,1,0:T(8,128)S(1)}, u32[]{:S(2)}, u32[]{:S(2)}) collective-permute-start(f32[4,24,8,128]{3,2,1,0:T(8,128)S(1)} %get-tuple-element.10), channel_id=1, source_target_pairs={{1,0},{2,1},{3,2},{4,3},{5,4},{6,5},{7,6},{9,8},{10,9},{11,10},{12... | collective-permute-start | bytes 1179656 | tf_op jit(solution)/shard_map/ppermute | solution.py:37
  18.9 5.0 %collective-permute-start.3 = (f32[4,24,8,128]{3,2,1,0:T(8,128)S(1)}, f32[4,24,8,128]{3,2,1,0:T(8,128)S(1)}, u32[]{:S(2)}, u32[]{:S(2)}) collective-permute-start(f32[4,24,8,128]{3,2,1,0:T(8,128)S(1)} %get-tuple-element.9), channel_id=1, source_target_pairs={{0,1},{1,2},{2,3},{3,4},{4,5},{5,6},{6,7},{8,9},{9,10},{10,11},{11... | collective-permute-start | bytes 1179656 | tf_op jit(solution)/shard_map/ppermute | solution.py:36
  23.9 0.7 fusion.88
  24.6 2.5 %select_select_fusion.1 = f32[8,16,128]{2,1,0:T(8,128)S(1)} fusion(s32[8,16,128]{2,1,0:T(8,128)S(1)} %copy-done.5, f32[]{:T(128)} %bitcast.3, f32[]{:T(128)} %bitcast.2, f32[]{:T(128)} %bitcast.1, f32[]{:T(128)} %bitcast), kind=kLoop, calls=%fused_computation.178 | loop fusion | flops 98304 | bytes 131088 | tf_op jit(solution)/shard_map/jit(_where)/select_n | solution.py:76
  27.1 2.4 %collective-permute-done.2 = f32[4,24,8,128]{3,2,1,0:T(8,128)S(1)} collective-permute-done((f32[4,24,8,128]{3,2,1,0:T(8,128)S(1)}, f32[4,24,8,128]{3,2,1,0:T(8,128)S(1)}, u32[]{:S(2)}, u32[]{:S(2)}) %collective-permute-start.2) | collective-permute-done | bytes 393248 | tf_op jit(solution)/shard_map/ppermute | solution.py:37
  29.5 0.9 %collective-permute-done.3 = f32[4,24,8,128]{3,2,1,0:T(8,128)S(1)} collective-permute-done((f32[4,24,8,128]{3,2,1,0:T(8,128)S(1)}, f32[4,24,8,128]{3,2,1,0:T(8,128)S(1)}, u32[]{:S(2)}, u32[]{:S(2)}) %collective-permute-start.3) | collective-permute-done | bytes 393248 | tf_op jit(solution)/shard_map/ppermute | solution.py:36
  30.6 0.6 copy-done.2
  31.3 2.9 %multiply_select_fusion = (f32[22,30,128]{2,1,0:T(8,128)S(1)}, f32[22,30,128]{2,1,0:T(8,128)S(1)}) fusion(pred[22,30]{1,0:T(8,128)(4,1)S(1)} %broadcast_and_fusion, f32[22,30,128]{2,1,0:T(8,128)S(1)} %slice.579, f32[24,32,128]{2,1,0:T(8,128)S(1)} %get-tuple-element.8, f32[24,32,128]{2,1,0:T(8,128)S(1)} %get-tuple-element.6, f32[]{:T(128)} %bitcast.10, ...), kind=kLoop, calls=%fused_computation.36 | loop fusion | flops 1436160 | bytes 2704036 | tf_op jit(solution)/shard_map/jit(_where)/select_n | solution.py:117
  34.2 0.3 fusion.10
  34.6 0.3 fusion.15
  36.4 0.6 broadcast_in_dim.356
  37.0 5.9 %all-to-all-start = ((bf16[8,2,128]{2,1,0:T(2,128)(2,1)}), bf16[8,2,128]{2,1,0:T(2,128)(2,1)S(1)}, u32[]{:S(2)}, u32[]{:S(2)}) async-start(bf16[8,2,128]{2,1,0:T(2,128)(2,1)} %broadcast_in_dim.356), calls=%async_computation | async-start | bytes 8192 | tf_op jit(solution)/shard_map/all_to_all | solution.py:138
  42.8 3.2 %all-to-all-done = bf16[8,2,128]{2,1,0:T(2,128)(2,1)S(1)} async-done(((bf16[8,2,128]{2,1,0:T(2,128)(2,1)}), bf16[8,2,128]{2,1,0:T(2,128)(2,1)S(1)}, u32[]{:S(2)}, u32[]{:S(2)}) %all-to-all-start) | async-done | bytes 4128 | tf_op jit(solution)/shard_map/all_to_all | solution.py:138
  46.0 0.6 gather_fusion
  47.3 8.3 %collective-permute-start.4 = (f32[2208]{0:T(1024)S(1)}, f32[2208]{0:T(1024)S(1)}, u32[]{:S(2)}, u32[]{:S(2)}) collective-permute-start(f32[2208]{0:T(1024)S(1)} %pad_maximum_fusion.17), channel_id=1, source_target_pairs={{0,8},{8,16},{16,24},{24,32},{32,40},{40,48},{48,56},{56,64},{64,7... | collective-permute-start | bytes 26504 | tf_op jit(solution)/shard_map/ppermute | solution.py:39
  55.7 1.9 %collective-permute-start.5 = (f32[2208]{0:T(1024)S(1)}, f32[2208]{0:T(1024)S(1)}, u32[]{:S(2)}, u32[]{:S(2)}) collective-permute-start(f32[2208]{0:T(1024)S(1)} %pad_maximum_fusion.18), channel_id=1, source_target_pairs={{8,0},{16,8},{24,16},{32,24},{40,32},{48,40},{56,48},{64,56},{72,6... | collective-permute-start | bytes 26504 | tf_op jit(solution)/shard_map/ppermute | solution.py:40
  57.7 0.8 slice.570
  58.5 5.8 %collective-permute-done.5 = f32[2208]{0:T(1024)S(1)} collective-permute-done((f32[2208]{0:T(1024)S(1)}, f32[2208]{0:T(1024)S(1)}, u32[]{:S(2)}, u32[]{:S(2)}) %collective-permute-start.5) | collective-permute-done | bytes 8864 | tf_op jit(solution)/shard_map/ppermute | solution.py:40
  64.7 4.3 %collective-permute-start.6 = (f32[1204]{0:T(1024)S(1)}, f32[1204]{0:T(1024)S(1)}, u32[]{:S(2)}, u32[]{:S(2)}) collective-permute-start(f32[1204]{0:T(1024)S(1)} %pad_maximum_fusion.19), channel_id=1, source_target_pairs={{0,1},{1,2},{2,3},{3,4},{4,5},{5,6},{6,7},{8,9},{9,10},{10,11},{11... | collective-permute-start | bytes 14456 | tf_op jit(solution)/shard_map/ppermute | solution.py:39
  69.2 1.9 %collective-permute-start.7 = (f32[1204]{0:T(1024)S(1)}, f32[1204]{0:T(1024)S(1)}, u32[]{:S(2)}, u32[]{:S(2)}) collective-permute-start(f32[1204]{0:T(1024)S(1)} %pad_maximum_fusion.20), channel_id=1, source_target_pairs={{1,0},{2,1},{3,2},{4,3},{5,4},{6,5},{7,6},{9,8},{10,9},{11,10},{12... | collective-permute-start | bytes 14456 | tf_op jit(solution)/shard_map/ppermute | solution.py:40
  71.4 4.3 %collective-permute-done.7 = f32[1204]{0:T(1024)S(1)} collective-permute-done((f32[1204]{0:T(1024)S(1)}, f32[1204]{0:T(1024)S(1)}, u32[]{:S(2)}, u32[]{:S(2)}) %collective-permute-start.7) | collective-permute-done | bytes 4848 | tf_op jit(solution)/shard_map/ppermute | solution.py:40
  76.5 0.3 fusion.26
  77.7 0.7 fusion.84
  78.4 0.9 %fusion.31 = f32[3,8,16,128]{3,2,1,0:T(8,128)} fusion(f32[3,10,18,128]{3,2,1,0:T(8,128)S(1)} %copy-done.4, f32[4,24,8,128]{3,2,1,0:T(8,128)S(1)} %copy-done.3, f32[4,8,16,128]{3,2,1,0:T(8,128)S(1)} %collective-permute-done, f32[4,8,16,128]{3,2,1,0:T(8,128)S(1)} %collective-permute-done.1, f32[1,8,16,128]{3,2,1,0:T(8,128)S(1)} %convert_bitcast_fusion, ...), kind=kLoop, calls=%fused_computation.78 | loop fusion | flops 1130496 | bytes 2308096 | tf_op jit(solution)/shard_map/sub | solution.py:193
  (98 shorter events, 5.9 us)
Async XLA Ops:
  0.6 46.0 %copy-start = (bf16[1,2,8,128,128]{4,3,2,1,0:T(8,128)(2,1)S(1)}, bf16[1,2,8,128,128]{4,3,2,1,0:T(8,128)(2,1)}, u32[]{:S(2)}) copy-start(bf16[1,2,8,128,128]{4,3,2,1,0:T(8,128)(2,1)} %param.13) | copy-start | bytes 1572868
  2.5 12.9 %collective-permute-start = (f32[4,8,16,128]{3,2,1,0:T(8,128)S(1)}, f32[4,8,16,128]{3,2,1,0:T(8,128)S(1)}, u32[]{:S(2)}, u32[]{:S(2)}) collective-permute-start(f32[4,8,16,128]{3,2,1,0:T(8,128)S(1)} %pad_maximum_fusion.2), channel_id=1, source_target_pairs={{8,0},{16,8},{24,16},{32,24},{40,32},{48,40},{56,48},{64,56},{72,6... | collective-permute-start | bytes 786440 | tf_op jit(solution)/shard_map/ppermute | solution.py:37
  5.1 10.3 %collective-permute-start.1 = (f32[4,8,16,128]{3,2,1,0:T(8,128)S(1)}, f32[4,8,16,128]{3,2,1,0:T(8,128)S(1)}, u32[]{:S(2)}, u32[]{:S(2)}) collective-permute-start(f32[4,8,16,128]{3,2,1,0:T(8,128)S(1)} %pad_maximum_fusion.2), channel_id=1, source_target_pairs={{0,8},{8,16},{16,24},{24,32},{32,40},{40,48},{48,56},{56,64},{64,7... | collective-permute-start | bytes 786440 | tf_op jit(solution)/shard_map/ppermute | solution.py:36
  15.4 8.6 %copy-start.6 = (f32[4]{0:T(128)S(1)}, f32[4]{0:T(128)}, u32[]{:S(2)}) copy-start(f32[4]{0:T(128)} %param.9) | copy-start | bytes 52
  15.4 9.3 %copy-start.5 = (s32[8,16,128]{2,1,0:T(8,128)S(1)}, s32[8,16,128]{2,1,0:T(8,128)}, u32[]{:S(2)}) copy-start(s32[8,16,128]{2,1,0:T(8,128)} %param.8) | copy-start | bytes 196612
  15.4 15.1 %copy-start.1 = (f32[3,8,16,128]{3,2,1,0:T(8,128)S(1)}, f32[3,8,16,128]{3,2,1,0:T(8,128)}, u32[]{:S(2)}) copy-start(f32[3,8,16,128]{3,2,1,0:T(8,128)} %param.7) | copy-start | bytes 589828
  16.5 13.0 %collective-permute-start.2 = (f32[4,24,8,128]{3,2,1,0:T(8,128)S(1)}, f32[4,24,8,128]{3,2,1,0:T(8,128)S(1)}, u32[]{:S(2)}, u32[]{:S(2)}) collective-permute-start(f32[4,24,8,128]{3,2,1,0:T(8,128)S(1)} %get-tuple-element.10), channel_id=1, source_target_pairs={{1,0},{2,1},{3,2},{4,3},{5,4},{6,5},{7,6},{9,8},{10,9},{11,10},{12... | collective-permute-start | bytes 1179656 | tf_op jit(solution)/shard_map/ppermute | solution.py:37
  18.9 11.5 %collective-permute-start.3 = (f32[4,24,8,128]{3,2,1,0:T(8,128)S(1)}, f32[4,24,8,128]{3,2,1,0:T(8,128)S(1)}, u32[]{:S(2)}, u32[]{:S(2)}) collective-permute-start(f32[4,24,8,128]{3,2,1,0:T(8,128)S(1)} %get-tuple-element.9), channel_id=1, source_target_pairs={{0,1},{1,2},{2,3},{3,4},{4,5},{5,6},{6,7},{8,9},{9,10},{10,11},{11... | collective-permute-start | bytes 1179656 | tf_op jit(solution)/shard_map/ppermute | solution.py:36
  30.4 0.7 copy-start.2
  35.3 0.8 %copy-start.7 = (s32[2,1,128]{2,1,0:T(1,128)S(1)}, s32[2,1,128]{2,1,0:T(1,128)}, u32[]{:S(2)}) copy-start(s32[2,1,128]{2,1,0:T(1,128)} %param.11) | copy-start | bytes 3076
  37.0 9.0 %all-to-all-start = ((bf16[8,2,128]{2,1,0:T(2,128)(2,1)}), bf16[8,2,128]{2,1,0:T(2,128)(2,1)S(1)}, u32[]{:S(2)}, u32[]{:S(2)}) async-start(bf16[8,2,128]{2,1,0:T(2,128)(2,1)} %broadcast_in_dim.356), calls=%async_computation | async-start | bytes 8192 | tf_op jit(solution)/shard_map/all_to_all | solution.py:138
  47.3 11.2 %collective-permute-start.4 = (f32[2208]{0:T(1024)S(1)}, f32[2208]{0:T(1024)S(1)}, u32[]{:S(2)}, u32[]{:S(2)}) collective-permute-start(f32[2208]{0:T(1024)S(1)} %pad_maximum_fusion.17), channel_id=1, source_target_pairs={{0,8},{8,16},{16,24},{24,32},{32,40},{40,48},{48,56},{56,64},{64,7... | collective-permute-start | bytes 26504 | tf_op jit(solution)/shard_map/ppermute | solution.py:39
  55.7 8.6 %collective-permute-start.5 = (f32[2208]{0:T(1024)S(1)}, f32[2208]{0:T(1024)S(1)}, u32[]{:S(2)}, u32[]{:S(2)}) collective-permute-start(f32[2208]{0:T(1024)S(1)} %pad_maximum_fusion.18), channel_id=1, source_target_pairs={{8,0},{16,8},{24,16},{32,24},{40,32},{48,40},{56,48},{64,56},{72,6... | collective-permute-start | bytes 26504 | tf_op jit(solution)/shard_map/ppermute | solution.py:40
  64.7 6.6 %collective-permute-start.6 = (f32[1204]{0:T(1024)S(1)}, f32[1204]{0:T(1024)S(1)}, u32[]{:S(2)}, u32[]{:S(2)}) collective-permute-start(f32[1204]{0:T(1024)S(1)} %pad_maximum_fusion.19), channel_id=1, source_target_pairs={{0,1},{1,2},{2,3},{3,4},{4,5},{5,6},{6,7},{8,9},{9,10},{10,11},{11... | collective-permute-start | bytes 14456 | tf_op jit(solution)/shard_map/ppermute | solution.py:39
  69.2 6.5 %collective-permute-start.7 = (f32[1204]{0:T(1024)S(1)}, f32[1204]{0:T(1024)S(1)}, u32[]{:S(2)}, u32[]{:S(2)}) collective-permute-start(f32[1204]{0:T(1024)S(1)} %pad_maximum_fusion.20), channel_id=1, source_target_pairs={{1,0},{2,1},{3,2},{4,3},{5,4},{6,5},{7,6},{9,8},{10,9},{11,10},{12... | collective-permute-start | bytes 14456 | tf_op jit(solution)/shard_map/ppermute | solution.py:40
  76.8 1.6 %copy-start.3 = (f32[4,24,8,128]{3,2,1,0:T(8,128)S(1)}, f32[4,24,8,128]{3,2,1,0:T(8,128)}, u32[]{:S(2)}) copy-start(f32[4,24,8,128]{3,2,1,0:T(8,128)} %copy-done.2) | copy-start | bytes 1179652
  76.8 1.6 %copy-start.4 = (f32[3,10,18,128]{3,2,1,0:T(8,128)S(1)}, f32[3,10,18,128]{3,2,1,0:T(8,128)}, u32[]{:S(2)}) copy-start(f32[3,10,18,128]{3,2,1,0:T(8,128)} %slice.570) | copy-start | bytes 829444

commit v9 on v8

--- a/solution.py
+++ b/solution.py
@@ -94,7 +94,12 @@
         return (ok_x[:, None] & ok_y[None, :])[:, :, None]
 
     halo = SWEEPS
-    data = jnp.concatenate([magnet, grain_ids.astype(jnp.float32)[None]], axis=0)
+    channel = lax.broadcasted_iota(jnp.int32, (magnet.shape[0] + 1,) + magnet.shape[1:], 0)
+    data = jnp.where(
+        channel == magnet.shape[0],
+        grain_ids.astype(jnp.float32)[None],
+        jnp.pad(magnet, ((0, 1), (0, 0), (0, 0), (0, 0))),
+    )
     wide = widen(data, halo, halo, 1, 2)
     m0, m1, m2 = wide[0], wide[1], wide[2]
     exch_coef = lookup(grain_ids, exch_table)

time: 79.8 us -> 78.9 us (0.989)
  other arithmetic: 15.7 us -> 14.8 us
    select_n x0 -> x1, other arithmetic: none -> 1.01 us  [body(): jnp.where(channel == magnet.shape[0], grain_ids.astype(jnp.float32)[None]...]
    concatenate x1, other arithmetic: 1.05 us -> 0.05 us  [widen(): block = jnp.concatenate([lo, block, hi], axis=dx)]
    concatenate x1 -> x0, other arithmetic: 0.94 us -> none  [body(): jnp.concatenate([magnet, grain_ids.astype(jnp.float32)[None]], axis=0)]
    broadcast_in_dim x1 -> x0, other arithmetic: 0.9 us -> none  [body(): grain_ids.astype(jnp.float32)[None]]
    convert_element_type x0 -> x1, other arithmetic: none -> 0.9 us  [body(): grain_ids.astype(jnp.float32)[None]]
  transfers between devices with their start and end apart: 9 -> 9, of which waited for: 5 -> 5; matrix products, arithmetic and copies ran while one was open for 10% -> 11% of each run, Pallas kernels for 0% -> 0%
where the time goes in v9:
time: 78.9 us; the launch traced here: 78.4 us
  starting transfers between devices  39 us (49%)
  waiting for transfers between devices  16.5 us (21%)
  other arithmetic  14.8 us (19%)
  local copies, waits for them, and re-layouts  6.81 us (9%)
  between operations  1.1 us (1%)
    ppermute x2, starting transfers between devices, swap(): from_prev = lax.ppermute(_pack(to_next), axis, _pairs(count, 1))  12.7 us
    ppermute x2, starting transfers between devices, swap(): from_prev = [lax.ppermute(to_next[0], axis, _pairs(count, 1))]  11.6 us
    ppermute x2, waiting for transfers between devices, swap(): from_next = lax.ppermute(_pack(to_prev), axis, _pairs(count, -1))  10.1 us
    all_to_all x1, starting transfers between devices, body(): lax.all_to_all(copies, 'gy', 0, 0, tiled=True).reshape(group * 2, NODES)  5.87 us
    ppermute x2, starting transfers between devices, swap(): from_next = [lax.ppermute(to_prev[0], axis, _pairs(count, -1))]  4.96 us
    ppermute x2, starting transfers between devices, swap(): from_next = lax.ppermute(_pack(to_prev), axis, _pairs(count, -1))  3.83 us
    all_to_all x1, waiting for transfers between devices, body(): lax.all_to_all(copies, 'gy', 0, 0, tiled=True).reshape(group * 2, NODES)  3.17 us
    select_n x1, other arithmetic, body(): scalar = jnp.where(inside(hs), source / DIAG, 0.0)  2.91 us
  transfers between devices with their start and end apart: 9, of which 5 were waited for; matrix products, arithmetic and copies ran while one was open for 11% of the time, Pallas kernels for 0%

profile of v9, /device:TPU:125, one launch (start us, length us, event | category | flops | bytes accessed | tf_op | source)
XLA Modules:
  0.0 78.4 jit_solution(14349182217575695148)
XLA Ops:
  0.7 0.9 %convert_element_type.41 = f32[8,16,128]{2,1,0:T(8,128)S(1)} convert(s32[8,16,128]{2,1,0:T(8,128)} %param.8) | non-fusion elementwise | flops 16384 | bytes 131072 | tf_op jit(solution)/shard_map/convert_element_type | solution.py:100
  1.6 1.0 %pad_select_fusion = f32[4,8,16,128]{3,2,1,0:T(8,128)S(1)} fusion(f32[3,8,16,128]{3,2,1,0:T(8,128)} %param.7, f32[8,16,128]{2,1,0:T(8,128)S(1)} %convert_element_type.41, pred[4]{0:T(512)(128)(4,1)S(1)} %iota_compare_fusion.5), kind=kLoop, calls=%fused_computation.62 | loop fusion | flops 65536 | bytes 524292 | tf_op jit(solution)/shard_map/jit(_where)/select_n | solution.py:98
  2.6 2.6 %collective-permute-start = (f32[4,8,16,128]{3,2,1,0:T(8,128)S(1)}, f32[4,8,16,128]{3,2,1,0:T(8,128)S(1)}, u32[]{:S(2)}, u32[]{:S(2)}) collective-permute-start(f32[4,8,16,128]{3,2,1,0:T(8,128)S(1)} %pad_select_fusion), channel_id=1, source_target_pairs={{8,0},{16,8},{24,16},{32,24},{40,32},{48,40},{56,48},{64,56},{72,6... | collective-permute-start | bytes 786440 | tf_op jit(solution)/shard_map/ppermute | solution.py:37
  5.2 6.6 %collective-permute-start.1 = (f32[4,8,16,128]{3,2,1,0:T(8,128)S(1)}, f32[4,8,16,128]{3,2,1,0:T(8,128)S(1)}, u32[]{:S(2)}, u32[]{:S(2)}) collective-permute-start(f32[4,8,16,128]{3,2,1,0:T(8,128)S(1)} %pad_select_fusion), channel_id=1, source_target_pairs={{0,8},{8,16},{16,24},{24,32},{32,40},{40,48},{48,56},{56,64},{64,7... | collective-permute-start | bytes 786440 | tf_op jit(solution)/shard_map/ppermute | solution.py:36
  11.8 0.7 compare_select_fusion
  12.5 0.7 and_bitcast_fusion
  13.2 1.5 %fusion.89 = (f32[1]{0:T(128)}, f32[1]{0:T(128)}, f32[1]{0:T(128)}, f32[1]{0:T(128)}) fusion(f32[4]{0:T(128)} %param.10), kind=kLoop, calls=%fused_computation.232 | loop fusion | bytes 32 | tf_op jit(solution)/shard_map/slice | solution.py:76
  15.6 2.4 %collective-permute-start.2 = (f32[4,24,8,128]{3,2,1,0:T(8,128)S(1)}, f32[4,24,8,128]{3,2,1,0:T(8,128)S(1)}, u32[]{:S(2)}, u32[]{:S(2)}) collective-permute-start(f32[4,24,8,128]{3,2,1,0:T(8,128)S(1)} %get-tuple-element.10), channel_id=1, source_target_pairs={{1,0},{2,1},{3,2},{4,3},{5,4},{6,5},{7,6},{9,8},{10,9},{11,10},{12... | collective-permute-start | bytes 1179656 | tf_op jit(solution)/shard_map/ppermute | solution.py:37
  18.0 5.0 %collective-permute-start.3 = (f32[4,24,8,128]{3,2,1,0:T(8,128)S(1)}, f32[4,24,8,128]{3,2,1,0:T(8,128)S(1)}, u32[]{:S(2)}, u32[]{:S(2)}) collective-permute-start(f32[4,24,8,128]{3,2,1,0:T(8,128)S(1)} %get-tuple-element.9), channel_id=1, source_target_pairs={{0,1},{1,2},{2,3},{3,4},{4,5},{5,6},{6,7},{8,9},{9,10},{10,11},{11... | collective-permute-start | bytes 1179656 | tf_op jit(solution)/shard_map/ppermute | solution.py:36
  23.0 0.7 fusion.88
  23.7 2.5 %select_select_fusion.1 = f32[8,16,128]{2,1,0:T(8,128)S(1)} fusion(s32[8,16,128]{2,1,0:T(8,128)S(1)} %copy-done.5, f32[]{:T(128)} %bitcast.3, f32[]{:T(128)} %bitcast.2, f32[]{:T(128)} %bitcast.1, f32[]{:T(128)} %bitcast), kind=kLoop, calls=%fused_computation.173 | loop fusion | flops 98304 | bytes 131088 | tf_op jit(solution)/shard_map/jit(_where)/select_n | solution.py:76
  26.2 2.3 %collective-permute-done.2 = f32[4,24,8,128]{3,2,1,0:T(8,128)S(1)} collective-permute-done((f32[4,24,8,128]{3,2,1,0:T(8,128)S(1)}, f32[4,24,8,128]{3,2,1,0:T(8,128)S(1)}, u32[]{:S(2)}, u32[]{:S(2)}) %collective-permute-start.2) | collective-permute-done | bytes 393248 | tf_op jit(solution)/shard_map/ppermute | solution.py:37
  28.5 0.9 %collective-permute-done.3 = f32[4,24,8,128]{3,2,1,0:T(8,128)S(1)} collective-permute-done((f32[4,24,8,128]{3,2,1,0:T(8,128)S(1)}, f32[4,24,8,128]{3,2,1,0:T(8,128)S(1)}, u32[]{:S(2)}, u32[]{:S(2)}) %collective-permute-start.3) | collective-permute-done | bytes 393248 | tf_op jit(solution)/shard_map/ppermute | solution.py:36
  29.6 0.6 copy-done.1
  30.3 2.9 %multiply_select_fusion = (f32[22,30,128]{2,1,0:T(8,128)S(1)}, f32[22,30,128]{2,1,0:T(8,128)S(1)}) fusion(pred[22,30]{1,0:T(8,128)(4,1)S(1)} %broadcast_and_fusion, f32[22,30,128]{2,1,0:T(8,128)S(1)} %slice.579, f32[24,32,128]{2,1,0:T(8,128)S(1)} %get-tuple-element.8, f32[24,32,128]{2,1,0:T(8,128)S(1)} %get-tuple-element.6, f32[]{:T(128)} %bitcast.9, ...), kind=kLoop, calls=%fused_computation.36 | loop fusion | flops 1436160 | bytes 2704036 | tf_op jit(solution)/shard_map/jit(_where)/select_n | solution.py:122
  33.2 0.3 fusion.10
  33.6 0.3 fusion.15
  35.4 0.6 broadcast_in_dim.362
  36.0 5.9 %all-to-all-start = ((bf16[8,2,128]{2,1,0:T(2,128)(2,1)}), bf16[8,2,128]{2,1,0:T(2,128)(2,1)S(1)}, u32[]{:S(2)}, u32[]{:S(2)}) async-start(bf16[8,2,128]{2,1,0:T(2,128)(2,1)} %broadcast_in_dim.362), calls=%async_computation | async-start | bytes 8192 | tf_op jit(solution)/shard_map/all_to_all | solution.py:143
  41.8 3.2 %all-to-all-done = bf16[8,2,128]{2,1,0:T(2,128)(2,1)S(1)} async-done(((bf16[8,2,128]{2,1,0:T(2,128)(2,1)}), bf16[8,2,128]{2,1,0:T(2,128)(2,1)S(1)}, u32[]{:S(2)}, u32[]{:S(2)}) %all-to-all-start) | async-done | bytes 4128 | tf_op jit(solution)/shard_map/all_to_all | solution.py:143
  45.0 0.6 gather_fusion
  46.3 8.4 %collective-permute-start.4 = (f32[2208]{0:T(1024)S(1)}, f32[2208]{0:T(1024)S(1)}, u32[]{:S(2)}, u32[]{:S(2)}) collective-permute-start(f32[2208]{0:T(1024)S(1)} %pad_maximum_fusion.12), channel_id=1, source_target_pairs={{0,8},{8,16},{16,24},{24,32},{32,40},{40,48},{48,56},{56,64},{64,7... | collective-permute-start | bytes 26504 | tf_op jit(solution)/shard_map/ppermute | solution.py:39
  54.9 1.9 %collective-permute-start.5 = (f32[2208]{0:T(1024)S(1)}, f32[2208]{0:T(1024)S(1)}, u32[]{:S(2)}, u32[]{:S(2)}) collective-permute-start(f32[2208]{0:T(1024)S(1)} %pad_maximum_fusion.13), channel_id=1, source_target_pairs={{8,0},{16,8},{24,16},{32,24},{40,32},{48,40},{56,48},{64,56},{72,6... | collective-permute-start | bytes 26504 | tf_op jit(solution)/shard_map/ppermute | solution.py:40
  56.8 0.8 slice.570
  57.7 5.8 %collective-permute-done.5 = f32[2208]{0:T(1024)S(1)} collective-permute-done((f32[2208]{0:T(1024)S(1)}, f32[2208]{0:T(1024)S(1)}, u32[]{:S(2)}, u32[]{:S(2)}) %collective-permute-start.5) | collective-permute-done | bytes 8864 | tf_op jit(solution)/shard_map/ppermute | solution.py:40
  63.9 4.3 %collective-permute-start.6 = (f32[1204]{0:T(1024)S(1)}, f32[1204]{0:T(1024)S(1)}, u32[]{:S(2)}, u32[]{:S(2)}) collective-permute-start(f32[1204]{0:T(1024)S(1)} %pad_maximum_fusion.14), channel_id=1, source_target_pairs={{0,1},{1,2},{2,3},{3,4},{4,5},{5,6},{6,7},{8,9},{9,10},{10,11},{11... | collective-permute-start | bytes 14456 | tf_op jit(solution)/shard_map/ppermute | solution.py:39
  68.4 1.9 %collective-permute-start.7 = (f32[1204]{0:T(1024)S(1)}, f32[1204]{0:T(1024)S(1)}, u32[]{:S(2)}, u32[]{:S(2)}) collective-permute-start(f32[1204]{0:T(1024)S(1)} %pad_maximum_fusion.15), channel_id=1, source_target_pairs={{1,0},{2,1},{3,2},{4,3},{5,4},{6,5},{7,6},{9,8},{10,9},{11,10},{12... | collective-permute-start | bytes 14456 | tf_op jit(solution)/shard_map/ppermute | solution.py:40
  70.5 4.3 %collective-permute-done.7 = f32[1204]{0:T(1024)S(1)} collective-permute-done((f32[1204]{0:T(1024)S(1)}, f32[1204]{0:T(1024)S(1)}, u32[]{:S(2)}, u32[]{:S(2)}) %collective-permute-start.7) | collective-permute-done | bytes 4848 | tf_op jit(solution)/shard_map/ppermute | solution.py:40
  75.6 0.3 fusion.26
  76.0 0.3 fusion.45
  76.9 0.7 fusion.84
  77.6 0.9 %fusion.31 = f32[3,8,16,128]{3,2,1,0:T(8,128)} fusion(f32[3,10,18,128]{3,2,1,0:T(8,128)S(1)} %copy-done.3, f32[4,24,8,128]{3,2,1,0:T(8,128)S(1)} %copy-done.2, f32[4,8,16,128]{3,2,1,0:T(8,128)S(1)} %collective-permute-done, f32[4,8,16,128]{3,2,1,0:T(8,128)S(1)} %pad_select_fusion, f32[4,8,16,128]{3,2,1,0:T(8,128)S(1)} %collective-permute-done.1, ...), kind=kLoop, calls=%fused_computation.78 | loop fusion | flops 933888 | bytes 2504704 | tf_op jit(solution)/shard_map/sub | solution.py:198
  (99 shorter events, 5.7 us)
Async XLA Ops:
  0.6 45.0 %copy-start = (bf16[1,2,8,128,128]{4,3,2,1,0:T(8,128)(2,1)S(1)}, bf16[1,2,8,128,128]{4,3,2,1,0:T(8,128)(2,1)}, u32[]{:S(2)}) copy-start(bf16[1,2,8,128,128]{4,3,2,1,0:T(8,128)(2,1)} %param.13) | copy-start | bytes 1572868
  2.6 12.9 %collective-permute-start = (f32[4,8,16,128]{3,2,1,0:T(8,128)S(1)}, f32[4,8,16,128]{3,2,1,0:T(8,128)S(1)}, u32[]{:S(2)}, u32[]{:S(2)}) collective-permute-start(f32[4,8,16,128]{3,2,1,0:T(8,128)S(1)} %pad_select_fusion), channel_id=1, source_target_pairs={{8,0},{16,8},{24,16},{32,24},{40,32},{48,40},{56,48},{64,56},{72,6... | collective-permute-start | bytes 786440 | tf_op jit(solution)/shard_map/ppermute | solution.py:37
  5.2 10.3 %collective-permute-start.1 = (f32[4,8,16,128]{3,2,1,0:T(8,128)S(1)}, f32[4,8,16,128]{3,2,1,0:T(8,128)S(1)}, u32[]{:S(2)}, u32[]{:S(2)}) collective-permute-start(f32[4,8,16,128]{3,2,1,0:T(8,128)S(1)} %pad_select_fusion), channel_id=1, source_target_pairs={{0,8},{8,16},{16,24},{24,32},{32,40},{40,48},{48,56},{56,64},{64,7... | collective-permute-start | bytes 786440 | tf_op jit(solution)/shard_map/ppermute | solution.py:36
  15.4 7.6 %copy-start.6 = (f32[4]{0:T(128)S(1)}, f32[4]{0:T(128)}, u32[]{:S(2)}) copy-start(f32[4]{0:T(128)} %param.9) | copy-start | bytes 52
  15.4 8.2 %copy-start.5 = (s32[8,16,128]{2,1,0:T(8,128)S(1)}, s32[8,16,128]{2,1,0:T(8,128)}, u32[]{:S(2)}) copy-start(s32[8,16,128]{2,1,0:T(8,128)} %param.8) | copy-start | bytes 196612
  15.6 13.0 %collective-permute-start.2 = (f32[4,24,8,128]{3,2,1,0:T(8,128)S(1)}, f32[4,24,8,128]{3,2,1,0:T(8,128)S(1)}, u32[]{:S(2)}, u32[]{:S(2)}) collective-permute-start(f32[4,24,8,128]{3,2,1,0:T(8,128)S(1)} %get-tuple-element.10), channel_id=1, source_target_pairs={{1,0},{2,1},{3,2},{4,3},{5,4},{6,5},{7,6},{9,8},{10,9},{11,10},{12... | collective-permute-start | bytes 1179656 | tf_op jit(solution)/shard_map/ppermute | solution.py:37
  18.0 11.5 %collective-permute-start.3 = (f32[4,24,8,128]{3,2,1,0:T(8,128)S(1)}, f32[4,24,8,128]{3,2,1,0:T(8,128)S(1)}, u32[]{:S(2)}, u32[]{:S(2)}) collective-permute-start(f32[4,24,8,128]{3,2,1,0:T(8,128)S(1)} %get-tuple-element.9), channel_id=1, source_target_pairs={{0,1},{1,2},{2,3},{3,4},{4,5},{5,6},{6,7},{8,9},{9,10},{10,11},{11... | collective-permute-start | bytes 1179656 | tf_op jit(solution)/shard_map/ppermute | solution.py:36
  29.4 0.7 copy-start.1
  34.3 0.8 %copy-start.7 = (s32[2,1,128]{2,1,0:T(1,128)S(1)}, s32[2,1,128]{2,1,0:T(1,128)}, u32[]{:S(2)}) copy-start(s32[2,1,128]{2,1,0:T(1,128)} %param.11) | copy-start | bytes 3076
  36.0 9.0 %all-to-all-start = ((bf16[8,2,128]{2,1,0:T(2,128)(2,1)}), bf16[8,2,128]{2,1,0:T(2,128)(2,1)S(1)}, u32[]{:S(2)}, u32[]{:S(2)}) async-start(bf16[8,2,128]{2,1,0:T(2,128)(2,1)} %broadcast_in_dim.362), calls=%async_computation | async-start | bytes 8192 | tf_op jit(solution)/shard_map/all_to_all | solution.py:143
  46.3 11.3 %collective-permute-start.4 = (f32[2208]{0:T(1024)S(1)}, f32[2208]{0:T(1024)S(1)}, u32[]{:S(2)}, u32[]{:S(2)}) collective-permute-start(f32[2208]{0:T(1024)S(1)} %pad_maximum_fusion.12), channel_id=1, source_target_pairs={{0,8},{8,16},{16,24},{24,32},{32,40},{40,48},{48,56},{56,64},{64,7... | collective-permute-start | bytes 26504 | tf_op jit(solution)/shard_map/ppermute | solution.py:39
  54.9 8.6 %collective-permute-start.5 = (f32[2208]{0:T(1024)S(1)}, f32[2208]{0:T(1024)S(1)}, u32[]{:S(2)}, u32[]{:S(2)}) collective-permute-start(f32[2208]{0:T(1024)S(1)} %pad_maximum_fusion.13), channel_id=1, source_target_pairs={{8,0},{16,8},{24,16},{32,24},{40,32},{48,40},{56,48},{64,56},{72,6... | collective-permute-start | bytes 26504 | tf_op jit(solution)/shard_map/ppermute | solution.py:40
  63.9 6.6 %collective-permute-start.6 = (f32[1204]{0:T(1024)S(1)}, f32[1204]{0:T(1024)S(1)}, u32[]{:S(2)}, u32[]{:S(2)}) collective-permute-start(f32[1204]{0:T(1024)S(1)} %pad_maximum_fusion.14), channel_id=1, source_target_pairs={{0,1},{1,2},{2,3},{3,4},{4,5},{5,6},{6,7},{8,9},{9,10},{10,11},{11... | collective-permute-start | bytes 14456 | tf_op jit(solution)/shard_map/ppermute | solution.py:39
  68.4 6.5 %collective-permute-start.7 = (f32[1204]{0:T(1024)S(1)}, f32[1204]{0:T(1024)S(1)}, u32[]{:S(2)}, u32[]{:S(2)}) collective-permute-start(f32[1204]{0:T(1024)S(1)} %pad_maximum_fusion.15), channel_id=1, source_target_pairs={{1,0},{2,1},{3,2},{4,3},{5,4},{6,5},{7,6},{9,8},{10,9},{11,10},{12... | collective-permute-start | bytes 14456 | tf_op jit(solution)/shard_map/ppermute | solution.py:40
  75.9 1.6 %copy-start.2 = (f32[4,24,8,128]{3,2,1,0:T(8,128)S(1)}, f32[4,24,8,128]{3,2,1,0:T(8,128)}, u32[]{:S(2)}) copy-start(f32[4,24,8,128]{3,2,1,0:T(8,128)} %copy-done.1) | copy-start | bytes 1179652
  75.9 1.6 %copy-start.3 = (f32[3,10,18,128]{3,2,1,0:T(8,128)S(1)}, f32[3,10,18,128]{3,2,1,0:T(8,128)}, u32[]{:S(2)}) copy-start(f32[3,10,18,128]{3,2,1,0:T(8,128)} %slice.570) | copy-start | bytes 829444
  75.9 1.6 %copy-start.4 = (f32[3,8,16,128]{3,2,1,0:T(8,128)S(1)}, f32[3,8,16,128]{3,2,1,0:T(8,128)}, u32[]{:S(2)}) copy-start(f32[3,8,16,128]{3,2,1,0:T(8,128)} %param.7) | copy-start | bytes 589828

commit v10 on v9

--- a/solution.py
+++ b/solution.py
@@ -48,14 +48,15 @@
         [lax.slice_in_dim(block, size_x - hx, size_x, axis=dx)],
         [lax.slice_in_dim(block, 0, hx, axis=dx)],
     )
-    block = jnp.concatenate([lo, block, hi], axis=dx)
     size_y = block.shape[dy]
-    (lo,), (hi,) = swap(
+    parts = (lo, block, hi)
+    (y_lo,), (y_hi,) = swap(
         "gy",
-        [lax.slice_in_dim(block, size_y - hy, size_y, axis=dy)],
-        [lax.slice_in_dim(block, 0, hy, axis=dy)],
-    )
-    return jnp.concatenate([lo, block, hi], axis=dy)
+        [jnp.concatenate([lax.slice_in_dim(p, size_y - hy, size_y, axis=dy) for p in parts], axis=dx)],
+        [jnp.concatenate([lax.slice_in_dim(p, 0, hy, axis=dy) for p in parts], axis=dx)],
+    )
+    block = jnp.concatenate(parts, axis=dx)
+    return jnp.concatenate([y_lo, block, y_hi], axis=dy)
 
 
 def zpad(a):

time: 78.9 us -> 77.9 us (0.987)
  starting transfers between devices: 39 us -> 34.5 us
  waiting for transfers between devices: 16.5 us -> 19.7 us
    ppermute x2, starting transfers between devices: 11.6 us -> 9.08 us  [swap(): from_prev = [lax.ppermute(to_next[0], axis, _pairs(count, 1))]]
    all_to_all x1, starting transfers between devices: 5.87 us -> 3.95 us  [body(): lax.all_to_all(copies, 'gy', 0, 0, tiled=True).reshape(group * 2, NODES)]
    ppermute x2, waiting for transfers between devices: 2.33 us -> 4.17 us  [swap(): from_next = [lax.ppermute(to_prev[0], axis, _pairs(count, -1))]]
    ppermute x2, waiting for transfers between devices: 0.9 us -> 2.25 us  [swap(): from_prev = [lax.ppermute(to_next[0], axis, _pairs(count, 1))]]
where the time goes in v10:
time: 77.9 us; the launch traced here: 77.4 us
  starting transfers between devices  34.5 us (44%)
  waiting for transfers between devices  19.7 us (25%)
  other arithmetic  15 us (19%)
  local copies, waits for them, and re-layouts  6.78 us (9%)
  between operations  1.15 us (1%)
    ppermute x2, starting transfers between devices, swap(): from_prev = lax.ppermute(_pack(to_next), axis, _pairs(count, 1))  12.2 us
    ppermute x2, waiting for transfers between devices, swap(): from_next = lax.ppermute(_pack(to_prev), axis, _pairs(count, -1))  10.1 us
    ppermute x2, starting transfers between devices, swap(): from_prev = [lax.ppermute(to_next[0], axis, _pairs(count, 1))]  9.08 us
    ppermute x2, starting transfers between devices, swap(): from_next = [lax.ppermute(to_prev[0], axis, _pairs(count, -1))]  5.51 us
    ppermute x2, waiting for transfers between devices, swap(): from_next = [lax.ppermute(to_prev[0], axis, _pairs(count, -1))]  4.17 us
    all_to_all x1, starting transfers between devices, body(): lax.all_to_all(copies, 'gy', 0, 0, tiled=True).reshape(group * 2, NODES)  3.95 us
    ppermute x2, starting transfers between devices, swap(): from_next = lax.ppermute(_pack(to_prev), axis, _pairs(count, -1))  3.83 us
    all_to_all x1, waiting for transfers between devices, body(): lax.all_to_all(copies, 'gy', 0, 0, tiled=True).reshape(group * 2, NODES)  3.17 us
  transfers between devices with their start and end apart: 9, of which 5 were waited for; matrix products, arithmetic and copies ran while one was open for 11% of the time, Pallas kernels for 0%

profile of v10, /device:TPU:125, one launch (start us, length us, event | category | flops | bytes accessed | tf_op | source)
XLA Modules:
  0.0 77.4 jit_solution(7957594551627332386)
XLA Ops:
  0.7 0.9 %convert_element_type.41 = f32[8,16,128]{2,1,0:T(8,128)S(1)} convert(s32[8,16,128]{2,1,0:T(8,128)} %param.8) | non-fusion elementwise | flops 16384 | bytes 131072 | tf_op jit(solution)/shard_map/convert_element_type | solution.py:101
  1.6 1.0 %pad_select_fusion = f32[4,8,16,128]{3,2,1,0:T(8,128)S(1)} fusion(f32[3,8,16,128]{3,2,1,0:T(8,128)} %param.7, f32[8,16,128]{2,1,0:T(8,128)S(1)} %convert_element_type.41, pred[4]{0:T(512)(128)(4,1)S(1)} %iota_compare_fusion.5), kind=kLoop, calls=%fused_computation.63 | loop fusion | flops 65536 | bytes 524292 | tf_op jit(solution)/shard_map/jit(_where)/select_n | solution.py:99
  2.6 2.7 %collective-permute-start = (f32[4,8,16,128]{3,2,1,0:T(8,128)S(1)}, f32[4,8,16,128]{3,2,1,0:T(8,128)S(1)}, u32[]{:S(2)}, u32[]{:S(2)}) collective-permute-start(f32[4,8,16,128]{3,2,1,0:T(8,128)S(1)} %pad_select_fusion), channel_id=1, source_target_pairs={{8,0},{16,8},{24,16},{32,24},{40,32},{48,40},{56,48},{64,56},{72,6... | collective-permute-start | bytes 786440 | tf_op jit(solution)/shard_map/ppermute | solution.py:37
  5.3 6.6 %collective-permute-start.1 = (f32[4,8,16,128]{3,2,1,0:T(8,128)S(1)}, f32[4,8,16,128]{3,2,1,0:T(8,128)S(1)}, u32[]{:S(2)}, u32[]{:S(2)}) collective-permute-start(f32[4,8,16,128]{3,2,1,0:T(8,128)S(1)} %pad_select_fusion), channel_id=1, source_target_pairs={{0,8},{8,16},{16,24},{24,32},{32,40},{40,48},{48,56},{56,64},{64,7... | collective-permute-start | bytes 786440 | tf_op jit(solution)/shard_map/ppermute | solution.py:36
  12.2 0.7 compare_select_fusion
  13.4 0.7 and_bitcast_fusion
  14.2 1.5 %fusion.91 = (f32[1]{0:T(128)}, f32[1]{0:T(128)}, f32[1]{0:T(128)}, f32[1]{0:T(128)}) fusion(f32[4]{0:T(128)} %param.10), kind=kLoop, calls=%fused_computation.235 | loop fusion | bytes 32 | tf_op jit(solution)/shard_map/slice | solution.py:77
  15.7 2.5 %collective-permute-start.3 = (f32[4,24,8,128]{3,2,1,0:T(8,128)S(1)}, f32[4,24,8,128]{3,2,1,0:T(8,128)S(1)}, u32[]{:S(2)}, u32[]{:S(2)}) collective-permute-start(f32[4,24,8,128]{3,2,1,0:T(8,128)S(1)} %pad_maximum_fusion.2), channel_id=1, source_target_pairs={{0,1},{1,2},{2,3},{3,4},{4,5},{5,6},{6,7},{8,9},{9,10},{10,11},{11... | collective-permute-start | bytes 1179656 | tf_op jit(solution)/shard_map/ppermute | solution.py:36
  18.3 2.8 %collective-permute-start.2 = (f32[4,24,8,128]{3,2,1,0:T(8,128)S(1)}, f32[4,24,8,128]{3,2,1,0:T(8,128)S(1)}, u32[]{:S(2)}, u32[]{:S(2)}) collective-permute-start(f32[4,24,8,128]{3,2,1,0:T(8,128)S(1)} %pad_maximum_fusion.1), channel_id=1, source_target_pairs={{1,0},{2,1},{3,2},{4,3},{5,4},{6,5},{7,6},{9,8},{10,9},{11,10},{12... | collective-permute-start | bytes 1179656 | tf_op jit(solution)/shard_map/ppermute | solution.py:37
  21.1 0.7 fusion.90
  21.8 2.6 %select_select_fusion.1 = f32[8,16,128]{2,1,0:T(8,128)S(1)} fusion(s32[8,16,128]{2,1,0:T(8,128)S(1)} %copy-done.5, f32[]{:T(128)} %bitcast.3, f32[]{:T(128)} %bitcast.2, f32[]{:T(128)} %bitcast.1, f32[]{:T(128)} %bitcast), kind=kLoop, calls=%fused_computation.174 | loop fusion | flops 98304 | bytes 131088 | tf_op jit(solution)/shard_map/jit(_where)/select_n | solution.py:77
  24.4 2.3 %collective-permute-done.3 = f32[4,24,8,128]{3,2,1,0:T(8,128)S(1)} collective-permute-done((f32[4,24,8,128]{3,2,1,0:T(8,128)S(1)}, f32[4,24,8,128]{3,2,1,0:T(8,128)S(1)}, u32[]{:S(2)}, u32[]{:S(2)}) %collective-permute-start.3) | collective-permute-done | bytes 393248 | tf_op jit(solution)/shard_map/ppermute | solution.py:36
  26.7 4.2 %collective-permute-done.2 = f32[4,24,8,128]{3,2,1,0:T(8,128)S(1)} collective-permute-done((f32[4,24,8,128]{3,2,1,0:T(8,128)S(1)}, f32[4,24,8,128]{3,2,1,0:T(8,128)S(1)}, u32[]{:S(2)}, u32[]{:S(2)}) %collective-permute-start.2) | collective-permute-done | bytes 393248 | tf_op jit(solution)/shard_map/ppermute | solution.py:37
  31.0 0.6 copy-done.1
  31.7 3.0 %multiply_select_fusion = (f32[22,30,128]{2,1,0:T(8,128)S(1)}, f32[22,30,128]{2,1,0:T(8,128)S(1)}) fusion(pred[22,30]{1,0:T(8,128)(4,1)S(1)} %broadcast_and_fusion, f32[22,30,128]{2,1,0:T(8,128)S(1)} %slice.599, f32[24,32,128]{2,1,0:T(8,128)S(1)} %get-tuple-element.8, f32[24,32,128]{2,1,0:T(8,128)S(1)} %get-tuple-element.6, f32[]{:T(128)} %bitcast.9, ...), kind=kLoop, calls=%fused_computation.37 | loop fusion | flops 1436160 | bytes 2704036 | tf_op jit(solution)/shard_map/jit(_where)/select_n | solution.py:123
  34.7 0.3 fusion.10
  35.0 0.3 fusion.15
  36.8 0.6 broadcast_in_dim.362
  37.4 3.9 %all-to-all-start = ((bf16[8,2,128]{2,1,0:T(2,128)(2,1)}), bf16[8,2,128]{2,1,0:T(2,128)(2,1)S(1)}, u32[]{:S(2)}, u32[]{:S(2)}) async-start(bf16[8,2,128]{2,1,0:T(2,128)(2,1)} %broadcast_in_dim.362), calls=%async_computation | async-start | bytes 8192 | tf_op jit(solution)/shard_map/all_to_all | solution.py:144
  41.4 3.2 %all-to-all-done = bf16[8,2,128]{2,1,0:T(2,128)(2,1)S(1)} async-done(((bf16[8,2,128]{2,1,0:T(2,128)(2,1)}), bf16[8,2,128]{2,1,0:T(2,128)(2,1)S(1)}, u32[]{:S(2)}, u32[]{:S(2)}) %all-to-all-start) | async-done | bytes 4128 | tf_op jit(solution)/shard_map/all_to_all | solution.py:144
  44.5 0.6 gather_fusion
  45.9 7.9 %collective-permute-start.4 = (f32[2208]{0:T(1024)S(1)}, f32[2208]{0:T(1024)S(1)}, u32[]{:S(2)}, u32[]{:S(2)}) collective-permute-start(f32[2208]{0:T(1024)S(1)} %pad_maximum_fusion.13), channel_id=1, source_target_pairs={{0,8},{8,16},{16,24},{24,32},{32,40},{40,48},{48,56},{56,64},{64,7... | collective-permute-start | bytes 26504 | tf_op jit(solution)/shard_map/ppermute | solution.py:39
  53.9 1.9 %collective-permute-start.5 = (f32[2208]{0:T(1024)S(1)}, f32[2208]{0:T(1024)S(1)}, u32[]{:S(2)}, u32[]{:S(2)}) collective-permute-start(f32[2208]{0:T(1024)S(1)} %pad_maximum_fusion.14), channel_id=1, source_target_pairs={{8,0},{16,8},{24,16},{32,24},{40,32},{48,40},{56,48},{64,56},{72,6... | collective-permute-start | bytes 26504 | tf_op jit(solution)/shard_map/ppermute | solution.py:40
  55.8 0.8 slice.590
  56.7 5.8 %collective-permute-done.5 = f32[2208]{0:T(1024)S(1)} collective-permute-done((f32[2208]{0:T(1024)S(1)}, f32[2208]{0:T(1024)S(1)}, u32[]{:S(2)}, u32[]{:S(2)}) %collective-permute-start.5) | collective-permute-done | bytes 8864 | tf_op jit(solution)/shard_map/ppermute | solution.py:40
  62.9 4.3 %collective-permute-start.6 = (f32[1204]{0:T(1024)S(1)}, f32[1204]{0:T(1024)S(1)}, u32[]{:S(2)}, u32[]{:S(2)}) collective-permute-start(f32[1204]{0:T(1024)S(1)} %pad_maximum_fusion.15), channel_id=1, source_target_pairs={{0,1},{1,2},{2,3},{3,4},{4,5},{5,6},{6,7},{8,9},{9,10},{10,11},{11... | collective-permute-start | bytes 14456 | tf_op jit(solution)/shard_map/ppermute | solution.py:39
  67.3 1.9 %collective-permute-start.7 = (f32[1204]{0:T(1024)S(1)}, f32[1204]{0:T(1024)S(1)}, u32[]{:S(2)}, u32[]{:S(2)}) collective-permute-start(f32[1204]{0:T(1024)S(1)} %pad_maximum_fusion.16), channel_id=1, source_target_pairs={{1,0},{2,1},{3,2},{4,3},{5,4},{6,5},{7,6},{9,8},{10,9},{11,10},{12... | collective-permute-start | bytes 14456 | tf_op jit(solution)/shard_map/ppermute | solution.py:40
  69.5 4.3 %collective-permute-done.7 = f32[1204]{0:T(1024)S(1)} collective-permute-done((f32[1204]{0:T(1024)S(1)}, f32[1204]{0:T(1024)S(1)}, u32[]{:S(2)}, u32[]{:S(2)}) %collective-permute-start.7) | collective-permute-done | bytes 4848 | tf_op jit(solution)/shard_map/ppermute | solution.py:40
  74.6 0.3 fusion.26
  74.9 0.3 fusion.45
  75.9 0.7 fusion.86
  76.6 0.9 %fusion.31 = f32[3,8,16,128]{3,2,1,0:T(8,128)} fusion(f32[3,10,18,128]{3,2,1,0:T(8,128)S(1)} %copy-done.3, f32[4,24,8,128]{3,2,1,0:T(8,128)S(1)} %collective-permute-done.3, f32[4,8,16,128]{3,2,1,0:T(8,128)S(1)} %collective-permute-done, f32[4,8,16,128]{3,2,1,0:T(8,128)S(1)} %pad_select_fusion, f32[4,8,16,128]{3,2,1,0:T(8,128)S(1)} %collective-permute-done.1, ...), kind=kLoop, calls=%fused_computation.79 | loop fusion | flops 933888 | bytes 2504704 | tf_op jit(solution)/shard_map/sub | solution.py:199
  (102 shorter events, 5.7 us)
Async XLA Ops:
  0.6 44.6 %copy-start = (bf16[1,2,8,128,128]{4,3,2,1,0:T(8,128)(2,1)S(1)}, bf16[1,2,8,128,128]{4,3,2,1,0:T(8,128)(2,1)}, u32[]{:S(2)}) copy-start(bf16[1,2,8,128,128]{4,3,2,1,0:T(8,128)(2,1)} %param.13) | copy-start | bytes 1572868
  2.6 18.5 %copy-start.6 = (f32[4]{0:T(128)S(1)}, f32[4]{0:T(128)}, u32[]{:S(2)}) copy-start(f32[4]{0:T(128)} %param.9) | copy-start | bytes 52
  2.6 19.2 %copy-start.5 = (s32[8,16,128]{2,1,0:T(8,128)S(1)}, s32[8,16,128]{2,1,0:T(8,128)}, u32[]{:S(2)}) copy-start(s32[8,16,128]{2,1,0:T(8,128)} %param.8) | copy-start | bytes 196612
  2.6 13.0 %collective-permute-start = (f32[4,8,16,128]{3,2,1,0:T(8,128)S(1)}, f32[4,8,16,128]{3,2,1,0:T(8,128)S(1)}, u32[]{:S(2)}, u32[]{:S(2)}) collective-permute-start(f32[4,8,16,128]{3,2,1,0:T(8,128)S(1)} %pad_select_fusion), channel_id=1, source_target_pairs={{8,0},{16,8},{24,16},{32,24},{40,32},{48,40},{56,48},{64,56},{72,6... | collective-permute-start | bytes 786440 | tf_op jit(solution)/shard_map/ppermute | solution.py:37
  5.3 10.4 %collective-permute-start.1 = (f32[4,8,16,128]{3,2,1,0:T(8,128)S(1)}, f32[4,8,16,128]{3,2,1,0:T(8,128)S(1)}, u32[]{:S(2)}, u32[]{:S(2)}) collective-permute-start(f32[4,8,16,128]{3,2,1,0:T(8,128)S(1)} %pad_select_fusion), channel_id=1, source_target_pairs={{0,8},{8,16},{16,24},{24,32},{32,40},{40,48},{48,56},{56,64},{64,7... | collective-permute-start | bytes 786440 | tf_op jit(solution)/shard_map/ppermute | solution.py:36
  15.7 10.9 %collective-permute-start.3 = (f32[4,24,8,128]{3,2,1,0:T(8,128)S(1)}, f32[4,24,8,128]{3,2,1,0:T(8,128)S(1)}, u32[]{:S(2)}, u32[]{:S(2)}) collective-permute-start(f32[4,24,8,128]{3,2,1,0:T(8,128)S(1)} %pad_maximum_fusion.2), channel_id=1, source_target_pairs={{0,1},{1,2},{2,3},{3,4},{4,5},{5,6},{6,7},{8,9},{9,10},{10,11},{11... | collective-permute-start | bytes 1179656 | tf_op jit(solution)/shard_map/ppermute | solution.py:36
  18.3 12.6 %collective-permute-start.2 = (f32[4,24,8,128]{3,2,1,0:T(8,128)S(1)}, f32[4,24,8,128]{3,2,1,0:T(8,128)S(1)}, u32[]{:S(2)}, u32[]{:S(2)}) collective-permute-start(f32[4,24,8,128]{3,2,1,0:T(8,128)S(1)} %pad_maximum_fusion.1), channel_id=1, source_target_pairs={{1,0},{2,1},{3,2},{4,3},{5,4},{6,5},{7,6},{9,8},{10,9},{11,10},{12... | collective-permute-start | bytes 1179656 | tf_op jit(solution)/shard_map/ppermute | solution.py:37
  30.8 0.7 copy-start.1
  35.8 0.8 %copy-start.7 = (s32[2,1,128]{2,1,0:T(1,128)S(1)}, s32[2,1,128]{2,1,0:T(1,128)}, u32[]{:S(2)}) copy-start(s32[2,1,128]{2,1,0:T(1,128)} %param.11) | copy-start | bytes 3076
  37.4 7.1 %all-to-all-start = ((bf16[8,2,128]{2,1,0:T(2,128)(2,1)}), bf16[8,2,128]{2,1,0:T(2,128)(2,1)S(1)}, u32[]{:S(2)}, u32[]{:S(2)}) async-start(bf16[8,2,128]{2,1,0:T(2,128)(2,1)} %broadcast_in_dim.362), calls=%async_computation | async-start | bytes 8192 | tf_op jit(solution)/shard_map/all_to_all | solution.py:144
  45.9 10.7 %collective-permute-start.4 = (f32[2208]{0:T(1024)S(1)}, f32[2208]{0:T(1024)S(1)}, u32[]{:S(2)}, u32[]{:S(2)}) collective-permute-start(f32[2208]{0:T(1024)S(1)} %pad_maximum_fusion.13), channel_id=1, source_target_pairs={{0,8},{8,16},{16,24},{24,32},{32,40},{40,48},{48,56},{56,64},{64,7... | collective-permute-start | bytes 26504 | tf_op jit(solution)/shard_map/ppermute | solution.py:39
  53.9 8.6 %collective-permute-start.5 = (f32[2208]{0:T(1024)S(1)}, f32[2208]{0:T(1024)S(1)}, u32[]{:S(2)}, u32[]{:S(2)}) collective-permute-start(f32[2208]{0:T(1024)S(1)} %pad_maximum_fusion.14), channel_id=1, source_target_pairs={{8,0},{16,8},{24,16},{32,24},{40,32},{48,40},{56,48},{64,56},{72,6... | collective-permute-start | bytes 26504 | tf_op jit(solution)/shard_map/ppermute | solution.py:40
  62.9 6.6 %collective-permute-start.6 = (f32[1204]{0:T(1024)S(1)}, f32[1204]{0:T(1024)S(1)}, u32[]{:S(2)}, u32[]{:S(2)}) collective-permute-start(f32[1204]{0:T(1024)S(1)} %pad_maximum_fusion.15), channel_id=1, source_target_pairs={{0,1},{1,2},{2,3},{3,4},{4,5},{5,6},{6,7},{8,9},{9,10},{10,11},{11... | collective-permute-start | bytes 14456 | tf_op jit(solution)/shard_map/ppermute | solution.py:39
  67.3 6.5 %collective-permute-start.7 = (f32[1204]{0:T(1024)S(1)}, f32[1204]{0:T(1024)S(1)}, u32[]{:S(2)}, u32[]{:S(2)}) collective-permute-start(f32[1204]{0:T(1024)S(1)} %pad_maximum_fusion.16), channel_id=1, source_target_pairs={{1,0},{2,1},{3,2},{4,3},{5,4},{6,5},{7,6},{9,8},{10,9},{11,10},{12... | collective-permute-start | bytes 14456 | tf_op jit(solution)/shard_map/ppermute | solution.py:40
  74.9 1.6 %copy-start.2 = (f32[4,24,8,128]{3,2,1,0:T(8,128)S(1)}, f32[4,24,8,128]{3,2,1,0:T(8,128)}, u32[]{:S(2)}) copy-start(f32[4,24,8,128]{3,2,1,0:T(8,128)} %copy-done.1) | copy-start | bytes 1179652
  74.9 1.6 %copy-start.3 = (f32[3,10,18,128]{3,2,1,0:T(8,128)S(1)}, f32[3,10,18,128]{3,2,1,0:T(8,128)}, u32[]{:S(2)}) copy-start(f32[3,10,18,128]{3,2,1,0:T(8,128)} %slice.590) | copy-start | bytes 829444
  74.9 1.6 %copy-start.4 = (f32[3,8,16,128]{3,2,1,0:T(8,128)S(1)}, f32[3,8,16,128]{3,2,1,0:T(8,128)}, u32[]{:S(2)}) copy-start(f32[3,8,16,128]{3,2,1,0:T(8,128)} %param.7) | copy-start | bytes 589828

commit v11 on v10

--- a/solution.py
+++ b/solution.py
@@ -140,7 +140,14 @@
     local_list = near_list[0]
     blank_pick = jnp.zeros((local_list.shape[0], local_list.shape[1], NODES), jnp.bfloat16)
     group = lax.axis_size("gy")
-    copies = jnp.broadcast_to(low_panels[None], (group,) + low_panels.shape)
+    copies = jnp.sum(
+        jnp.where(
+            jnp.broadcast_to(onehot[None], (group,) + onehot.shape),
+            face_vals[None, :, None, :],
+            0.0,
+        ),
+        axis=3,
+    ).astype(jnp.bfloat16)
     piece = lax.all_to_all(copies, "gy", 0, 0, tiled=True).reshape(group * 2, NODES)
     valid = (local_list >= 0) & (local_list < piece.shape[0])
     picked = piece[jnp.clip(local_list, 0, piece.shape[0] - 1)]

time: 77.9 us -> 78.3 us (level)
  other arithmetic: 15 us -> 16.6 us
  starting transfers between devices: 34.5 us -> 33.1 us
    ppermute x2, starting transfers between devices: 12.2 us -> 10.7 us  [swap(): from_prev = lax.ppermute(_pack(to_next), axis, _pairs(count, 1))]
    reduce_sum x0 -> x1, other arithmetic: none -> 0.96 us  [body(): jnp.sum(jnp.where(jnp.broadcast_to(onehot[None], (group,) + onehot.shape)...]
    ppermute x2, waiting for transfers between devices: 2.25 us -> 3.1 us  [swap(): from_prev = [lax.ppermute(to_next[0], axis, _pairs(count, 1))]]
  transfers between devices with their start and end apart: 9 -> 9, of which waited for: 5 -> 5; matrix products, arithmetic and copies ran while one was open for 11% -> 12% of each run, Pallas kernels for 0% -> 0%
where the time goes in v11:
time: 78.3 us; the launch traced here: 77.8 us
  starting transfers between devices  33.1 us (42%)
  waiting for transfers between devices  20.4 us (26%)
  other arithmetic  16.6 us (21%)
  local copies, waits for them, and re-layouts  6.36 us (8%)
  between operations  1.16 us (1%)
    ppermute x2, starting transfers between devices, swap(): from_prev = lax.ppermute(_pack(to_next), axis, _pairs(count, 1))  10.7 us
    ppermute x2, waiting for transfers between devices, swap(): from_next = lax.ppermute(_pack(to_prev), axis, _pairs(count, -1))  10.1 us
    ppermute x2, starting transfers between devices, swap(): from_prev = [lax.ppermute(to_next[0], axis, _pairs(count, 1))]  9.08 us
    ppermute x2, starting transfers between devices, swap(): from_next = [lax.ppermute(to_prev[0], axis, _pairs(count, -1))]  5.51 us
    ppermute x2, waiting for transfers between devices, swap(): from_next = [lax.ppermute(to_prev[0], axis, _pairs(count, -1))]  4.16 us
    all_to_all x1, starting transfers between devices, body(): lax.all_to_all(copies, 'gy', 0, 0, tiled=True).reshape(group * 2, NODES)  3.95 us
    ppermute x2, starting transfers between devices, swap(): from_next = lax.ppermute(_pack(to_prev), axis, _pairs(count, -1))  3.83 us
    ppermute x2, waiting for transfers between devices, swap(): from_prev = [lax.ppermute(to_next[0], axis, _pairs(count, 1))]  3.1 us
  transfers between devices with their start and end apart: 9, of which 5 were waited for; matrix products, arithmetic and copies ran while one was open for 12% of the time, Pallas kernels for 0%

profile of v11, /device:TPU:125, one launch (start us, length us, event | category | flops | bytes accessed | tf_op | source)
XLA Modules:
  0.0 77.8 jit_solution(14743620346530037930)
XLA Ops:
  0.7 0.9 %convert_element_type.37 = f32[8,16,128]{2,1,0:T(8,128)S(1)} convert(s32[8,16,128]{2,1,0:T(8,128)} %param.8) | non-fusion elementwise | flops 16384 | bytes 131072 | tf_op jit(solution)/shard_map/convert_element_type | solution.py:101
  1.6 1.0 %pad_select_fusion = f32[4,8,16,128]{3,2,1,0:T(8,128)S(1)} fusion(f32[3,8,16,128]{3,2,1,0:T(8,128)} %param.7, f32[8,16,128]{2,1,0:T(8,128)S(1)} %convert_element_type.37, pred[4]{0:T(512)(128)(4,1)S(1)} %iota_compare_fusion.5), kind=kLoop, calls=%fused_computation.64 | loop fusion | flops 65536 | bytes 524292 | tf_op jit(solution)/shard_map/jit(_where)/select_n | solution.py:99
  2.6 2.7 %collective-permute-start = (f32[4,8,16,128]{3,2,1,0:T(8,128)S(1)}, f32[4,8,16,128]{3,2,1,0:T(8,128)S(1)}, u32[]{:S(2)}, u32[]{:S(2)}) collective-permute-start(f32[4,8,16,128]{3,2,1,0:T(8,128)S(1)} %pad_select_fusion), channel_id=1, source_target_pairs={{8,0},{16,8},{24,16},{32,24},{40,32},{48,40},{56,48},{64,56},{72,6... | collective-permute-start | bytes 786440 | tf_op jit(solution)/shard_map/ppermute | solution.py:37
  5.3 6.6 %collective-permute-start.1 = (f32[4,8,16,128]{3,2,1,0:T(8,128)S(1)}, f32[4,8,16,128]{3,2,1,0:T(8,128)S(1)}, u32[]{:S(2)}, u32[]{:S(2)}) collective-permute-start(f32[4,8,16,128]{3,2,1,0:T(8,128)S(1)} %pad_select_fusion), channel_id=1, source_target_pairs={{0,8},{8,16},{16,24},{24,32},{32,40},{40,48},{48,56},{56,64},{64,7... | collective-permute-start | bytes 786440 | tf_op jit(solution)/shard_map/ppermute | solution.py:36
  12.2 0.8 %iota_compare_fusion = pred[2,128,128]{2,1,0:T(8,128)(4,1)S(1)} fusion(s32[2,128]{1,0:T(2,128)} %bitcast.82), kind=kLoop, calls=%fused_computation.134 | loop fusion | flops 32768 | bytes 33792 | tf_op jit(solution)/shard_map/eq | solution.py:136
  13.0 0.7 compare_select_fusion
  14.2 0.7 and_bitcast_fusion
  15.0 1.5 %fusion.91 = (f32[1]{0:T(128)}, f32[1]{0:T(128)}, f32[1]{0:T(128)}, f32[1]{0:T(128)}) fusion(f32[4]{0:T(128)} %param.10), kind=kLoop, calls=%fused_computation.237 | loop fusion | bytes 32 | tf_op jit(solution)/shard_map/slice | solution.py:77
  16.5 2.5 %collective-permute-start.3 = (f32[4,24,8,128]{3,2,1,0:T(8,128)S(1)}, f32[4,24,8,128]{3,2,1,0:T(8,128)S(1)}, u32[]{:S(2)}, u32[]{:S(2)}) collective-permute-start(f32[4,24,8,128]{3,2,1,0:T(8,128)S(1)} %pad_maximum_fusion.2), channel_id=1, source_target_pairs={{0,1},{1,2},{2,3},{3,4},{4,5},{5,6},{6,7},{8,9},{9,10},{10,11},{11... | collective-permute-start | bytes 1179656 | tf_op jit(solution)/shard_map/ppermute | solution.py:36
  19.1 2.8 %collective-permute-start.2 = (f32[4,24,8,128]{3,2,1,0:T(8,128)S(1)}, f32[4,24,8,128]{3,2,1,0:T(8,128)S(1)}, u32[]{:S(2)}, u32[]{:S(2)}) collective-permute-start(f32[4,24,8,128]{3,2,1,0:T(8,128)S(1)} %pad_maximum_fusion.1), channel_id=1, source_target_pairs={{1,0},{2,1},{3,2},{4,3},{5,4},{6,5},{7,6},{9,8},{10,9},{11,10},{12... | collective-permute-start | bytes 1179656 | tf_op jit(solution)/shard_map/ppermute | solution.py:37
  21.9 0.7 fusion.90
  22.6 2.6 %select_select_fusion.1 = f32[8,16,128]{2,1,0:T(8,128)S(1)} fusion(s32[8,16,128]{2,1,0:T(8,128)S(1)} %copy-done.5, f32[]{:T(128)} %bitcast.3, f32[]{:T(128)} %bitcast.2, f32[]{:T(128)} %bitcast.1, f32[]{:T(128)} %bitcast), kind=kLoop, calls=%fused_computation.175 | loop fusion | flops 98304 | bytes 131088 | tf_op jit(solution)/shard_map/jit(_where)/select_n | solution.py:77
  25.1 3.1 %collective-permute-done.3 = f32[4,24,8,128]{3,2,1,0:T(8,128)S(1)} collective-permute-done((f32[4,24,8,128]{3,2,1,0:T(8,128)S(1)}, f32[4,24,8,128]{3,2,1,0:T(8,128)S(1)}, u32[]{:S(2)}, u32[]{:S(2)}) %collective-permute-start.3) | collective-permute-done | bytes 393248 | tf_op jit(solution)/shard_map/ppermute | solution.py:36
  28.2 4.2 %collective-permute-done.2 = f32[4,24,8,128]{3,2,1,0:T(8,128)S(1)} collective-permute-done((f32[4,24,8,128]{3,2,1,0:T(8,128)S(1)}, f32[4,24,8,128]{3,2,1,0:T(8,128)S(1)}, u32[]{:S(2)}, u32[]{:S(2)}) %collective-permute-start.2) | collective-permute-done | bytes 393248 | tf_op jit(solution)/shard_map/ppermute | solution.py:37
  32.6 0.6 copy-done.1
  33.3 2.9 %multiply_select_fusion = (f32[22,30,128]{2,1,0:T(8,128)S(1)}, f32[22,30,128]{2,1,0:T(8,128)S(1)}) fusion(pred[22,30]{1,0:T(8,128)(4,1)S(1)} %broadcast_and_fusion, f32[22,30,128]{2,1,0:T(8,128)S(1)} %slice.599, f32[24,32,128]{2,1,0:T(8,128)S(1)} %get-tuple-element.8, f32[24,32,128]{2,1,0:T(8,128)S(1)} %get-tuple-element.6, f32[]{:T(128)} %bitcast.9, ...), kind=kLoop, calls=%fused_computation.38 | loop fusion | flops 1436160 | bytes 2704036 | tf_op jit(solution)/shard_map/jit(_where)/select_n | solution.py:123
  36.2 0.3 fusion.10
  36.5 0.3 fusion.15
  38.3 1.0 %select_reduce_fusion = bf16[8,2,128]{2,1,0:T(2,128)(2,1)} fusion(f32[2,128]{1,0:T(2,128)S(1)} %bitcast.86, pred[2,128,128]{2,1,0:T(8,128)(4,1)S(1)} %iota_compare_fusion), kind=kLoop, calls=%fused_computation.2 | loop fusion | flops 522240 | bytes 37888 | tf_op jit(solution)/shard_map/reduce_sum | solution.py:143
  39.3 3.9 %all-to-all-start = ((bf16[8,2,128]{2,1,0:T(2,128)(2,1)}), bf16[8,2,128]{2,1,0:T(2,128)(2,1)S(1)}, u32[]{:S(2)}, u32[]{:S(2)}) async-start(bf16[8,2,128]{2,1,0:T(2,128)(2,1)} %select_reduce_fusion), calls=%async_computation | async-start | bytes 8192 | tf_op jit(solution)/shard_map/all_to_all | solution.py:151
  43.4 3.0 %all-to-all-done = bf16[8,2,128]{2,1,0:T(2,128)(2,1)S(1)} async-done(((bf16[8,2,128]{2,1,0:T(2,128)(2,1)}), bf16[8,2,128]{2,1,0:T(2,128)(2,1)S(1)}, u32[]{:S(2)}, u32[]{:S(2)}) %all-to-all-start) | async-done | bytes 4128 | tf_op jit(solution)/shard_map/all_to_all | solution.py:151
  46.4 0.6 gather_fusion
  47.7 6.4 %collective-permute-start.4 = (f32[2208]{0:T(1024)S(1)}, f32[2208]{0:T(1024)S(1)}, u32[]{:S(2)}, u32[]{:S(2)}) collective-permute-start(f32[2208]{0:T(1024)S(1)} %pad_maximum_fusion.13), channel_id=1, source_target_pairs={{0,8},{8,16},{16,24},{24,32},{32,40},{40,48},{48,56},{56,64},{64,7... | collective-permute-start | bytes 26504 | tf_op jit(solution)/shard_map/ppermute | solution.py:39
  54.2 1.9 %collective-permute-start.5 = (f32[2208]{0:T(1024)S(1)}, f32[2208]{0:T(1024)S(1)}, u32[]{:S(2)}, u32[]{:S(2)}) collective-permute-start(f32[2208]{0:T(1024)S(1)} %pad_maximum_fusion.14), channel_id=1, source_target_pairs={{8,0},{16,8},{24,16},{32,24},{40,32},{48,40},{56,48},{64,56},{72,6... | collective-permute-start | bytes 26504 | tf_op jit(solution)/shard_map/ppermute | solution.py:40
  56.2 0.8 slice.590
  57.0 5.8 %collective-permute-done.5 = f32[2208]{0:T(1024)S(1)} collective-permute-done((f32[2208]{0:T(1024)S(1)}, f32[2208]{0:T(1024)S(1)}, u32[]{:S(2)}, u32[]{:S(2)}) %collective-permute-start.5) | collective-permute-done | bytes 8864 | tf_op jit(solution)/shard_map/ppermute | solution.py:40
  63.2 4.3 %collective-permute-start.6 = (f32[1204]{0:T(1024)S(1)}, f32[1204]{0:T(1024)S(1)}, u32[]{:S(2)}, u32[]{:S(2)}) collective-permute-start(f32[1204]{0:T(1024)S(1)} %pad_maximum_fusion.15), channel_id=1, source_target_pairs={{0,1},{1,2},{2,3},{3,4},{4,5},{5,6},{6,7},{8,9},{9,10},{10,11},{11... | collective-permute-start | bytes 14456 | tf_op jit(solution)/shard_map/ppermute | solution.py:39
  67.7 1.9 %collective-permute-start.7 = (f32[1204]{0:T(1024)S(1)}, f32[1204]{0:T(1024)S(1)}, u32[]{:S(2)}, u32[]{:S(2)}) collective-permute-start(f32[1204]{0:T(1024)S(1)} %pad_maximum_fusion.16), channel_id=1, source_target_pairs={{1,0},{2,1},{3,2},{4,3},{5,4},{6,5},{7,6},{9,8},{10,9},{11,10},{12... | collective-permute-start | bytes 14456 | tf_op jit(solution)/shard_map/ppermute | solution.py:40
  69.9 4.3 %collective-permute-done.7 = f32[1204]{0:T(1024)S(1)} collective-permute-done((f32[1204]{0:T(1024)S(1)}, f32[1204]{0:T(1024)S(1)}, u32[]{:S(2)}, u32[]{:S(2)}) %collective-permute-start.7) | collective-permute-done | bytes 4848 | tf_op jit(solution)/shard_map/ppermute | solution.py:40
  75.0 0.3 fusion.26
  76.3 0.7 fusion.86
  76.9 0.9 %fusion.31 = f32[3,8,16,128]{3,2,1,0:T(8,128)} fusion(f32[3,10,18,128]{3,2,1,0:T(8,128)S(1)} %copy-done.3, f32[4,24,8,128]{3,2,1,0:T(8,128)S(1)} %collective-permute-done.3, f32[4,8,16,128]{3,2,1,0:T(8,128)S(1)} %collective-permute-done, f32[4,8,16,128]{3,2,1,0:T(8,128)S(1)} %pad_select_fusion, f32[4,8,16,128]{3,2,1,0:T(8,128)S(1)} %collective-permute-done.1, ...), kind=kLoop, calls=%fused_computation.80 | loop fusion | flops 933888 | bytes 2504704 | tf_op jit(solution)/shard_map/sub | solution.py:206
  (105 shorter events, 6.1 us)
Async XLA Ops:
  0.6 46.4 %copy-start = (bf16[1,2,8,128,128]{4,3,2,1,0:T(8,128)(2,1)S(1)}, bf16[1,2,8,128,128]{4,3,2,1,0:T(8,128)(2,1)}, u32[]{:S(2)}) copy-start(bf16[1,2,8,128,128]{4,3,2,1,0:T(8,128)(2,1)} %param.13) | copy-start | bytes 1572868
  2.6 19.3 %copy-start.7 = (f32[4]{0:T(128)S(1)}, f32[4]{0:T(128)}, u32[]{:S(2)}) copy-start(f32[4]{0:T(128)} %param.9) | copy-start | bytes 52
  2.6 20.0 %copy-start.5 = (s32[8,16,128]{2,1,0:T(8,128)S(1)}, s32[8,16,128]{2,1,0:T(8,128)}, u32[]{:S(2)}) copy-start(s32[8,16,128]{2,1,0:T(8,128)} %param.8) | copy-start | bytes 196612
  2.6 13.8 %collective-permute-start = (f32[4,8,16,128]{3,2,1,0:T(8,128)S(1)}, f32[4,8,16,128]{3,2,1,0:T(8,128)S(1)}, u32[]{:S(2)}, u32[]{:S(2)}) collective-permute-start(f32[4,8,16,128]{3,2,1,0:T(8,128)S(1)} %pad_select_fusion), channel_id=1, source_target_pairs={{8,0},{16,8},{24,16},{32,24},{40,32},{48,40},{56,48},{64,56},{72,6... | collective-permute-start | bytes 786440 | tf_op jit(solution)/shard_map/ppermute | solution.py:37
  5.3 11.1 %collective-permute-start.1 = (f32[4,8,16,128]{3,2,1,0:T(8,128)S(1)}, f32[4,8,16,128]{3,2,1,0:T(8,128)S(1)}, u32[]{:S(2)}, u32[]{:S(2)}) collective-permute-start(f32[4,8,16,128]{3,2,1,0:T(8,128)S(1)} %pad_select_fusion), channel_id=1, source_target_pairs={{0,8},{8,16},{16,24},{24,32},{32,40},{40,48},{48,56},{56,64},{64,7... | collective-permute-start | bytes 786440 | tf_op jit(solution)/shard_map/ppermute | solution.py:36
  16.5 11.7 %collective-permute-start.3 = (f32[4,24,8,128]{3,2,1,0:T(8,128)S(1)}, f32[4,24,8,128]{3,2,1,0:T(8,128)S(1)}, u32[]{:S(2)}, u32[]{:S(2)}) collective-permute-start(f32[4,24,8,128]{3,2,1,0:T(8,128)S(1)} %pad_maximum_fusion.2), channel_id=1, source_target_pairs={{0,1},{1,2},{2,3},{3,4},{4,5},{5,6},{6,7},{8,9},{9,10},{10,11},{11... | collective-permute-start | bytes 1179656 | tf_op jit(solution)/shard_map/ppermute | solution.py:36
  19.1 13.3 %collective-permute-start.2 = (f32[4,24,8,128]{3,2,1,0:T(8,128)S(1)}, f32[4,24,8,128]{3,2,1,0:T(8,128)S(1)}, u32[]{:S(2)}, u32[]{:S(2)}) collective-permute-start(f32[4,24,8,128]{3,2,1,0:T(8,128)S(1)} %pad_maximum_fusion.1), channel_id=1, source_target_pairs={{1,0},{2,1},{3,2},{4,3},{5,4},{6,5},{7,6},{9,8},{10,9},{11,10},{12... | collective-permute-start | bytes 1179656 | tf_op jit(solution)/shard_map/ppermute | solution.py:37
  32.4 0.8 copy-start.1
  37.3 5.9 %copy-start.6 = (s32[2,1,128]{2,1,0:T(1,128)S(1)}, s32[2,1,128]{2,1,0:T(1,128)}, u32[]{:S(2)}) copy-start(s32[2,1,128]{2,1,0:T(1,128)} %param.11) | copy-start | bytes 3076
  39.3 7.1 %all-to-all-start = ((bf16[8,2,128]{2,1,0:T(2,128)(2,1)}), bf16[8,2,128]{2,1,0:T(2,128)(2,1)S(1)}, u32[]{:S(2)}, u32[]{:S(2)}) async-start(bf16[8,2,128]{2,1,0:T(2,128)(2,1)} %select_reduce_fusion), calls=%async_computation | async-start | bytes 8192 | tf_op jit(solution)/shard_map/all_to_all | solution.py:151
  47.7 9.3 %collective-permute-start.4 = (f32[2208]{0:T(1024)S(1)}, f32[2208]{0:T(1024)S(1)}, u32[]{:S(2)}, u32[]{:S(2)}) collective-permute-start(f32[2208]{0:T(1024)S(1)} %pad_maximum_fusion.13), channel_id=1, source_target_pairs={{0,8},{8,16},{16,24},{24,32},{32,40},{40,48},{48,56},{56,64},{64,7... | collective-permute-start | bytes 26504 | tf_op jit(solution)/shard_map/ppermute | solution.py:39
  54.2 8.6 %collective-permute-start.5 = (f32[2208]{0:T(1024)S(1)}, f32[2208]{0:T(1024)S(1)}, u32[]{:S(2)}, u32[]{:S(2)}) collective-permute-start(f32[2208]{0:T(1024)S(1)} %pad_maximum_fusion.14), channel_id=1, source_target_pairs={{8,0},{16,8},{24,16},{32,24},{40,32},{48,40},{56,48},{64,56},{72,6... | collective-permute-start | bytes 26504 | tf_op jit(solution)/shard_map/ppermute | solution.py:40
  63.2 6.6 %collective-permute-start.6 = (f32[1204]{0:T(1024)S(1)}, f32[1204]{0:T(1024)S(1)}, u32[]{:S(2)}, u32[]{:S(2)}) collective-permute-start(f32[1204]{0:T(1024)S(1)} %pad_maximum_fusion.15), channel_id=1, source_target_pairs={{0,1},{1,2},{2,3},{3,4},{4,5},{5,6},{6,7},{8,9},{9,10},{10,11},{11... | collective-permute-start | bytes 14456 | tf_op jit(solution)/shard_map/ppermute | solution.py:39
  67.7 6.5 %collective-permute-start.7 = (f32[1204]{0:T(1024)S(1)}, f32[1204]{0:T(1024)S(1)}, u32[]{:S(2)}, u32[]{:S(2)}) collective-permute-start(f32[1204]{0:T(1024)S(1)} %pad_maximum_fusion.16), channel_id=1, source_target_pairs={{1,0},{2,1},{3,2},{4,3},{5,4},{6,5},{7,6},{9,8},{10,9},{11,10},{12... | collective-permute-start | bytes 14456 | tf_op jit(solution)/shard_map/ppermute | solution.py:40
  75.3 1.6 %copy-start.2 = (f32[4,24,8,128]{3,2,1,0:T(8,128)S(1)}, f32[4,24,8,128]{3,2,1,0:T(8,128)}, u32[]{:S(2)}) copy-start(f32[4,24,8,128]{3,2,1,0:T(8,128)} %copy-done.1) | copy-start | bytes 1179652
  75.3 1.6 %copy-start.3 = (f32[3,10,18,128]{3,2,1,0:T(8,128)S(1)}, f32[3,10,18,128]{3,2,1,0:T(8,128)}, u32[]{:S(2)}) copy-start(f32[3,10,18,128]{3,2,1,0:T(8,128)} %slice.590) | copy-start | bytes 829444
  75.3 1.6 %copy-start.4 = (f32[3,8,16,128]{3,2,1,0:T(8,128)S(1)}, f32[3,8,16,128]{3,2,1,0:T(8,128)}, u32[]{:S(2)}) copy-start(f32[3,8,16,128]{3,2,1,0:T(8,128)} %param.7) | copy-start | bytes 589828

commit v12 on v10

--- a/solution.py
+++ b/solution.py
@@ -158,12 +158,13 @@
         [planes[:, cells_x - he :], scalar[cells_x - 1 :]],
         [planes[:, :he], scalar[:1]],
     )
-    planes_x = jnp.concatenate([p_lo, planes, p_hi], axis=1)
+    pieces = (p_lo, planes, p_hi)
     (q_lo, t_lo), (q_hi, t_hi) = swap(
         "gy",
-        [planes_x[:, :, cells_y - he :], scalar[:, cells_y - 1 :]],
-        [planes_x[:, :, :he], scalar[:, :1]],
-    )
+        [jnp.concatenate([p[:, :, cells_y - he :] for p in pieces], axis=1), scalar[:, cells_y - 1 :]],
+        [jnp.concatenate([p[:, :, :he] for p in pieces], axis=1), scalar[:, :1]],
+    )
+    planes_x = jnp.concatenate(pieces, axis=1)
     planes_w = jnp.concatenate([q_lo, planes_x, q_hi], axis=2)
 
     column = jnp.concatenate([s_lo, scalar, s_hi], axis=0)

time: 77.9 us -> 78 us (level)
  no operation moved by 1% of the time
where the time goes in v12:
time: 78 us; the launch traced here: 77.4 us
  starting transfers between devices  34.5 us (44%)
  waiting for transfers between devices  19.6 us (25%)
  other arithmetic  14.9 us (19%)
  local copies, waits for them, and re-layouts  6.95 us (9%)
  between operations  1.17 us (2%)
    ppermute x2, starting transfers between devices, swap(): from_prev = lax.ppermute(_pack(to_next), axis, _pairs(count, 1))  12.2 us
    ppermute x2, waiting for transfers between devices, swap(): from_next = lax.ppermute(_pack(to_prev), axis, _pairs(count, -1))  10.8 us
    ppermute x2, starting transfers between devices, swap(): from_prev = [lax.ppermute(to_next[0], axis, _pairs(count, 1))]  9.08 us
    ppermute x2, starting transfers between devices, swap(): from_next = [lax.ppermute(to_prev[0], axis, _pairs(count, -1))]  5.51 us
    ppermute x2, waiting for transfers between devices, swap(): from_next = [lax.ppermute(to_prev[0], axis, _pairs(count, -1))]  4.16 us
    all_to_all x1, starting transfers between devices, body(): lax.all_to_all(copies, 'gy', 0, 0, tiled=True).reshape(group * 2, NODES)  3.95 us
    ppermute x2, starting transfers between devices, swap(): from_next = lax.ppermute(_pack(to_prev), axis, _pairs(count, -1))  3.83 us
    select_n x1, other arithmetic, body(): scalar = jnp.where(inside(hs), source / DIAG, 0.0)  2.91 us
  transfers between devices with their start and end apart: 9, of which 5 were waited for; matrix products, arithmetic and copies ran while one was open for 11% of the time, Pallas kernels for 0%

profile of v12, /device:TPU:125, one launch (start us, length us, event | category | flops | bytes accessed | tf_op | source)
XLA Modules:
  0.0 77.4 jit_solution(18174552679019795020)
XLA Ops:
  0.7 0.9 %convert_element_type.41 = f32[8,16,128]{2,1,0:T(8,128)S(1)} convert(s32[8,16,128]{2,1,0:T(8,128)} %param.8) | non-fusion elementwise | flops 16384 | bytes 131072 | tf_op jit(solution)/shard_map/convert_element_type | solution.py:101
  1.6 1.0 %pad_select_fusion = f32[4,8,16,128]{3,2,1,0:T(8,128)S(1)} fusion(f32[3,8,16,128]{3,2,1,0:T(8,128)} %param.7, f32[8,16,128]{2,1,0:T(8,128)S(1)} %convert_element_type.41, pred[4]{0:T(512)(128)(4,1)S(1)} %iota_compare_fusion.5), kind=kLoop, calls=%fused_computation.63 | loop fusion | flops 65536 | bytes 524292 | tf_op jit(solution)/shard_map/jit(_where)/select_n | solution.py:99
  2.6 2.7 %collective-permute-start = (f32[4,8,16,128]{3,2,1,0:T(8,128)S(1)}, f32[4,8,16,128]{3,2,1,0:T(8,128)S(1)}, u32[]{:S(2)}, u32[]{:S(2)}) collective-permute-start(f32[4,8,16,128]{3,2,1,0:T(8,128)S(1)} %pad_select_fusion), channel_id=1, source_target_pairs={{8,0},{16,8},{24,16},{32,24},{40,32},{48,40},{56,48},{64,56},{72,6... | collective-permute-start | bytes 786440 | tf_op jit(solution)/shard_map/ppermute | solution.py:37
  5.3 6.6 %collective-permute-start.1 = (f32[4,8,16,128]{3,2,1,0:T(8,128)S(1)}, f32[4,8,16,128]{3,2,1,0:T(8,128)S(1)}, u32[]{:S(2)}, u32[]{:S(2)}) collective-permute-start(f32[4,8,16,128]{3,2,1,0:T(8,128)S(1)} %pad_select_fusion), channel_id=1, source_target_pairs={{0,8},{8,16},{16,24},{24,32},{32,40},{40,48},{48,56},{56,64},{64,7... | collective-permute-start | bytes 786440 | tf_op jit(solution)/shard_map/ppermute | solution.py:36
  12.2 0.7 compare_select_fusion
  13.4 0.7 and_bitcast_fusion
  14.2 1.4 %fusion.93 = (f32[1]{0:T(128)}, f32[1]{0:T(128)}, f32[1]{0:T(128)}, f32[1]{0:T(128)}) fusion(f32[4]{0:T(128)} %param.10), kind=kLoop, calls=%fused_computation.238 | loop fusion | bytes 32 | tf_op jit(solution)/shard_map/slice | solution.py:77
  15.7 2.5 %collective-permute-start.3 = (f32[4,24,8,128]{3,2,1,0:T(8,128)S(1)}, f32[4,24,8,128]{3,2,1,0:T(8,128)S(1)}, u32[]{:S(2)}, u32[]{:S(2)}) collective-permute-start(f32[4,24,8,128]{3,2,1,0:T(8,128)S(1)} %pad_maximum_fusion.2), channel_id=1, source_target_pairs={{0,1},{1,2},{2,3},{3,4},{4,5},{5,6},{6,7},{8,9},{9,10},{10,11},{11... | collective-permute-start | bytes 1179656 | tf_op jit(solution)/shard_map/ppermute | solution.py:36
  18.3 2.8 %collective-permute-start.2 = (f32[4,24,8,128]{3,2,1,0:T(8,128)S(1)}, f32[4,24,8,128]{3,2,1,0:T(8,128)S(1)}, u32[]{:S(2)}, u32[]{:S(2)}) collective-permute-start(f32[4,24,8,128]{3,2,1,0:T(8,128)S(1)} %pad_maximum_fusion.1), channel_id=1, source_target_pairs={{1,0},{2,1},{3,2},{4,3},{5,4},{6,5},{7,6},{9,8},{10,9},{11,10},{12... | collective-permute-start | bytes 1179656 | tf_op jit(solution)/shard_map/ppermute | solution.py:37
  21.1 0.7 fusion.92
  21.8 2.6 %select_select_fusion.1 = f32[8,16,128]{2,1,0:T(8,128)S(1)} fusion(s32[8,16,128]{2,1,0:T(8,128)S(1)} %copy-done.5, f32[]{:T(128)} %bitcast.3, f32[]{:T(128)} %bitcast.2, f32[]{:T(128)} %bitcast.1, f32[]{:T(128)} %bitcast), kind=kLoop, calls=%fused_computation.174 | loop fusion | flops 98304 | bytes 131088 | tf_op jit(solution)/shard_map/jit(_where)/select_n | solution.py:77
  24.4 2.2 %collective-permute-done.3 = f32[4,24,8,128]{3,2,1,0:T(8,128)S(1)} collective-permute-done((f32[4,24,8,128]{3,2,1,0:T(8,128)S(1)}, f32[4,24,8,128]{3,2,1,0:T(8,128)S(1)}, u32[]{:S(2)}, u32[]{:S(2)}) %collective-permute-start.3) | collective-permute-done | bytes 393248 | tf_op jit(solution)/shard_map/ppermute | solution.py:36
  26.7 4.2 %collective-permute-done.2 = f32[4,24,8,128]{3,2,1,0:T(8,128)S(1)} collective-permute-done((f32[4,24,8,128]{3,2,1,0:T(8,128)S(1)}, f32[4,24,8,128]{3,2,1,0:T(8,128)S(1)}, u32[]{:S(2)}, u32[]{:S(2)}) %collective-permute-start.2) | collective-permute-done | bytes 393248 | tf_op jit(solution)/shard_map/ppermute | solution.py:37
  31.0 0.6 copy-done.1
  31.7 2.9 %multiply_select_fusion = (f32[22,30,128]{2,1,0:T(8,128)S(1)}, f32[22,30,128]{2,1,0:T(8,128)S(1)}) fusion(pred[22,30]{1,0:T(8,128)(4,1)S(1)} %broadcast_and_fusion, f32[22,30,128]{2,1,0:T(8,128)S(1)} %slice.615, f32[24,32,128]{2,1,0:T(8,128)S(1)} %get-tuple-element.8, f32[24,32,128]{2,1,0:T(8,128)S(1)} %get-tuple-element.6, f32[]{:T(128)} %bitcast.9, ...), kind=kLoop, calls=%fused_computation.37 | loop fusion | flops 1436160 | bytes 2704036 | tf_op jit(solution)/shard_map/jit(_where)/select_n | solution.py:123
  34.6 0.3 fusion.10
  35.0 0.3 fusion.15
  36.8 0.6 broadcast_in_dim.362
  37.4 3.9 %all-to-all-start = ((bf16[8,2,128]{2,1,0:T(2,128)(2,1)}), bf16[8,2,128]{2,1,0:T(2,128)(2,1)S(1)}, u32[]{:S(2)}, u32[]{:S(2)}) async-start(bf16[8,2,128]{2,1,0:T(2,128)(2,1)} %broadcast_in_dim.362), calls=%async_computation | async-start | bytes 8192 | tf_op jit(solution)/shard_map/all_to_all | solution.py:144
  41.3 0.8 %slice.606 = f32[3,10,18,128]{3,2,1,0:T(8,128)} slice(f32[4,24,32,128]{3,2,1,0:T(8,128)S(1)} %pad_maximum_fusion), slice={[0:3], [7:17], [7:25], [0:128]} | slice | bytes 552960 | tf_op jit(solution)/shard_map/slice | solution.py:131
  42.1 2.4 %all-to-all-done = bf16[8,2,128]{2,1,0:T(2,128)(2,1)S(1)} async-done(((bf16[8,2,128]{2,1,0:T(2,128)(2,1)}), bf16[8,2,128]{2,1,0:T(2,128)(2,1)S(1)}, u32[]{:S(2)}, u32[]{:S(2)}) %all-to-all-start) | async-done | bytes 4128 | tf_op jit(solution)/shard_map/all_to_all | solution.py:144
  44.5 0.6 gather_fusion
  45.9 7.9 %collective-permute-start.4 = (f32[2208]{0:T(1024)S(1)}, f32[2208]{0:T(1024)S(1)}, u32[]{:S(2)}, u32[]{:S(2)}) collective-permute-start(f32[2208]{0:T(1024)S(1)} %pad_maximum_fusion.14), channel_id=1, source_target_pairs={{0,8},{8,16},{16,24},{24,32},{32,40},{40,48},{48,56},{56,64},{64,7... | collective-permute-start | bytes 26504 | tf_op jit(solution)/shard_map/ppermute | solution.py:39
  53.9 1.9 %collective-permute-start.5 = (f32[2208]{0:T(1024)S(1)}, f32[2208]{0:T(1024)S(1)}, u32[]{:S(2)}, u32[]{:S(2)}) collective-permute-start(f32[2208]{0:T(1024)S(1)} %pad_maximum_fusion.15), channel_id=1, source_target_pairs={{8,0},{16,8},{24,16},{32,24},{40,32},{48,40},{56,48},{64,56},{72,6... | collective-permute-start | bytes 26504 | tf_op jit(solution)/shard_map/ppermute | solution.py:40
  56.0 6.5 %collective-permute-done.5 = f32[2208]{0:T(1024)S(1)} collective-permute-done((f32[2208]{0:T(1024)S(1)}, f32[2208]{0:T(1024)S(1)}, u32[]{:S(2)}, u32[]{:S(2)}) %collective-permute-start.5) | collective-permute-done | bytes 8864 | tf_op jit(solution)/shard_map/ppermute | solution.py:40
  62.9 4.3 %collective-permute-start.6 = (f32[1204]{0:T(1024)S(1)}, f32[1204]{0:T(1024)S(1)}, u32[]{:S(2)}, u32[]{:S(2)}) collective-permute-start(f32[1204]{0:T(1024)S(1)} %pad_maximum_fusion.16), channel_id=1, source_target_pairs={{0,1},{1,2},{2,3},{3,4},{4,5},{5,6},{6,7},{8,9},{9,10},{10,11},{11... | collective-permute-start | bytes 14456 | tf_op jit(solution)/shard_map/ppermute | solution.py:39
  67.4 1.9 %collective-permute-start.7 = (f32[1204]{0:T(1024)S(1)}, f32[1204]{0:T(1024)S(1)}, u32[]{:S(2)}, u32[]{:S(2)}) collective-permute-start(f32[1204]{0:T(1024)S(1)} %pad_maximum_fusion.17), channel_id=1, source_target_pairs={{1,0},{2,1},{3,2},{4,3},{5,4},{6,5},{7,6},{9,8},{10,9},{11,10},{12... | collective-permute-start | bytes 14456 | tf_op jit(solution)/shard_map/ppermute | solution.py:40
  69.6 4.3 %collective-permute-done.7 = f32[1204]{0:T(1024)S(1)} collective-permute-done((f32[1204]{0:T(1024)S(1)}, f32[1204]{0:T(1024)S(1)}, u32[]{:S(2)}, u32[]{:S(2)}) %collective-permute-start.7) | collective-permute-done | bytes 4848 | tf_op jit(solution)/shard_map/ppermute | solution.py:40
  74.6 0.3 fusion.26
  75.0 0.3 fusion.45
  75.9 0.7 fusion.86
  76.6 0.9 %fusion.31 = f32[3,8,16,128]{3,2,1,0:T(8,128)} fusion(f32[3,10,18,128]{3,2,1,0:T(8,128)S(1)} %copy-done.3, f32[4,24,8,128]{3,2,1,0:T(8,128)S(1)} %collective-permute-done.3, f32[4,8,16,128]{3,2,1,0:T(8,128)S(1)} %collective-permute-done, f32[4,8,16,128]{3,2,1,0:T(8,128)S(1)} %pad_select_fusion, f32[4,8,16,128]{3,2,1,0:T(8,128)S(1)} %collective-permute-done.1, ...), kind=kLoop, calls=%fused_computation.79 | loop fusion | flops 933888 | bytes 2504704 | tf_op jit(solution)/shard_map/sub | solution.py:200
  (104 shorter events, 5.8 us)
Async XLA Ops:
  0.6 44.5 %copy-start = (bf16[1,2,8,128,128]{4,3,2,1,0:T(8,128)(2,1)S(1)}, bf16[1,2,8,128,128]{4,3,2,1,0:T(8,128)(2,1)}, u32[]{:S(2)}) copy-start(bf16[1,2,8,128,128]{4,3,2,1,0:T(8,128)(2,1)} %param.13) | copy-start | bytes 1572868
  2.6 18.5 %copy-start.6 = (f32[4]{0:T(128)S(1)}, f32[4]{0:T(128)}, u32[]{:S(2)}) copy-start(f32[4]{0:T(128)} %param.9) | copy-start | bytes 52
  2.6 19.2 %copy-start.5 = (s32[8,16,128]{2,1,0:T(8,128)S(1)}, s32[8,16,128]{2,1,0:T(8,128)}, u32[]{:S(2)}) copy-start(s32[8,16,128]{2,1,0:T(8,128)} %param.8) | copy-start | bytes 196612
  2.6 13.0 %collective-permute-start = (f32[4,8,16,128]{3,2,1,0:T(8,128)S(1)}, f32[4,8,16,128]{3,2,1,0:T(8,128)S(1)}, u32[]{:S(2)}, u32[]{:S(2)}) collective-permute-start(f32[4,8,16,128]{3,2,1,0:T(8,128)S(1)} %pad_select_fusion), channel_id=1, source_target_pairs={{8,0},{16,8},{24,16},{32,24},{40,32},{48,40},{56,48},{64,56},{72,6... | collective-permute-start | bytes 786440 | tf_op jit(solution)/shard_map/ppermute | solution.py:37
  5.3 10.4 %collective-permute-start.1 = (f32[4,8,16,128]{3,2,1,0:T(8,128)S(1)}, f32[4,8,16,128]{3,2,1,0:T(8,128)S(1)}, u32[]{:S(2)}, u32[]{:S(2)}) collective-permute-start(f32[4,8,16,128]{3,2,1,0:T(8,128)S(1)} %pad_select_fusion), channel_id=1, source_target_pairs={{0,8},{8,16},{16,24},{24,32},{32,40},{40,48},{48,56},{56,64},{64,7... | collective-permute-start | bytes 786440 | tf_op jit(solution)/shard_map/ppermute | solution.py:36
  15.7 10.9 %collective-permute-start.3 = (f32[4,24,8,128]{3,2,1,0:T(8,128)S(1)}, f32[4,24,8,128]{3,2,1,0:T(8,128)S(1)}, u32[]{:S(2)}, u32[]{:S(2)}) collective-permute-start(f32[4,24,8,128]{3,2,1,0:T(8,128)S(1)} %pad_maximum_fusion.2), channel_id=1, source_target_pairs={{0,1},{1,2},{2,3},{3,4},{4,5},{5,6},{6,7},{8,9},{9,10},{10,11},{11... | collective-permute-start | bytes 1179656 | tf_op jit(solution)/shard_map/ppermute | solution.py:36
  18.3 12.5 %collective-permute-start.2 = (f32[4,24,8,128]{3,2,1,0:T(8,128)S(1)}, f32[4,24,8,128]{3,2,1,0:T(8,128)S(1)}, u32[]{:S(2)}, u32[]{:S(2)}) collective-permute-start(f32[4,24,8,128]{3,2,1,0:T(8,128)S(1)} %pad_maximum_fusion.1), channel_id=1, source_target_pairs={{1,0},{2,1},{3,2},{4,3},{5,4},{6,5},{7,6},{9,8},{10,9},{11,10},{12... | collective-permute-start | bytes 1179656 | tf_op jit(solution)/shard_map/ppermute | solution.py:37
  30.8 0.8 copy-start.1
  35.7 0.8 %copy-start.7 = (s32[2,1,128]{2,1,0:T(1,128)S(1)}, s32[2,1,128]{2,1,0:T(1,128)}, u32[]{:S(2)}) copy-start(s32[2,1,128]{2,1,0:T(1,128)} %param.11) | copy-start | bytes 3076
  37.4 7.1 %all-to-all-start = ((bf16[8,2,128]{2,1,0:T(2,128)(2,1)}), bf16[8,2,128]{2,1,0:T(2,128)(2,1)S(1)}, u32[]{:S(2)}, u32[]{:S(2)}) async-start(bf16[8,2,128]{2,1,0:T(2,128)(2,1)} %broadcast_in_dim.362), calls=%async_computation | async-start | bytes 8192 | tf_op jit(solution)/shard_map/all_to_all | solution.py:144
  45.9 10.0 %collective-permute-start.4 = (f32[2208]{0:T(1024)S(1)}, f32[2208]{0:T(1024)S(1)}, u32[]{:S(2)}, u32[]{:S(2)}) collective-permute-start(f32[2208]{0:T(1024)S(1)} %pad_maximum_fusion.14), channel_id=1, source_target_pairs={{0,8},{8,16},{16,24},{24,32},{32,40},{40,48},{48,56},{56,64},{64,7... | collective-permute-start | bytes 26504 | tf_op jit(solution)/shard_map/ppermute | solution.py:39
  53.9 8.6 %collective-permute-start.5 = (f32[2208]{0:T(1024)S(1)}, f32[2208]{0:T(1024)S(1)}, u32[]{:S(2)}, u32[]{:S(2)}) collective-permute-start(f32[2208]{0:T(1024)S(1)} %pad_maximum_fusion.15), channel_id=1, source_target_pairs={{8,0},{16,8},{24,16},{32,24},{40,32},{48,40},{56,48},{64,56},{72,6... | collective-permute-start | bytes 26504 | tf_op jit(solution)/shard_map/ppermute | solution.py:40
  62.9 6.6 %collective-permute-start.6 = (f32[1204]{0:T(1024)S(1)}, f32[1204]{0:T(1024)S(1)}, u32[]{:S(2)}, u32[]{:S(2)}) collective-permute-start(f32[1204]{0:T(1024)S(1)} %pad_maximum_fusion.16), channel_id=1, source_target_pairs={{0,1},{1,2},{2,3},{3,4},{4,5},{5,6},{6,7},{8,9},{9,10},{10,11},{11... | collective-permute-start | bytes 14456 | tf_op jit(solution)/shard_map/ppermute | solution.py:39
  67.4 6.5 %collective-permute-start.7 = (f32[1204]{0:T(1024)S(1)}, f32[1204]{0:T(1024)S(1)}, u32[]{:S(2)}, u32[]{:S(2)}) collective-permute-start(f32[1204]{0:T(1024)S(1)} %pad_maximum_fusion.17), channel_id=1, source_target_pairs={{1,0},{2,1},{3,2},{4,3},{5,4},{6,5},{7,6},{9,8},{10,9},{11,10},{12... | collective-permute-start | bytes 14456 | tf_op jit(solution)/shard_map/ppermute | solution.py:40
  74.9 1.6 %copy-start.2 = (f32[4,24,8,128]{3,2,1,0:T(8,128)S(1)}, f32[4,24,8,128]{3,2,1,0:T(8,128)}, u32[]{:S(2)}) copy-start(f32[4,24,8,128]{3,2,1,0:T(8,128)} %copy-done.1) | copy-start | bytes 1179652
  75.0 1.6 %copy-start.3 = (f32[3,10,18,128]{3,2,1,0:T(8,128)S(1)}, f32[3,10,18,128]{3,2,1,0:T(8,128)}, u32[]{:S(2)}) copy-start(f32[3,10,18,128]{3,2,1,0:T(8,128)} %slice.606) | copy-start | bytes 829444
  75.0 1.6 %copy-start.4 = (f32[3,8,16,128]{3,2,1,0:T(8,128)S(1)}, f32[3,8,16,128]{3,2,1,0:T(8,128)}, u32[]{:S(2)}) copy-start(f32[3,8,16,128]{3,2,1,0:T(8,128)} %param.7) | copy-start | bytes 589828

commit v13 on v10

--- a/solution.py
+++ b/solution.py
@@ -138,13 +138,10 @@
     panels = jnp.sum(jnp.where(onehot, face_vals[:, None, :], 0.0), axis=2)
     low_panels = panels.astype(jnp.bfloat16)
     local_list = near_list[0]
-    blank_pick = jnp.zeros((local_list.shape[0], local_list.shape[1], NODES), jnp.bfloat16)
     group = lax.axis_size("gy")
     copies = jnp.broadcast_to(low_panels[None], (group,) + low_panels.shape)
     piece = lax.all_to_all(copies, "gy", 0, 0, tiled=True).reshape(group * 2, NODES)
-    valid = (local_list >= 0) & (local_list < piece.shape[0])
-    picked = piece[jnp.clip(local_list, 0, piece.shape[0] - 1)]
-    chosen = jnp.where(valid[:, :, None], picked, blank_pick)
+    chosen = piece[jnp.clip(local_list, 0, piece.shape[0] - 1)]
     double = (
         jnp.einsum("tkij,tkj->ti", near_blocks[0], chosen, preferred_element_type=jnp.float32)
         - 0.5 * panels

time: 77.9 us -> 77.8 us (level)
  starting transfers between devices: 34.5 us -> 35.5 us
  other arithmetic: 15 us -> 14.2 us
    ppermute x2, starting transfers between devices: 12.2 us -> 13.1 us  [swap(): from_prev = lax.ppermute(_pack(to_next), axis, _pairs(count, 1))]
  transfers between devices with their start and end apart: 9 -> 9, of which waited for: 5 -> 6; matrix products, arithmetic and copies ran while one was open for 11% -> 10% of each run, Pallas kernels for 0% -> 0%
where the time goes in v13:
time: 77.8 us; the launch traced here: 77.2 us
  starting transfers between devices  35.5 us (46%)
  waiting for transfers between devices  19.5 us (25%)
  other arithmetic  14.2 us (18%)
  local copies, waits for them, and re-layouts  6.68 us (9%)
  between operations  1.14 us (1%)
    ppermute x2, starting transfers between devices, swap(): from_prev = lax.ppermute(_pack(to_next), axis, _pairs(count, 1))  13.1 us
    ppermute x2, waiting for transfers between devices, swap(): from_next = lax.ppermute(_pack(to_prev), axis, _pairs(count, -1))  10.1 us
    ppermute x2, starting transfers between devices, swap(): from_prev = [lax.ppermute(to_next[0], axis, _pairs(count, 1))]  9.08 us
    ppermute x2, starting transfers between devices, swap(): from_next = [lax.ppermute(to_prev[0], axis, _pairs(count, -1))]  5.51 us
    ppermute x2, waiting for transfers between devices, swap(): from_next = [lax.ppermute(to_prev[0], axis, _pairs(count, -1))]  4.16 us
    all_to_all x1, starting transfers between devices, body(): lax.all_to_all(copies, 'gy', 0, 0, tiled=True).reshape(group * 2, NODES)  3.95 us
    ppermute x2, starting transfers between devices, swap(): from_next = lax.ppermute(_pack(to_prev), axis, _pairs(count, -1))  3.83 us
    all_to_all x1, waiting for transfers between devices, body(): lax.all_to_all(copies, 'gy', 0, 0, tiled=True).reshape(group * 2, NODES)  3.17 us
  transfers between devices with their start and end apart: 9, of which 6 were waited for; matrix products, arithmetic and copies ran while one was open for 10% of the time, Pallas kernels for 0%

profile of v13, /device:TPU:125, one launch (start us, length us, event | category | flops | bytes accessed | tf_op | source)
XLA Modules:
  0.0 77.2 jit_solution(18195549166674677938)
XLA Ops:
  0.7 0.9 %convert_element_type.41 = f32[8,16,128]{2,1,0:T(8,128)S(1)} convert(s32[8,16,128]{2,1,0:T(8,128)} %param.8) | non-fusion elementwise | flops 16384 | bytes 131072 | tf_op jit(solution)/shard_map/convert_element_type | solution.py:101
  1.6 1.0 %pad_select_fusion = f32[4,8,16,128]{3,2,1,0:T(8,128)S(1)} fusion(f32[3,8,16,128]{3,2,1,0:T(8,128)} %param.7, f32[8,16,128]{2,1,0:T(8,128)S(1)} %convert_element_type.41, pred[4]{0:T(512)(128)(4,1)S(1)} %iota_compare_fusion.5), kind=kLoop, calls=%fused_computation.63 | loop fusion | flops 65536 | bytes 524292 | tf_op jit(solution)/shard_map/jit(_where)/select_n | solution.py:99
  2.6 2.7 %collective-permute-start = (f32[4,8,16,128]{3,2,1,0:T(8,128)S(1)}, f32[4,8,16,128]{3,2,1,0:T(8,128)S(1)}, u32[]{:S(2)}, u32[]{:S(2)}) collective-permute-start(f32[4,8,16,128]{3,2,1,0:T(8,128)S(1)} %pad_select_fusion), channel_id=1, source_target_pairs={{8,0},{16,8},{24,16},{32,24},{40,32},{48,40},{56,48},{64,56},{72,6... | collective-permute-start | bytes 786440 | tf_op jit(solution)/shard_map/ppermute | solution.py:37
  5.3 6.6 %collective-permute-start.1 = (f32[4,8,16,128]{3,2,1,0:T(8,128)S(1)}, f32[4,8,16,128]{3,2,1,0:T(8,128)S(1)}, u32[]{:S(2)}, u32[]{:S(2)}) collective-permute-start(f32[4,8,16,128]{3,2,1,0:T(8,128)S(1)} %pad_select_fusion), channel_id=1, source_target_pairs={{0,8},{8,16},{16,24},{24,32},{32,40},{40,48},{48,56},{56,64},{64,7... | collective-permute-start | bytes 786440 | tf_op jit(solution)/shard_map/ppermute | solution.py:36
  12.7 0.7 compare_select_fusion
  13.5 1.5 %fusion.90 = (f32[1]{0:T(128)}, f32[1]{0:T(128)}, f32[1]{0:T(128)}, f32[1]{0:T(128)}) fusion(f32[4]{0:T(128)} %param.10), kind=kLoop, calls=%fused_computation.232 | loop fusion | bytes 32 | tf_op jit(solution)/shard_map/slice | solution.py:77
  15.3 2.5 %collective-permute-start.3 = (f32[4,24,8,128]{3,2,1,0:T(8,128)S(1)}, f32[4,24,8,128]{3,2,1,0:T(8,128)S(1)}, u32[]{:S(2)}, u32[]{:S(2)}) collective-permute-start(f32[4,24,8,128]{3,2,1,0:T(8,128)S(1)} %pad_maximum_fusion.2), channel_id=1, source_target_pairs={{0,1},{1,2},{2,3},{3,4},{4,5},{5,6},{6,7},{8,9},{9,10},{10,11},{11... | collective-permute-start | bytes 1179656 | tf_op jit(solution)/shard_map/ppermute | solution.py:36
  17.8 2.8 %collective-permute-start.2 = (f32[4,24,8,128]{3,2,1,0:T(8,128)S(1)}, f32[4,24,8,128]{3,2,1,0:T(8,128)S(1)}, u32[]{:S(2)}, u32[]{:S(2)}) collective-permute-start(f32[4,24,8,128]{3,2,1,0:T(8,128)S(1)} %pad_maximum_fusion.1), channel_id=1, source_target_pairs={{1,0},{2,1},{3,2},{4,3},{5,4},{6,5},{7,6},{9,8},{10,9},{11,10},{12... | collective-permute-start | bytes 1179656 | tf_op jit(solution)/shard_map/ppermute | solution.py:37
  20.6 0.7 fusion.89
  21.3 2.6 %select_select_fusion.1 = f32[8,16,128]{2,1,0:T(8,128)S(1)} fusion(s32[8,16,128]{2,1,0:T(8,128)S(1)} %copy-done.5, f32[]{:T(128)} %bitcast.3, f32[]{:T(128)} %bitcast.2, f32[]{:T(128)} %bitcast.1, f32[]{:T(128)} %bitcast), kind=kLoop, calls=%fused_computation.174 | loop fusion | flops 98304 | bytes 131088 | tf_op jit(solution)/shard_map/jit(_where)/select_n | solution.py:77
  23.9 1.8 %collective-permute-done.3 = f32[4,24,8,128]{3,2,1,0:T(8,128)S(1)} collective-permute-done((f32[4,24,8,128]{3,2,1,0:T(8,128)S(1)}, f32[4,24,8,128]{3,2,1,0:T(8,128)S(1)}, u32[]{:S(2)}, u32[]{:S(2)}) %collective-permute-start.3) | collective-permute-done | bytes 393248 | tf_op jit(solution)/shard_map/ppermute | solution.py:36
  25.7 4.2 %collective-permute-done.2 = f32[4,24,8,128]{3,2,1,0:T(8,128)S(1)} collective-permute-done((f32[4,24,8,128]{3,2,1,0:T(8,128)S(1)}, f32[4,24,8,128]{3,2,1,0:T(8,128)S(1)}, u32[]{:S(2)}, u32[]{:S(2)}) %collective-permute-start.2) | collective-permute-done | bytes 393248 | tf_op jit(solution)/shard_map/ppermute | solution.py:37
  30.2 0.5 copy-done.1
  30.7 3.0 %multiply_select_fusion = (f32[22,30,128]{2,1,0:T(8,128)S(1)}, f32[22,30,128]{2,1,0:T(8,128)S(1)}) fusion(pred[22,30]{1,0:T(8,128)(4,1)S(1)} %broadcast_and_fusion, f32[22,30,128]{2,1,0:T(8,128)S(1)} %slice.599, f32[24,32,128]{2,1,0:T(8,128)S(1)} %get-tuple-element.8, f32[24,32,128]{2,1,0:T(8,128)S(1)} %get-tuple-element.6, f32[]{:T(128)} %bitcast.8, ...), kind=kLoop, calls=%fused_computation.37 | loop fusion | flops 1436160 | bytes 2704036 | tf_op jit(solution)/shard_map/jit(_where)/select_n | solution.py:123
  33.7 0.3 fusion.10
  34.0 0.3 fusion.15
  35.8 0.6 broadcast_in_dim.349
  36.4 3.9 %all-to-all-start = ((bf16[8,2,128]{2,1,0:T(2,128)(2,1)}), bf16[8,2,128]{2,1,0:T(2,128)(2,1)S(1)}, u32[]{:S(2)}, u32[]{:S(2)}) async-start(bf16[8,2,128]{2,1,0:T(2,128)(2,1)} %broadcast_in_dim.349), calls=%async_computation | async-start | bytes 8192 | tf_op jit(solution)/shard_map/all_to_all | solution.py:143
  40.3 3.2 %all-to-all-done = bf16[8,2,128]{2,1,0:T(2,128)(2,1)S(1)} async-done(((bf16[8,2,128]{2,1,0:T(2,128)(2,1)}), bf16[8,2,128]{2,1,0:T(2,128)(2,1)S(1)}, u32[]{:S(2)}, u32[]{:S(2)}) %all-to-all-start) | async-done | bytes 4128 | tf_op jit(solution)/shard_map/all_to_all | solution.py:143
  43.5 0.6 gather_fusion
  44.7 8.8 %collective-permute-start.4 = (f32[2208]{0:T(1024)S(1)}, f32[2208]{0:T(1024)S(1)}, u32[]{:S(2)}, u32[]{:S(2)}) collective-permute-start(f32[2208]{0:T(1024)S(1)} %pad_maximum_fusion.13), channel_id=1, source_target_pairs={{0,8},{8,16},{16,24},{24,32},{32,40},{40,48},{48,56},{56,64},{64,7... | collective-permute-start | bytes 26504 | tf_op jit(solution)/shard_map/ppermute | solution.py:39
  53.7 1.9 %collective-permute-start.5 = (f32[2208]{0:T(1024)S(1)}, f32[2208]{0:T(1024)S(1)}, u32[]{:S(2)}, u32[]{:S(2)}) collective-permute-start(f32[2208]{0:T(1024)S(1)} %pad_maximum_fusion.14), channel_id=1, source_target_pairs={{8,0},{16,8},{24,16},{32,24},{40,32},{48,40},{56,48},{64,56},{72,6... | collective-permute-start | bytes 26504 | tf_op jit(solution)/shard_map/ppermute | solution.py:40
  55.6 0.8 slice.590
  56.5 5.8 %collective-permute-done.5 = f32[2208]{0:T(1024)S(1)} collective-permute-done((f32[2208]{0:T(1024)S(1)}, f32[2208]{0:T(1024)S(1)}, u32[]{:S(2)}, u32[]{:S(2)}) %collective-permute-start.5) | collective-permute-done | bytes 8864 | tf_op jit(solution)/shard_map/ppermute | solution.py:40
  62.7 4.3 %collective-permute-start.6 = (f32[1204]{0:T(1024)S(1)}, f32[1204]{0:T(1024)S(1)}, u32[]{:S(2)}, u32[]{:S(2)}) collective-permute-start(f32[1204]{0:T(1024)S(1)} %pad_maximum_fusion.15), channel_id=1, source_target_pairs={{0,1},{1,2},{2,3},{3,4},{4,5},{5,6},{6,7},{8,9},{9,10},{10,11},{11... | collective-permute-start | bytes 14456 | tf_op jit(solution)/shard_map/ppermute | solution.py:39
  67.2 1.9 %collective-permute-start.7 = (f32[1204]{0:T(1024)S(1)}, f32[1204]{0:T(1024)S(1)}, u32[]{:S(2)}, u32[]{:S(2)}) collective-permute-start(f32[1204]{0:T(1024)S(1)} %pad_maximum_fusion.16), channel_id=1, source_target_pairs={{1,0},{2,1},{3,2},{4,3},{5,4},{6,5},{7,6},{9,8},{10,9},{11,10},{12... | collective-permute-start | bytes 14456 | tf_op jit(solution)/shard_map/ppermute | solution.py:40
  69.4 4.3 %collective-permute-done.7 = f32[1204]{0:T(1024)S(1)} collective-permute-done((f32[1204]{0:T(1024)S(1)}, f32[1204]{0:T(1024)S(1)}, u32[]{:S(2)}, u32[]{:S(2)}) %collective-permute-start.7) | collective-permute-done | bytes 4848 | tf_op jit(solution)/shard_map/ppermute | solution.py:40
  74.4 0.3 fusion.26
  74.8 0.3 fusion.45
  75.1 0.3 fusion.56
  75.7 0.7 fusion.85
  76.4 0.9 %fusion.31 = f32[3,8,16,128]{3,2,1,0:T(8,128)} fusion(f32[3,10,18,128]{3,2,1,0:T(8,128)S(1)} %copy-done.3, f32[4,24,8,128]{3,2,1,0:T(8,128)S(1)} %collective-permute-done.3, f32[4,8,16,128]{3,2,1,0:T(8,128)S(1)} %collective-permute-done, f32[4,8,16,128]{3,2,1,0:T(8,128)S(1)} %pad_select_fusion, f32[4,8,16,128]{3,2,1,0:T(8,128)S(1)} %collective-permute-done.1, ...), kind=kLoop, calls=%fused_computation.79 | loop fusion | flops 933888 | bytes 2504704 | tf_op jit(solution)/shard_map/sub | solution.py:196
  (100 shorter events, 5.6 us)
Async XLA Ops:
  0.6 43.4 %copy-start = (bf16[1,2,8,128,128]{4,3,2,1,0:T(8,128)(2,1)S(1)}, bf16[1,2,8,128,128]{4,3,2,1,0:T(8,128)(2,1)}, u32[]{:S(2)}) copy-start(bf16[1,2,8,128,128]{4,3,2,1,0:T(8,128)(2,1)} %param.13) | copy-start | bytes 1572868
  2.6 18.0 %copy-start.6 = (f32[4]{0:T(128)S(1)}, f32[4]{0:T(128)}, u32[]{:S(2)}) copy-start(f32[4]{0:T(128)} %param.9) | copy-start | bytes 52
  2.6 18.7 %copy-start.5 = (s32[8,16,128]{2,1,0:T(8,128)S(1)}, s32[8,16,128]{2,1,0:T(8,128)}, u32[]{:S(2)}) copy-start(s32[8,16,128]{2,1,0:T(8,128)} %param.8) | copy-start | bytes 196612
  2.6 12.4 %collective-permute-start = (f32[4,8,16,128]{3,2,1,0:T(8,128)S(1)}, f32[4,8,16,128]{3,2,1,0:T(8,128)S(1)}, u32[]{:S(2)}, u32[]{:S(2)}) collective-permute-start(f32[4,8,16,128]{3,2,1,0:T(8,128)S(1)} %pad_select_fusion), channel_id=1, source_target_pairs={{8,0},{16,8},{24,16},{32,24},{40,32},{48,40},{56,48},{64,56},{72,6... | collective-permute-start | bytes 786440 | tf_op jit(solution)/shard_map/ppermute | solution.py:37
  5.3 9.9 %collective-permute-start.1 = (f32[4,8,16,128]{3,2,1,0:T(8,128)S(1)}, f32[4,8,16,128]{3,2,1,0:T(8,128)S(1)}, u32[]{:S(2)}, u32[]{:S(2)}) collective-permute-start(f32[4,8,16,128]{3,2,1,0:T(8,128)S(1)} %pad_select_fusion), channel_id=1, source_target_pairs={{0,8},{8,16},{16,24},{24,32},{32,40},{40,48},{48,56},{56,64},{64,7... | collective-permute-start | bytes 786440 | tf_op jit(solution)/shard_map/ppermute | solution.py:36
  15.3 10.4 %collective-permute-start.3 = (f32[4,24,8,128]{3,2,1,0:T(8,128)S(1)}, f32[4,24,8,128]{3,2,1,0:T(8,128)S(1)}, u32[]{:S(2)}, u32[]{:S(2)}) collective-permute-start(f32[4,24,8,128]{3,2,1,0:T(8,128)S(1)} %pad_maximum_fusion.2), channel_id=1, source_target_pairs={{0,1},{1,2},{2,3},{3,4},{4,5},{5,6},{6,7},{8,9},{9,10},{10,11},{11... | collective-permute-start | bytes 1179656 | tf_op jit(solution)/shard_map/ppermute | solution.py:36
  17.8 12.1 %collective-permute-start.2 = (f32[4,24,8,128]{3,2,1,0:T(8,128)S(1)}, f32[4,24,8,128]{3,2,1,0:T(8,128)S(1)}, u32[]{:S(2)}, u32[]{:S(2)}) collective-permute-start(f32[4,24,8,128]{3,2,1,0:T(8,128)S(1)} %pad_maximum_fusion.1), channel_id=1, source_target_pairs={{1,0},{2,1},{3,2},{4,3},{5,4},{6,5},{7,6},{9,8},{10,9},{11,10},{12... | collective-permute-start | bytes 1179656 | tf_op jit(solution)/shard_map/ppermute | solution.py:37
  29.9 0.7 copy-start.1
  34.7 0.8 %copy-start.7 = (s32[2,1,128]{2,1,0:T(1,128)S(1)}, s32[2,1,128]{2,1,0:T(1,128)}, u32[]{:S(2)}) copy-start(s32[2,1,128]{2,1,0:T(1,128)} %param.11) | copy-start | bytes 3076
  36.4 7.1 %all-to-all-start = ((bf16[8,2,128]{2,1,0:T(2,128)(2,1)}), bf16[8,2,128]{2,1,0:T(2,128)(2,1)S(1)}, u32[]{:S(2)}, u32[]{:S(2)}) async-start(bf16[8,2,128]{2,1,0:T(2,128)(2,1)} %broadcast_in_dim.349), calls=%async_computation | async-start | bytes 8192 | tf_op jit(solution)/shard_map/all_to_all | solution.py:143
  44.7 11.7 %collective-permute-start.4 = (f32[2208]{0:T(1024)S(1)}, f32[2208]{0:T(1024)S(1)}, u32[]{:S(2)}, u32[]{:S(2)}) collective-permute-start(f32[2208]{0:T(1024)S(1)} %pad_maximum_fusion.13), channel_id=1, source_target_pairs={{0,8},{8,16},{16,24},{24,32},{32,40},{40,48},{48,56},{56,64},{64,7... | collective-permute-start | bytes 26504 | tf_op jit(solution)/shard_map/ppermute | solution.py:39
  53.7 8.6 %collective-permute-start.5 = (f32[2208]{0:T(1024)S(1)}, f32[2208]{0:T(1024)S(1)}, u32[]{:S(2)}, u32[]{:S(2)}) collective-permute-start(f32[2208]{0:T(1024)S(1)} %pad_maximum_fusion.14), channel_id=1, source_target_pairs={{8,0},{16,8},{24,16},{32,24},{40,32},{48,40},{56,48},{64,56},{72,6... | collective-permute-start | bytes 26504 | tf_op jit(solution)/shard_map/ppermute | solution.py:40
  62.7 6.6 %collective-permute-start.6 = (f32[1204]{0:T(1024)S(1)}, f32[1204]{0:T(1024)S(1)}, u32[]{:S(2)}, u32[]{:S(2)}) collective-permute-start(f32[1204]{0:T(1024)S(1)} %pad_maximum_fusion.15), channel_id=1, source_target_pairs={{0,1},{1,2},{2,3},{3,4},{4,5},{5,6},{6,7},{8,9},{9,10},{10,11},{11... | collective-permute-start | bytes 14456 | tf_op jit(solution)/shard_map/ppermute | solution.py:39
  67.2 6.5 %collective-permute-start.7 = (f32[1204]{0:T(1024)S(1)}, f32[1204]{0:T(1024)S(1)}, u32[]{:S(2)}, u32[]{:S(2)}) collective-permute-start(f32[1204]{0:T(1024)S(1)} %pad_maximum_fusion.16), channel_id=1, source_target_pairs={{1,0},{2,1},{3,2},{4,3},{5,4},{6,5},{7,6},{9,8},{10,9},{11,10},{12... | collective-permute-start | bytes 14456 | tf_op jit(solution)/shard_map/ppermute | solution.py:40
  74.7 1.6 %copy-start.2 = (f32[4,24,8,128]{3,2,1,0:T(8,128)S(1)}, f32[4,24,8,128]{3,2,1,0:T(8,128)}, u32[]{:S(2)}) copy-start(f32[4,24,8,128]{3,2,1,0:T(8,128)} %copy-done.1) | copy-start | bytes 1179652
  74.7 1.6 %copy-start.3 = (f32[3,10,18,128]{3,2,1,0:T(8,128)S(1)}, f32[3,10,18,128]{3,2,1,0:T(8,128)}, u32[]{:S(2)}) copy-start(f32[3,10,18,128]{3,2,1,0:T(8,128)} %slice.590) | copy-start | bytes 829444
  74.8 1.6 %copy-start.4 = (f32[3,8,16,128]{3,2,1,0:T(8,128)S(1)}, f32[3,8,16,128]{3,2,1,0:T(8,128)}, u32[]{:S(2)}) copy-start(f32[3,8,16,128]{3,2,1,0:T(8,128)} %param.7) | copy-start | bytes 589828
